TPU v7x, 256 devices: a whole 4x4x8 slice. The times are simulated.
256 devices in a mesh: seq: 64 (over z_hi, y, x, core), tp: 4 (over z_lo).
Axes of the slice: x: 4, y: 4, z: 8 (z_hi: 2, z_lo: 4; z = z_hi * 4 + z_lo), core: 2. Of those that a mesh axis runs over, the one named last changes fastest.
Arguments:
- hidden_in: bfloat16 [16384, 2048], P(('seq', 'tp')), may hold values from -6 to 6
- attention_gain: float32 [2048], replicated, may hold values from 0.1 to 1.9
- attention_trainer_copy: float32 [2048, 5120], P(('seq', 'tp')), may hold values from -0.125 to 0.125
- query_gain: float32 [128], replicated, may hold values from 0.1 to 1.9
- key_gain: float32 [128], replicated, may hold values from 0.1 to 1.9
- output_proj: bfloat16 [4096, 2048], P('tp'), may hold values from -0.09375 to 0.09375
- post_gain: float32 [2048], replicated, may hold values from 0.1 to 1.9
- router_weight: bfloat16 [2048, 128], replicated, may hold values from -0.125 to 0.125
- gate_up_master: float32 [128, 2048, 1536], P(None, ('seq', 'tp')), may hold values from -0.125 to 0.125
- down_weight: bfloat16 [128, 768, 2048], P('seq', 'tp'), may hold values from -0.21875 to 0.21875
- routes: int32 [16384, 8], P(('seq', 'tp')), may hold values from 0 to 127, all different within a row; in each aligned block of 64 rows (0 to 63, 64 to 127, ...) at most 8 rows name the same one
- lengths: int32 [64], P('seq'), may hold values from 1 to 256, 8192 in all
- page_table: int32 [64, 2], P('seq'), may hold values from 0 to 3, as said below
Outputs:
- hidden_leaving: bfloat16 [16384, 2048], P(('seq', 'tp'))
- cache_pages: bfloat16 [256, 2, 4, 128, 128], P('seq', None, 'tp')
Inputs may be any that keep to these rules, and one draw needn't show every extreme that they name: `routes`: each row names 8 different experts. In each aligned block of 64 rows (the rows of one device) no expert is named by more than 8 rows, a bound that some block reaches. `lengths`: some prompt has exactly 256 live positions. `page_table`: the 2 slots of one prompt are distinct.
All inputs are finite; a program needn't handle non-finite values. No bound on the sum of `lengths` on one device may be relied on, other than what follows from the above.
Results may differ from a plain program's by a relative error of at most 0.0085.
Values may be sent and summed in bfloat16 or wider, within the bound.
No kernel may reach another device: no remote copies, remote signals or barrier semaphores. Data moves between devices by JAX's collectives and lax.ppermute only.
A program may use at most 128 MiB of HBM per device.

v0:
```python
import math

import jax
import jax.numpy as jnp
from jax import lax
from jax.sharding import PartitionSpec as P

QUERY_HEADS = 32
KEY_VALUE_HEADS = 4
HEAD_SIZE = 128
FF = 768
TOPK = 8
PAGE_POSITIONS = 128


EPS = 1e-06
THETA = 1000000.0


def laid_out(pieces, dim):
    pieces = jnp.moveaxis(pieces, 0, dim)
    lengths = pieces.shape
    return pieces.reshape(*lengths[:dim], lengths[dim] * lengths[dim + 1], *lengths[dim + 2 :])


def from_everyone(array, axis):
    peers = lax.axis_size(axis)
    return lax.all_to_all(
        jnp.broadcast_to(array[None], (peers, *array.shape)), axis, 0, 0, tiled=True
    )


def collect(array, axis, dim):
    return laid_out(from_everyone(array, axis), dim)


def in_blocks(array, dim, peers):
    lengths = array.shape
    pieces = array.reshape(*lengths[:dim], peers, lengths[dim] // peers, *lengths[dim + 1 :])
    return jnp.moveaxis(pieces, dim, 0)


def summed_on_arrival(array, axis, dim):
    peers = lax.axis_size(axis)
    pieces = lax.all_to_all(in_blocks(array, dim, peers), axis, 0, 0, tiled=True)
    return jnp.sum(pieces.astype(jnp.float32), axis=0)


def rms_scale(values, gain):
    return values * lax.rsqrt(jnp.mean(values * values, axis=-1, keepdims=True) + EPS) * gain


def rotate(values, positions):
    half_dim = values.shape[-1] // 2
    frequency = THETA ** (-2.0 * jnp.arange(half_dim, dtype=jnp.float32) / values.shape[-1])
    angles = positions.astype(jnp.float32)[:, None] * frequency[None, :]
    cosine = jnp.cos(angles)[:, None, :]
    sine = jnp.sin(angles)[:, None, :]
    first_half = values[..., :half_dim]
    second_half = values[..., half_dim:]
    return jnp.concatenate(
        [first_half * cosine - second_half * sine, second_half * cosine + first_half * sine],
        axis=-1,
    )


def attend_prompt(query_rows, keys_rotated, values_in, prompt_length):
    column_span = query_rows.shape[0]
    scores = jnp.einsum(
        "qhgd,khd->hgqk", query_rows, keys_rotated, preferred_element_type=jnp.float32
    ) / math.sqrt(query_rows.shape[-1])
    places = jnp.arange(column_span)
    allowed = (places[None, :] <= places[:, None]) & (places[None, :] < prompt_length)
    weights = jnp.where(allowed, jnp.exp(scores), 0.0)
    probs = (weights / jnp.sum(weights, axis=-1, keepdims=True)).astype(jnp.bfloat16)
    context_rows = jnp.einsum(
        "hgqk,khd->qhgd", probs, values_in, preferred_element_type=jnp.float32
    )
    return context_rows.astype(jnp.bfloat16).reshape(column_span, -1)


def regroup(features, seq_count, tensor_parallel_count):
    leading = features.shape[:-1]
    blocks = features.reshape(leading + (seq_count, tensor_parallel_count, -1))
    return jnp.swapaxes(blocks, -3, -2).reshape(leading + (-1,))


def on_device(
    hidden_in,
    attention_gain,
    attention_trainer_copy,
    query_gain,
    key_gain,
    output_proj,
    post_gain,
    router_weight,
    gate_up_master,
    down_weight,
    routes,
    lengths,
    page_table,
):
    tensor_parallel_count = lax.axis_size("tp")
    seq_count = lax.axis_size("seq")
    tp_place = lax.axis_index("tp")
    quarter = hidden_in.shape[0]
    width = hidden_in.shape[1]
    experts_all = router_weight.shape[1]
    exp_here = experts_all // seq_count
    capacity = max(2, 2 * quarter * TOPK // experts_all)
    quarter_units = FF // tensor_parallel_count
    heads_here = QUERY_HEADS // tensor_parallel_count
    key_value_local = KEY_VALUE_HEADS // tensor_parallel_count
    prompt_rows = collect(hidden_in, "tp", 0)
    column_span = prompt_rows.shape[0]
    normed = rms_scale(prompt_rows.astype(jnp.float32), attention_gain).astype(jnp.bfloat16)
    trainer_rows = attention_trainer_copy.shape[0]
    query_cols = attention_trainer_copy[:, : QUERY_HEADS * HEAD_SIZE].reshape(
        trainer_rows, tensor_parallel_count, heads_here * HEAD_SIZE
    )
    key_columns = attention_trainer_copy[
        :, QUERY_HEADS * HEAD_SIZE : (QUERY_HEADS + KEY_VALUE_HEADS) * HEAD_SIZE
    ].reshape(trainer_rows, tensor_parallel_count, key_value_local * HEAD_SIZE)
    value_columns = attention_trainer_copy[
        :, (QUERY_HEADS + KEY_VALUE_HEADS) * HEAD_SIZE :
    ].reshape(trainer_rows, tensor_parallel_count, key_value_local * HEAD_SIZE)
    joined = (
        jnp.concatenate([query_cols, key_columns, value_columns], axis=2)
        .reshape(trainer_rows, -1)
        .astype(jnp.bfloat16)
    )
    head_rows = lax.all_to_all(joined, "tp", split_axis=1, concat_axis=0, tiled=True)
    projected_rows = jnp.dot(
        normed,
        lax.all_gather(head_rows, "seq", axis=0, tiled=True),
        preferred_element_type=jnp.float32,
    )
    positions = jnp.arange(column_span)
    query_rows = projected_rows[:, : heads_here * HEAD_SIZE].reshape(
        column_span, heads_here, HEAD_SIZE
    )
    keys_raw = projected_rows[
        :, heads_here * HEAD_SIZE : (heads_here + key_value_local) * HEAD_SIZE
    ].reshape(column_span, key_value_local, HEAD_SIZE)
    values_local_rows = (
        projected_rows[:, (heads_here + key_value_local) * HEAD_SIZE :]
        .reshape(column_span, key_value_local, HEAD_SIZE)
        .astype(jnp.bfloat16)
    )
    query_rows = rotate(rms_scale(query_rows, query_gain), positions).astype(jnp.bfloat16)
    keys_rotated = rotate(rms_scale(keys_raw, key_gain), positions).astype(jnp.bfloat16)
    prompt_length = lengths[0]
    context_rows = attend_prompt(
        query_rows.reshape(column_span, key_value_local, QUERY_HEADS // KEY_VALUE_HEADS, HEAD_SIZE),
        keys_rotated,
        values_local_rows,
        prompt_length,
    )
    attention_sums = summed_on_arrival(
        jnp.dot(context_rows, output_proj, preferred_element_type=jnp.float32).astype(jnp.bfloat16),
        "tp",
        0,
    )
    after_attn = hidden_in.astype(jnp.float32) + attention_sums
    mixed = rms_scale(after_attn, post_gain).astype(jnp.bfloat16)
    logits = jnp.dot(mixed, router_weight, preferred_element_type=jnp.float32)
    chosen = jnp.take_along_axis(logits, routes, axis=1)
    raised = jnp.exp(chosen)
    gates = raised / jnp.sum(raised, axis=1, keepdims=True)
    pair_expert = routes.reshape(-1)
    hits = (pair_expert[:, None] == jnp.arange(experts_all, dtype=jnp.int32)[None, :]).astype(
        jnp.int32
    )
    before = jnp.cumsum(hits, axis=0) - hits
    slot_index = jnp.sum(before * hits, axis=1)
    target = pair_expert * capacity + slot_index
    mixed_order = regroup(mixed, seq_count, tensor_parallel_count)
    outgoing = (
        jnp.zeros((experts_all * capacity, width), jnp.bfloat16)
        .at[target]
        .set(jnp.repeat(mixed_order, TOPK, axis=0))
    )
    outgoing = outgoing.reshape(seq_count, exp_here, capacity, width)
    incoming = lax.all_to_all(outgoing, "seq", split_axis=0, concat_axis=0, tiled=True)
    by_expert = lax.all_to_all(
        gate_up_master.astype(jnp.bfloat16), "seq", split_axis=0, concat_axis=1, tiled=True
    )
    full_gate_up, full_down = (
        lax.all_gather(by_expert, "tp", axis=1, tiled=True),
        lax.all_gather(down_weight, "tp", axis=1, tiled=True),
    )
    results = []
    for expert_slot in range(exp_here):
        flat_rows = incoming[:, expert_slot].reshape(-1, width)
        both = jnp.dot(flat_rows, full_gate_up[expert_slot], preferred_element_type=jnp.float32)
        units = (jax.nn.silu(both[:, :FF]) * both[:, FF:]).astype(jnp.bfloat16)
        summed = jnp.zeros((flat_rows.shape[0], width), jnp.float32)
        for block_index in range(tensor_parallel_count):
            lower = block_index * quarter_units
            produced = jnp.dot(
                units[:, lower : lower + quarter_units],
                full_down[expert_slot, lower : lower + quarter_units],
                preferred_element_type=jnp.float32,
            )
            summed = summed + lax.optimization_barrier(produced.astype(jnp.bfloat16)).astype(
                jnp.float32
            )
        results.append(summed.astype(jnp.bfloat16).reshape(seq_count, capacity, width))
    expert_result = jnp.stack(results, axis=1)
    returned = lax.all_to_all(expert_result, "seq", split_axis=0, concat_axis=0, tiled=True)
    pair_out = returned.reshape(experts_all * capacity, width)[target]
    combined = jnp.sum(
        gates[:, :, None] * pair_out.reshape(quarter, TOPK, width).astype(jnp.float32), axis=1
    )
    own_places = tp_place * quarter + jnp.arange(quarter)
    live_rows = own_places < prompt_length
    hidden_leaving = jnp.where(live_rows[:, None], after_attn + combined, 0.0).astype(jnp.bfloat16)
    live = (positions < prompt_length)[:, None, None]
    zero_value = jnp.zeros((), jnp.bfloat16)
    keys_kept = jnp.where(live, keys_rotated, zero_value)
    values_kept = jnp.where(live, values_local_rows, zero_value)
    pages_here = column_span // PAGE_POSITIONS
    prompt_pages = jnp.stack([keys_kept, values_kept], axis=1)
    prompt_pages = prompt_pages.reshape(
        pages_here, PAGE_POSITIONS, 2, key_value_local, HEAD_SIZE
    ).transpose(0, 2, 3, 1, 4)
    paged_cache = jnp.zeros(
        (2 * pages_here, 2, key_value_local, PAGE_POSITIONS, HEAD_SIZE), jnp.bfloat16
    )
    paged_cache = paged_cache.at[page_table[0]].set(prompt_pages)
    return (hidden_leaving, paged_cache)


def solution(mesh):
    return jax.shard_map(
        on_device,
        mesh=mesh,
        in_specs=(
            P(("seq", "tp"), None),
            P(),
            P(("seq", "tp"), None),
            P(),
            P(),
            P("tp", None),
            P(),
            P(),
            P(None, ("seq", "tp"), None),
            P("seq", "tp", None),
            P(("seq", "tp"), None),
            P("seq"),
            P("seq", None),
        ),
        out_specs=(P(("seq", "tp"), None), P("seq", None, "tp", None, None)),
        check_vma=False,
    )
```

profile of v0, /device:TPU:2, one launch (start us, length us, event | category | flops | bytes accessed | tf_op | source)
XLA Modules:
  0.0 763.6 jit_solution(16134831410229490834)
XLA Ops:
  8.2 11.6 %all_to_all.54 = bf16[8,4,1280]{2,0,1:T(8,128)(2,1)} all-to-all(bf16[8,4,1280]{2,0,1:T(8,128)(2,1)S(1)} %pad_maximum_fusion.1), channel_id=1, replica_groups=mesh['seq'=64,'tp'=4] {'tp'}, dimensions={1} | all-to-all | bytes 163840 | tf_op jit(solution)/shard_map/all_to_all | solution.py:132
  19.9 3.2 convert_element_type.172
  23.1 89.9 %all_to_all.55 = bf16[128,8,1536]{2,1,0:T(8,128)(2,1)S(1)} all-to-all(bf16[128,8,1536]{2,1,0:T(8,128)(2,1)S(1)} %convert_element_type.172), channel_id=1, replica_groups=mesh['seq'=64,'tp'=4] {'seq'}, dimensions={0} | all-to-all | bytes 6291456 | tf_op jit(solution)/shard_map/all_to_all | solution.py:185
  113.0 2.0 copy.146
  117.1 5.7 all-to-all-start
  124.8 43.0 %all-to-all-done = bf16[4,64,2048]{2,1,0:T(8,128)(2,1)S(1)} async-done(((bf16[4,64,2048]{2,1,0:T(8,128)(2,1)}), bf16[4,64,2048]{2,1,0:T(8,128)(2,1)S(1)}, u32[]{:S(2)}, u32[]{:S(2)}) %all-to-all-start) | async-done | bytes 1048608 | tf_op jit(solution)/shard_map/all_to_all | solution.py:28
  169.6 4.3 fusion.51
  182.1 2.3 convolution_convert_fusion.8
  184.4 4.8 all-to-all-start.2
  190.4 58.5 %all-to-all-done.2 = bf16[4,64,2048]{2,1,0:T(8,128)(2,1)S(1)} async-done(((bf16[4,64,2048]{2,1,0:T(8,128)(2,1)}), bf16[4,64,2048]{2,1,0:T(8,128)(2,1)S(1)}, u32[]{:S(2)}, u32[]{:S(2)}) %all-to-all-start.2) | async-done | bytes 1048608 | tf_op jit(solution)/shard_map/all_to_all | solution.py:45
  250.0 6.3 scatter_custom_fusion
  256.2 8.8 %all-to-all-start.3 = ((bf16[64,2,8,2048]{3,2,1,0:T(8,128)(2,1)}), bf16[64,2,8,2048]{3,2,1,0:T(8,128)(2,1)}, u32[]{:S(2)}, u32[]{:S(2)}) async-start(bf16[64,2,8,2048]{3,2,1,0:T(8,128)(2,1)} %bitcast.168), calls=%async_computation.3 | async-start | bytes 8388608 | tf_op jit(solution)/shard_map/all_to_all | solution.py:184
  265.7 116.9 %all-to-all-done.3 = bf16[64,2,8,2048]{3,2,1,0:T(8,128)(2,1)} async-done(((bf16[64,2,8,2048]{3,2,1,0:T(8,128)(2,1)}), bf16[64,2,8,2048]{3,2,1,0:T(8,128)(2,1)}, u32[]{:S(2)}, u32[]{:S(2)}) %all-to-all-start.3) | async-done | bytes 4194336 | tf_op jit(solution)/shard_map/all_to_all | solution.py:184
  382.6 116.6 %all-gather.6.cloned.1.call-done = bf16[2,2048,1536]{2,1,0:T(8,128)(2,1)} async-done(((bf16[2,512,1536]{2,1,0:T(8,128)(2,1)}), bf16[2,2048,1536]{2,1,0:T(8,128)(2,1)}) %all-gather.6.cloned.1.call-update) | async-done | bytes 12582928 | tf_op jit(solution)/shard_map/all_gather | solution.py:189
  499.2 6.3 fusion.1
  506.3 5.0 fusion
  511.8 111.2 %all-gather.8.cloned.1.call-done = bf16[2,768,2048]{2,1,0:T(8,128)(2,1)} async-done(((bf16[2,192,2048]{2,1,0:T(8,128)(2,1)}), bf16[2,768,2048]{2,1,0:T(8,128)(2,1)}) %all-gather.8.cloned.1.call-update) | async-done | bytes 6291472 | tf_op jit(solution)/shard_map/all_gather | solution.py:190
  623.0 2.0 convolution_convert_fusion
  632.5 4.0 fusion.3
  636.5 2.3 pad_maximum_fusion
  638.8 11.9 %all-to-all-start.5 = ((bf16[64,2,8,2048]{3,2,1,0:T(8,128)(2,1)}), bf16[64,2,8,2048]{3,2,1,0:T(8,128)(2,1)}, u32[]{:S(2)}, u32[]{:S(2)}) async-start(bf16[64,2,8,2048]{3,2,1,0:T(8,128)(2,1)} %pad_maximum_fusion), calls=%async_computation.5 | async-start | bytes 8388608 | tf_op jit(solution)/shard_map/all_to_all | solution.py:210
  653.1 3.6 gather_fusion.1
  657.0 90.2 %all-to-all-done.5 = bf16[64,2,8,2048]{3,2,1,0:T(8,128)(2,1)} async-done(((bf16[64,2,8,2048]{3,2,1,0:T(8,128)(2,1)}), bf16[64,2,8,2048]{3,2,1,0:T(8,128)(2,1)}, u32[]{:S(2)}, u32[]{:S(2)}) %all-to-all-start.5) | async-done | bytes 4194336 | tf_op jit(solution)/shard_map/all_to_all | solution.py:210
  747.2 7.1 gather_fusion
  (120 shorter events, 30.9 us)
Async XLA Ops:
  7.2 645.7 %copy-start = (bf16[2048,128]{1,0:T(8,128)(2,1)S(1)}, bf16[2048,128]{1,0:T(8,128)(2,1)}, u32[]{:S(2)}) copy-start(bf16[2048,128]{1,0:T(8,128)(2,1)} %param.20) | copy-start | bytes 1572868
  7.2 162.4 %all-gather.4.cloned.1.call-start = ((), (), s32[]{:S(2)}) async-start(), calls=%async_computation.6 | async-start | bytes 5324800 | tf_op jit(solution)/shard_map/all_gather | solution.py:135
  19.9 479.4 %all-gather.6.cloned.1.call-start = ((), (), s32[]{:S(2)}) async-start(), calls=%async_computation.7 | async-start | bytes 15728640 | tf_op jit(solution)/shard_map/all_gather | solution.py:189
  115.0 0.9 copy-start.2
  115.9 52.2 %copy-start.11 = (f32[2048]{0:T(1024)S(1)}, f32[2048]{0:T(1024)}, u32[]{:S(2)}) copy-start(f32[2048]{0:T(1024)} %param.14) | copy-start | bytes 24580
  117.1 50.7 %all-to-all-start = ((bf16[4,64,2048]{2,1,0:T(8,128)(2,1)}), bf16[4,64,2048]{2,1,0:T(8,128)(2,1)S(1)}, u32[]{:S(2)}, u32[]{:S(2)}) async-start(bf16[4,64,2048]{2,1,0:T(8,128)(2,1)} %broadcast_in_dim.49), calls=%async_computation | async-start | bytes 2097152 | tf_op jit(solution)/shard_map/all_to_all | solution.py:28
  123.4 50.5 %copy-start.13 = (f32[64]{0:T(128)}, f32[64]{0:T(128)S(1)}, u32[]{:S(2)}) copy-start(f32[64]{0:T(128)S(1)} %multiply_power_fusion) | copy-start | bytes 772
  173.9 5.8 copy-start.3
  177.0 1.5 copy-start.5
  177.0 1.5 copy-start.7
  178.0 0.8 copy-start.10
  179.7 2.4 copy-start.15
  184.4 4.8 copy-start.9
  184.4 64.5 %all-to-all-start.2 = ((bf16[4,64,2048]{2,1,0:T(8,128)(2,1)}), bf16[4,64,2048]{2,1,0:T(8,128)(2,1)S(1)}, u32[]{:S(2)}, u32[]{:S(2)}) async-start(bf16[4,64,2048]{2,1,0:T(8,128)(2,1)} %bitcast.18), calls=%async_computation.2 | async-start | bytes 2097152 | tf_op jit(solution)/shard_map/all_to_all | solution.py:45
  189.5 59.8 %copy-start.12 = (f32[2048]{0:T(1024)S(1)}, f32[2048]{0:T(1024)}, u32[]{:S(2)}) copy-start(f32[2048]{0:T(1024)} %param.19) | copy-start | bytes 24580
  256.2 126.4 %all-to-all-start.3 = ((bf16[64,2,8,2048]{3,2,1,0:T(8,128)(2,1)}), bf16[64,2,8,2048]{3,2,1,0:T(8,128)(2,1)}, u32[]{:S(2)}, u32[]{:S(2)}) async-start(bf16[64,2,8,2048]{3,2,1,0:T(8,128)(2,1)} %bitcast.168), calls=%async_computation.3 | async-start | bytes 8388608 | tf_op jit(solution)/shard_map/all_to_all | solution.py:184
  265.0 358.0 %all-gather.8.cloned.1.call-start = ((), (), s32[]{:S(2)}) async-start(), calls=%async_computation.8 | async-start | bytes 7864320 | tf_op jit(solution)/shard_map/all_gather | solution.py:190
  499.2 7.0 copy-start.14
  623.0 5.8 copy-start.1
  638.8 12.2 %copy-start.16 = (s32[1,2]{1,0:T(1,128)S(1)}, s32[1,2]{1,0:T(1,128)}, u32[]{:S(2)}) copy-start(s32[1,2]{1,0:T(1,128)} %param.25) | copy-start | bytes 28
  638.8 12.2 %copy-start.6 = (bf16[256,1,64]{2,0,1:T(8,128)(2,1)S(1)}, bf16[256,1,64]{2,0,1:T(8,128)(2,1)}, u32[]{:S(2)}) copy-start(bf16[256,1,64]{2,0,1:T(8,128)(2,1)} %copy-done.5) | copy-start | bytes 98308
  638.8 12.2 %copy-start.8 = (bf16[256,1,64]{2,0,1:T(8,128)(2,1)S(1)}, bf16[256,1,64]{2,0,1:T(8,128)(2,1)}, u32[]{:S(2)}) copy-start(bf16[256,1,64]{2,0,1:T(8,128)(2,1)} %copy-done.7) | copy-start | bytes 98308
  638.8 108.4 %all-to-all-start.5 = ((bf16[64,2,8,2048]{3,2,1,0:T(8,128)(2,1)}), bf16[64,2,8,2048]{3,2,1,0:T(8,128)(2,1)}, u32[]{:S(2)}, u32[]{:S(2)}) async-start(bf16[64,2,8,2048]{3,2,1,0:T(8,128)(2,1)} %pad_maximum_fusion), calls=%async_computation.5 | async-start | bytes 8388608 | tf_op jit(solution)/shard_map/all_to_all | solution.py:210
  652.9 3.9 copy-start.4
Sparse Core Ops, SparseCore 0:
  20.0 149.5 all-gather.3
  171.4 327.8 all-gather.5
  501.0 121.9 all-gather.7
where the time goes:
time: 767 us; the launch traced here: 764 us
  waiting for transfers between devices  537 us (70%)
  blocking collectives  102 us (13%)
  starting transfers between devices  31.5 us (4%)
  matrix products  29.1 us (4%)
  local copies, waits for them, and re-layouts  26.3 us (3%)
  other arithmetic  23.1 us (3%)
  between operations  15 us (2%)
    all_to_all x1, waiting for transfers between devices, on_device(): lax.all_to_all(outgoing, 'seq', split_axis=0, concat_axis=0, tiled=True)  117 us
    all_gather x1, waiting for transfers between devices, on_device(): lax.all_gather(by_expert, 'tp', axis=1, tiled=True)  117 us
    all_gather x1, waiting for transfers between devices, on_device(): lax.all_gather(down_weight, 'tp', axis=1, tiled=True)  111 us
    all_to_all x1, waiting for transfers between devices, on_device(): lax.all_to_all(expert_result, 'seq', split_axis=0, concat_axis=0, tiled=T...  90.2 us
    all_to_all x1, blocking collectives, on_device(): lax.all_to_all(gate_up_master.astype(jnp.bfloat16), 'seq', split_axis=0,...  89.9 us
    all_to_all x1, waiting for transfers between devices, summed_on_arrival(): lax.all_to_all(in_blocks(array, dim, peers), axis, 0, 0, tiled=True)  58.5 us
    all_to_all x1, waiting for transfers between devices, from_everyone(): lax.all_to_all(jnp.broadcast_to(array[None], (peers, *array.shape)), axis...  43 us
  transfers between devices with their start and end apart: 7, of which 7 were waited for; matrix products, arithmetic and copies ran while one was open for 6% of the time, Pallas kernels for 0%

commit v1 on v0

--- a/solution.py
+++ b/solution.py
@@ -1,9 +1,10 @@
+import functools
 import math
 
 import jax
 import jax.numpy as jnp
 from jax import lax
-from jax.sharding import PartitionSpec as P
+from jax.sharding import Mesh, PartitionSpec as P
 
 QUERY_HEADS = 32
 KEY_VALUE_HEADS = 4
@@ -99,42 +100,75 @@
     routes,
     lengths,
     page_table,
+    *,
+    n_zh,
+    n_sub,
+    n_tp,
 ):
-    tensor_parallel_count = lax.axis_size("tp")
-    seq_count = lax.axis_size("seq")
+    zh = lax.axis_index("zh")
     tp_place = lax.axis_index("tp")
     quarter = hidden_in.shape[0]
     width = hidden_in.shape[1]
     experts_all = router_weight.shape[1]
-    exp_here = experts_all // seq_count
-    capacity = max(2, 2 * quarter * TOPK // experts_all)
-    quarter_units = FF // tensor_parallel_count
-    heads_here = QUERY_HEADS // tensor_parallel_count
-    key_value_local = KEY_VALUE_HEADS // tensor_parallel_count
-    prompt_rows = collect(hidden_in, "tp", 0)
+    half_experts = experts_all // n_zh
+    heads_here = QUERY_HEADS // n_tp
+    key_value_local = KEY_VALUE_HEADS // n_tp
+    ff_half = FF // 2
+    ff_quarter = FF // n_tp
+    capacity = 2 * 8
+    within = ("sub", "tp")
+    n_within = n_sub * n_tp
+
+    gate_up_half = gate_up_master.astype(jnp.bfloat16)
+    trainer_block = gate_up_half.shape[1]
+    gate_up_half = gate_up_half.reshape(n_zh, half_experts, trainer_block, 2 * FF)
+    gate_up_half = lax.all_to_all(gate_up_half, "zh", 0, 0, tiled=True)
+    pieces = gate_up_half.reshape(n_zh, n_sub, 2, trainer_block, 2 * FF)
+    gate_part = pieces[..., :FF].reshape(n_zh, n_sub, 2, trainer_block, 2, ff_half)
+    up_part = pieces[..., FF:].reshape(n_zh, n_sub, 2, trainer_block, 2, ff_half)
+    pieces = jnp.concatenate([gate_part, up_part], axis=-1)
+    pieces = pieces.transpose(1, 4, 2, 0, 3, 5).reshape(n_within, n_zh * trainer_block, FF)
+    pieces = lax.all_to_all(pieces, within, 0, 0, tiled=True)
+    expert_gate_up = (
+        pieces.reshape(n_sub, n_tp, n_zh, trainer_block, FF)
+        .transpose(2, 0, 1, 3, 4)
+        .reshape(-1, FF)
+    )
+    parity = tp_place % 2
+    kept = lax.dynamic_index_in_dim(down_weight, parity, 0, keepdims=False)
+    given = lax.dynamic_index_in_dim(down_weight, 1 - parity, 0, keepdims=False)
+    got = lax.ppermute(given, "tp", perm=[(i, i ^ 1) for i in range(n_tp)])
+    down_first = jnp.where(parity == 0, kept, got)
+    down_second = jnp.where(parity == 0, got, kept)
+
+    prompt_rows = lax.all_gather(hidden_in, "tp", axis=0, tiled=True)
     column_span = prompt_rows.shape[0]
     normed = rms_scale(prompt_rows.astype(jnp.float32), attention_gain).astype(jnp.bfloat16)
     trainer_rows = attention_trainer_copy.shape[0]
     query_cols = attention_trainer_copy[:, : QUERY_HEADS * HEAD_SIZE].reshape(
-        trainer_rows, tensor_parallel_count, heads_here * HEAD_SIZE
+        trainer_rows, n_tp, heads_here * HEAD_SIZE
     )
     key_columns = attention_trainer_copy[
         :, QUERY_HEADS * HEAD_SIZE : (QUERY_HEADS + KEY_VALUE_HEADS) * HEAD_SIZE
-    ].reshape(trainer_rows, tensor_parallel_count, key_value_local * HEAD_SIZE)
+    ].reshape(trainer_rows, n_tp, key_value_local * HEAD_SIZE)
     value_columns = attention_trainer_copy[
         :, (QUERY_HEADS + KEY_VALUE_HEADS) * HEAD_SIZE :
-    ].reshape(trainer_rows, tensor_parallel_count, key_value_local * HEAD_SIZE)
+    ].reshape(trainer_rows, n_tp, key_value_local * HEAD_SIZE)
     joined = (
         jnp.concatenate([query_cols, key_columns, value_columns], axis=2)
         .reshape(trainer_rows, -1)
         .astype(jnp.bfloat16)
     )
     head_rows = lax.all_to_all(joined, "tp", split_axis=1, concat_axis=0, tiled=True)
-    projected_rows = jnp.dot(
-        normed,
-        lax.all_gather(head_rows, "seq", axis=0, tiled=True),
-        preferred_element_type=jnp.float32,
-    )
+    head_rows = lax.all_gather(head_rows, "zh", axis=0, tiled=True)
+    head_rows = lax.all_gather(head_rows, "sub", axis=0, tiled=True)
+    seq_block = head_rows.shape[0] // (n_zh * n_sub)
+    normed_order = (
+        normed.reshape(column_span, n_zh, n_sub, seq_block)
+        .transpose(0, 2, 1, 3)
+        .reshape(column_span, -1)
+    )
+    projected_rows = jnp.dot(normed_order, head_rows, preferred_element_type=jnp.float32)
     positions = jnp.arange(column_span)
     query_rows = projected_rows[:, : heads_here * HEAD_SIZE].reshape(
         column_span, heads_here, HEAD_SIZE
@@ -167,50 +201,57 @@
     chosen = jnp.take_along_axis(logits, routes, axis=1)
     raised = jnp.exp(chosen)
     gates = raised / jnp.sum(raised, axis=1, keepdims=True)
-    pair_expert = routes.reshape(-1)
-    hits = (pair_expert[:, None] == jnp.arange(experts_all, dtype=jnp.int32)[None, :]).astype(
-        jnp.int32
-    )
+
+    both_rows = lax.all_gather(mixed, "zh", axis=0, tiled=True)
+    both_routes = lax.all_gather(routes, "zh", axis=0, tiled=True)
+    both_gates = lax.all_gather(gates, "zh", axis=0, tiled=True)
+    row_count = both_rows.shape[0]
+    pair_expert = both_routes.reshape(-1)
+    local_pair = (pair_expert // half_experts) == zh
+    local_expert = pair_expert % half_experts
+    hits = (
+        (local_expert[:, None] == jnp.arange(half_experts, dtype=jnp.int32)[None, :])
+        & local_pair[:, None]
+    ).astype(jnp.int32)
     before = jnp.cumsum(hits, axis=0) - hits
     slot_index = jnp.sum(before * hits, axis=1)
-    target = pair_expert * capacity + slot_index
-    mixed_order = regroup(mixed, seq_count, tensor_parallel_count)
+    target = jnp.where(local_pair, local_expert * capacity + slot_index, half_experts * capacity)
     outgoing = (
-        jnp.zeros((experts_all * capacity, width), jnp.bfloat16)
+        jnp.zeros((half_experts * capacity, width), jnp.bfloat16)
         .at[target]
-        .set(jnp.repeat(mixed_order, TOPK, axis=0))
-    )
-    outgoing = outgoing.reshape(seq_count, exp_here, capacity, width)
-    incoming = lax.all_to_all(outgoing, "seq", split_axis=0, concat_axis=0, tiled=True)
-    by_expert = lax.all_to_all(
-        gate_up_master.astype(jnp.bfloat16), "seq", split_axis=0, concat_axis=1, tiled=True
-    )
-    full_gate_up, full_down = (
-        lax.all_gather(by_expert, "tp", axis=1, tiled=True),
-        lax.all_gather(down_weight, "tp", axis=1, tiled=True),
-    )
-    results = []
-    for expert_slot in range(exp_here):
-        flat_rows = incoming[:, expert_slot].reshape(-1, width)
-        both = jnp.dot(flat_rows, full_gate_up[expert_slot], preferred_element_type=jnp.float32)
-        units = (jax.nn.silu(both[:, :FF]) * both[:, FF:]).astype(jnp.bfloat16)
-        summed = jnp.zeros((flat_rows.shape[0], width), jnp.float32)
-        for block_index in range(tensor_parallel_count):
-            lower = block_index * quarter_units
-            produced = jnp.dot(
-                units[:, lower : lower + quarter_units],
-                full_down[expert_slot, lower : lower + quarter_units],
-                preferred_element_type=jnp.float32,
-            )
-            summed = summed + lax.optimization_barrier(produced.astype(jnp.bfloat16)).astype(
-                jnp.float32
-            )
-        results.append(summed.astype(jnp.bfloat16).reshape(seq_count, capacity, width))
-    expert_result = jnp.stack(results, axis=1)
-    returned = lax.all_to_all(expert_result, "seq", split_axis=0, concat_axis=0, tiled=True)
-    pair_out = returned.reshape(experts_all * capacity, width)[target]
+        .set(jnp.repeat(both_rows, TOPK, axis=0), mode="drop")
+    )
+    outgoing = jnp.broadcast_to(
+        outgoing.reshape(n_sub, 1, 2, capacity, width), (n_sub, 2, 2, capacity, width)
+    ).reshape(n_within, capacity, width)
+    incoming = lax.all_to_all(outgoing, within, 0, 0, tiled=True)
+    flat_rows = incoming.reshape(-1, width)
+    both = jnp.dot(flat_rows, expert_gate_up, preferred_element_type=jnp.float32)
+    units = (jax.nn.silu(both[:, :ff_half]) * both[:, ff_half:]).astype(jnp.bfloat16)
+    produced_first = jnp.dot(
+        units[:, :ff_quarter], down_first, preferred_element_type=jnp.float32
+    ).astype(jnp.bfloat16)
+    produced_second = jnp.dot(
+        units[:, ff_quarter:], down_second, preferred_element_type=jnp.float32
+    ).astype(jnp.bfloat16)
+    half_sum = (produced_first.astype(jnp.float32) + produced_second.astype(jnp.float32)).astype(
+        jnp.bfloat16
+    )
+    returned = lax.all_to_all(
+        half_sum.reshape(n_within, capacity, width), within, 0, 0, tiled=True
+    ).reshape(n_sub, 2, 2, capacity, width)
+    expert_out = (returned[:, 0].astype(jnp.float32) + returned[:, 1].astype(jnp.float32)).astype(
+        jnp.bfloat16
+    )
+    expert_out = expert_out.reshape(half_experts * capacity, width)
+    pair_out = expert_out[jnp.minimum(target, half_experts * capacity - 1)]
+    pair_gates = jnp.where(local_pair, both_gates.reshape(-1), 0.0)
+    partial = jnp.sum(
+        (pair_gates[:, None] * pair_out.astype(jnp.float32)).reshape(row_count, TOPK, width),
+        axis=1,
+    )
     combined = jnp.sum(
-        gates[:, :, None] * pair_out.reshape(quarter, TOPK, width).astype(jnp.float32), axis=1
+        lax.all_to_all(partial.reshape(n_zh, quarter, width), "zh", 0, 0, tiled=True), axis=0
     )
     own_places = tp_place * quarter + jnp.arange(quarter)
     live_rows = own_places < prompt_length
@@ -232,24 +273,30 @@
 
 
 def solution(mesh):
+    n_seq, n_tp = mesh.devices.shape
+    n_zh = 2
+    n_sub = n_seq // n_zh
+    split_mesh = Mesh(mesh.devices.reshape(n_zh, n_sub, n_tp), ("zh", "sub", "tp"))
+    rows = ("zh", "sub", "tp")
+    seq = ("zh", "sub")
     return jax.shard_map(
-        on_device,
-        mesh=mesh,
+        functools.partial(on_device, n_zh=n_zh, n_sub=n_sub, n_tp=n_tp),
+        mesh=split_mesh,
         in_specs=(
-            P(("seq", "tp"), None),
-            P(),
-            P(("seq", "tp"), None),
+            P(rows, None),
+            P(),
+            P(rows, None),
             P(),
             P(),
             P("tp", None),
             P(),
             P(),
-            P(None, ("seq", "tp"), None),
-            P("seq", "tp", None),
-            P(("seq", "tp"), None),
-            P("seq"),
-            P("seq", None),
+            P(None, rows, None),
+            P(seq, "tp", None),
+            P(rows, None),
+            P(seq),
+            P(seq, None),
         ),
-        out_specs=(P(("seq", "tp"), None), P("seq", None, "tp", None, None)),
+        out_specs=(P(rows, None), P(seq, None, "tp", None, None)),
         check_vma=False,
     )

time: 767 us -> 796 us (1.038)
  waiting for transfers between devices: 537 us -> 368 us
  blocking collectives: 102 us -> 221 us
  local copies, waits for them, and re-layouts: 26.3 us -> 54.9 us
  other arithmetic: 23.1 us -> 51.5 us
  starting transfers between devices: 31.5 us -> 47.6 us
    all_gather x0 -> x4, blocking collectives: none -> 210 us  [the longest x1 131 us: on_device(): both_gates = lax.all_gather(gates, 'zh', axis=0, tiled=True)]
    all_gather x3 -> x2, waiting for transfers between devices: 228 us -> 106 us  [the longest x1 94.7 us: on_device(): head_rows = lax.all_gather(head_rows, 'sub', axis=0, tiled=True)]
    all_to_all x1 -> x0, blocking collectives: 89.9 us -> none  [on_device(): lax.all_to_all(gate_up_master.astype(jnp.bfloat16), 'seq', split_axis=0,...]
    all_to_all x1, waiting for transfers between devices: 58.5 us -> 9.23 us  [summed_on_arrival(): lax.all_to_all(in_blocks(array, dim, peers), axis, 0, 0, tiled=True)]
    all_to_all x3 -> x5, starting transfers between devices: 26.4 us -> 40.8 us  [the longest x1 12.4 us: on_device(): incoming = lax.all_to_all(outgoing, within, 0, 0, tiled=True)]
    another operation x8 -> x6, other arithmetic: 9.23 us -> 20.1 us  [the longest x2 6.32 us: on_device(): expert_result = jnp.stack(results, axis=1)]
    reshape x1 -> x6, local copies, waits for them, and re-layouts: 0.2 us -> 10 us  [the longest x1 4.38 us: on_device(): pieces[..., :FF].reshape(n_zh, n_sub, 2, trainer_block, 2, ff_half)]
    all_to_all x3 -> x5, waiting for transfers between devices: 250 us -> 252 us  [the longest x1 179 us: on_device(): incoming = lax.all_to_all(outgoing, within, 0, 0, tiled=True)]
  transfers between devices with their start and end apart: 7 -> 9, of which waited for: 7 -> 6; matrix products, arithmetic and copies ran while one was open for 6% -> 11% of each run, Pallas kernels for 0% -> 0%
where the time goes in v1:
time: 796 us; the launch traced here: 786 us
  waiting for transfers between devices  368 us (46%)
  blocking collectives  221 us (28%)
  local copies, waits for them, and re-layouts  54.9 us (7%)
  other arithmetic  51.5 us (6%)
  starting transfers between devices  47.6 us (6%)
  matrix products  27.6 us (3%)
  between operations  15.5 us (2%)
    all_to_all x1, waiting for transfers between devices, on_device(): incoming = lax.all_to_all(outgoing, within, 0, 0, tiled=True)  179 us
    all_gather x1, blocking collectives, on_device(): both_gates = lax.all_gather(gates, 'zh', axis=0, tiled=True)  131 us
    all_gather x1, waiting for transfers between devices, on_device(): head_rows = lax.all_gather(head_rows, 'sub', axis=0, tiled=True)  94.7 us
    all_gather x1, blocking collectives, on_device(): both_routes = lax.all_gather(routes, 'zh', axis=0, tiled=True)  56.1 us
    all_to_all x1, waiting for transfers between devices, on_device(): lax.all_to_all(half_sum.reshape(n_within, capacity, width), within, 0, 0,...  51 us
    all_to_all x1, waiting for transfers between devices, on_device(): lax.all_to_all(partial.reshape(n_zh, quarter, width), 'zh', 0, 0, tiled=T...  22.2 us
    another operation x6, other arithmetic  20.1 us
  transfers between devices with their start and end apart: 9, of which 6 were waited for; matrix products, arithmetic and copies ran while one was open for 11% of the time, Pallas kernels for 0%

profile of v1, /device:TPU:2, one launch (start us, length us, event | category | flops | bytes accessed | tf_op | source)
XLA Modules:
  0.0 786.4 jit_solution(13324233152515847075)
XLA Ops:
  8.9 11.5 %all_to_all.46 = bf16[8,4,1280]{2,0,1:T(8,128)(2,1)S(1)} all-to-all(bf16[8,4,1280]{2,0,1:T(8,128)(2,1)S(1)} %pad_maximum_fusion), channel_id=1, replica_groups=mesh['zh'=2,'sub'=32,'tp'=4] {'tp'}, dimensions={1} | all-to-all | bytes 163840 | tf_op jit(solution)/shard_map/all_to_all | solution.py:162
  20.4 10.0 %all_gather.19 = bf16[64,1280]{1,0:T(8,128)(2,1)} all-gather(bf16[32,1280]{1,0:T(8,128)(2,1)S(1)} %bitcast.171), channel_id=1, replica_groups=mesh['zh'=2,'sub'=32,'tp'=4] {'zh'}, dimensions={0}, use_global_device_ids=true | all-gather | bytes 245760 | tf_op jit(solution)/shard_map/all_gather | solution.py:163
  35.4 6.8 all-to-all-start.3
  43.5 11.5 %all-gather.5.cloned.1.call-done = bf16[256,2048]{1,0:T(8,128)(2,1)} async-done(((bf16[64,2048]{1,0:T(8,128)(2,1)}), bf16[256,2048]{1,0:T(8,128)(2,1)}) %all-gather.5.cloned.1.call-update) | async-done | bytes 1048592 | tf_op jit(solution)/shard_map/all_gather | solution.py:144
  57.3 94.7 %all-gather.7.cloned.1.call-done = bf16[2048,1280]{1,0:T(8,128)(2,1)} async-done(((bf16[64,1280]{1,0:T(8,128)(2,1)}), bf16[2048,1280]{1,0:T(8,128)(2,1)}) %all-gather.7.cloned.1.call-update) | async-done | bytes 5242896 | tf_op jit(solution)/shard_map/all_gather | solution.py:164
  178.0 5.6 maximum_bitcast_fusion
  186.0 9.2 %all-to-all-done.1 = bf16[4,64,2048]{2,1,0:T(8,128)(2,1)} async-done(((bf16[4,64,2048]{2,1,0:T(8,128)(2,1)}), bf16[4,64,2048]{2,1,0:T(8,128)(2,1)}, u32[]{:S(2)}, u32[]{:S(2)}) %all-to-all-start.1) | async-done | bytes 1048608 | tf_op jit(solution)/shard_map/all_to_all | solution.py:46
  195.2 8.5 %all-to-all-start.4 = ((bf16[128,16,768]{2,1,0:T(8,128)(2,1)}), bf16[128,16,768]{2,1,0:T(8,128)(2,1)}, u32[]{:S(2)}, u32[]{:S(2)}) async-start(bf16[128,16,768]{2,1,0:T(8,128)(2,1)} %bitcast.162), calls=%async_computation.4 | async-start | bytes 6291456 | tf_op jit(solution)/shard_map/all_to_all | solution.py:131
  203.7 56.1 %all-gather = s32[2,64,8]{1,2,0:T(8,128)S(1)} all-gather(s32[1,64,8]{1,2,0:T(8,128)S(1)} %bitcast.178), channel_id=1, replica_groups=mesh['zh'=2,'sub'=32,'tp'=4] {'zh'}, dimensions={0}, use_global_device_ids=true | all-gather | bytes 6144 | tf_op jit(solution)/shard_map/all_gather | solution.py:206
  260.3 18.0 %reduce-window.6 = s32[64,8,128]{2,1,0:T(8,128)S(1)} reduce-window(s32[64,8,128]{2,1,0:T(8,128)S(1)} %fusion.30, s32[]{:T(128)} %constant.107.clone.1), window={size=1x1x128 pad=0_0x0_0x127_0}, to_apply=%region_7.8 | reduce-window | flops 8323072 | bytes 524292 | tf_op jit(solution)/shard_map/reduce-window
  280.8 12.7 %all_gather.23 = bf16[128,2048]{1,0:T(8,128)(2,1)} all-gather(bf16[64,2048]{1,0:T(8,128)(2,1)S(1)} %multiply_convert_fusion), channel_id=1, replica_groups=mesh['zh'=2,'sub'=32,'tp'=4] {'zh'}, dimensions={0}, use_global_device_ids=true | all-gather | bytes 786432 | tf_op jit(solution)/shard_map/all_gather | solution.py:205
  293.5 9.5 %scatter_custom_fusion = bf16[1024,2048]{1,0:T(8,128)(2,1)} fusion(s32[1024]{0:T(1024)S(1)} %bitcast.182, bf16[128,2048]{1,0:T(8,128)(2,1)} %all_gather.23, bf16[]{:T(256)} %constant.116.clone.1), kind=kCustom, calls=%fused_computation.10 | custom fusion | bytes 4718594 | tf_op jit(solution)/shard_map/scatter | solution.py:222
  303.0 6.8 broadcast_in_dim.107
  309.7 12.4 %all-to-all-start.2 = ((bf16[128,16,2048]{2,1,0:T(8,128)(2,1)}), bf16[128,16,2048]{2,1,0:T(8,128)(2,1)}, u32[]{:S(2)}, u32[]{:S(2)}) async-start(bf16[128,16,2048]{2,1,0:T(8,128)(2,1)} %bitcast.160), calls=%async_computation.2 | async-start | bytes 16777216 | tf_op jit(solution)/shard_map/all_to_all | solution.py:227
  329.8 178.7 %all-to-all-done.2 = bf16[128,16,2048]{2,1,0:T(8,128)(2,1)} async-done(((bf16[128,16,2048]{2,1,0:T(8,128)(2,1)}), bf16[128,16,2048]{2,1,0:T(8,128)(2,1)}, u32[]{:S(2)}, u32[]{:S(2)}) %all-to-all-start.2) | async-done | bytes 8388640 | tf_op jit(solution)/shard_map/all_to_all | solution.py:227
  508.6 10.4 %fusion.64 = f32[2048,768]{0,1:T(8,128)S(1)} fusion(bf16[2048,2048]{1,0:T(8,128)(2,1)} %bitcast.31, bf16[2048,768]{1,0:T(8,128)(2,1)} %bitcast.168), kind=kOutput, calls=%fused_computation.154 | convolution fusion | flops 6442450944 | bytes 17825792 | tf_op jit(solution)/shard_map/dot_general | solution.py:229
  522.8 6.8 add_convert_fusion
  529.6 8.7 %all-to-all-start.5 = ((bf16[128,16,2048]{2,1,0:T(8,128)(2,1)}), bf16[128,16,2048]{2,1,0:T(8,128)(2,1)}, u32[]{:S(2)}, u32[]{:S(2)}) async-start(bf16[128,16,2048]{2,1,0:T(8,128)(2,1)} %bitcast.159), calls=%async_computation.5 | async-start | bytes 16777216 | tf_op jit(solution)/shard_map/all_to_all | solution.py:240
  542.7 130.9 %all-gather.1 = f32[2,64,8]{1,2,0:T(8,128)S(1)} all-gather(f32[1,64,8]{1,2,0:T(8,128)S(1)} %divide_bitcast_fusion), channel_id=1, replica_groups=mesh['zh'=2,'sub'=32,'tp'=4] {'zh'}, dimensions={0}, use_global_device_ids=true | all-gather | bytes 6144 | tf_op jit(solution)/shard_map/all_gather | solution.py:207
  673.8 51.0 %all-to-all-done.5 = bf16[128,16,2048]{2,1,0:T(8,128)(2,1)} async-done(((bf16[128,16,2048]{2,1,0:T(8,128)(2,1)}), bf16[128,16,2048]{2,1,0:T(8,128)(2,1)}, u32[]{:S(2)}, u32[]{:S(2)}) %all-to-all-start.5) | async-done | bytes 8388640 | tf_op jit(solution)/shard_map/all_to_all | solution.py:240
  724.8 5.7 add_convert_fusion.1
  730.5 11.6 %gather_fusion = bf16[1024,2048]{1,0:T(8,128)(2,1)} fusion(bf16[1024,2048]{1,0:T(8,128)(2,1)} %bitcast.158, s32[1024]{0:T(1024)S(1)} %broadcast_clamp_fusion), kind=kCustom, calls=%fused_computation | custom fusion | bytes 8392704 | tf_op jit(solution)/shard_map/gather | solution.py:247
  742.1 7.5 fusion
  755.0 22.2 %all-to-all-done.6 = f32[2,64,2048]{2,1,0:T(8,128)} async-done(((f32[2,64,2048]{2,1,0:T(8,128)}), f32[2,64,2048]{2,1,0:T(8,128)}, u32[]{:S(2)}, u32[]{:S(2)}) %all-to-all-start.6) | async-done | bytes 1048608 | tf_op jit(solution)/shard_map/all_to_all | solution.py:254
  (118 shorter events, 64.1 us)
Async XLA Ops:
  7.2 531.5 %copy-start = (bf16[2048,128]{1,0:T(8,128)(2,1)S(1)}, bf16[2048,128]{1,0:T(8,128)(2,1)}, u32[]{:S(2)}) copy-start(bf16[2048,128]{1,0:T(8,128)(2,1)} %param.20) | copy-start | bytes 1572868
  7.2 47.9 %all-gather.5.cloned.1.call-start = ((), (), s32[]{:S(2)}) async-start(), calls=%async_computation.7 | async-start | bytes 1310720 | tf_op jit(solution)/shard_map/all_gather | solution.py:144
  7.9 144.1 %all-gather.7.cloned.1.call-start = ((), (), s32[]{:S(2)}) async-start(), calls=%async_computation.8 | async-start | bytes 5406720 | tf_op jit(solution)/shard_map/all_gather | solution.py:164
  35.4 128.5 %all-to-all-start.3 = ((bf16[2,64,8,1536]{3,2,1,0:T(8,128)(2,1)}), bf16[2,64,8,1536]{3,2,1,0:T(8,128)(2,1)}, u32[]{:S(2)}, u32[]{:S(2)}) async-start(bf16[2,64,8,1536]{3,2,1,0:T(8,128)(2,1)} %bitcast.163), calls=%async_computation.3 | async-start | bytes 6291456 | tf_op jit(solution)/shard_map/all_to_all | solution.py:125
  42.2 14.6 %copy-start.5 = (f32[2048]{0:T(1024)S(1)}, f32[2048]{0:T(1024)}, u32[]{:S(2)}) copy-start(f32[2048]{0:T(1024)} %param.14) | copy-start | bytes 24580
  156.0 1.1 copy-start.7
  156.1 1.7 copy-start.8
  159.4 2.2 copy-start.9
  163.9 31.3 %all-to-all-start.1 = ((bf16[4,64,2048]{2,1,0:T(8,128)(2,1)}), bf16[4,64,2048]{2,1,0:T(8,128)(2,1)}, u32[]{:S(2)}, u32[]{:S(2)}) async-start(bf16[4,64,2048]{2,1,0:T(8,128)(2,1)} %bitcast.20), calls=%async_computation.1 | async-start | bytes 2097152 | tf_op jit(solution)/shard_map/all_to_all | solution.py:46
  195.2 8.5 %copy-start.4 = (s32[64,8]{0,1:T(8,128)S(1)}, s32[64,8]{0,1:T(8,128)}, u32[]{:S(2)}) copy-start(s32[64,8]{0,1:T(8,128)} %param.23) | copy-start | bytes 6148
  195.2 107.8 %all-to-all-start.4 = ((bf16[128,16,768]{2,1,0:T(8,128)(2,1)}), bf16[128,16,768]{2,1,0:T(8,128)(2,1)}, u32[]{:S(2)}, u32[]{:S(2)}) async-start(bf16[128,16,768]{2,1,0:T(8,128)(2,1)} %bitcast.162), calls=%async_computation.4 | async-start | bytes 6291456 | tf_op jit(solution)/shard_map/all_to_all | solution.py:131
  203.7 76.8 %copy-start.1 = (bf16[64,2048]{1,0:T(8,128)(2,1)S(1)}, bf16[64,2048]{1,0:T(8,128)(2,1)}, u32[]{:S(2)}) copy-start(bf16[64,2048]{1,0:T(8,128)(2,1)} %param.13) | copy-start | bytes 786436
  203.7 77.0 %copy-start.6 = (f32[2048]{0:T(1024)S(1)}, f32[2048]{0:T(1024)}, u32[]{:S(2)}) copy-start(f32[2048]{0:T(1024)} %param.19) | copy-start | bytes 24580
  309.7 198.9 %all-to-all-start.2 = ((bf16[128,16,2048]{2,1,0:T(8,128)(2,1)}), bf16[128,16,2048]{2,1,0:T(8,128)(2,1)}, u32[]{:S(2)}, u32[]{:S(2)}) async-start(bf16[128,16,2048]{2,1,0:T(8,128)(2,1)} %bitcast.160), calls=%async_computation.2 | async-start | bytes 16777216 | tf_op jit(solution)/shard_map/all_to_all | solution.py:227
  324.2 195.8 %collective-permute-start = (bf16[192,2048]{1,0:T(8,128)(2,1)}, bf16[192,2048]{1,0:T(8,128)(2,1)}, u32[]{:S(2)}, u32[]{:S(2)}) collective-permute-start(bf16[192,2048]{1,0:T(8,128)(2,1)} %dynamic-slice_bitcast_fusion), channel_id=1, source_target_pairs={{0,1},{1,0},{2,3},{3,2},{4,5},{5,4},{6,7},{7,6},{8,9},{9,8},{10,11... | collective-permute-start | bytes 2359304 | tf_op jit(solution)/shard_map/ppermute | solution.py:140
  519.0 1.4 copy-start.2
  529.6 195.2 %all-to-all-start.5 = ((bf16[128,16,2048]{2,1,0:T(8,128)(2,1)}), bf16[128,16,2048]{2,1,0:T(8,128)(2,1)}, u32[]{:S(2)}, u32[]{:S(2)}) async-start(bf16[128,16,2048]{2,1,0:T(8,128)(2,1)} %bitcast.159), calls=%async_computation.5 | async-start | bytes 16777216 | tf_op jit(solution)/shard_map/all_to_all | solution.py:240
  742.1 11.9 %copy-start.10 = (s32[1,2]{1,0:T(1,128)S(1)}, s32[1,2]{1,0:T(1,128)}, u32[]{:S(2)}) copy-start(s32[1,2]{1,0:T(1,128)} %param.25) | copy-start | bytes 28
  749.5 27.7 %all-to-all-start.6 = ((f32[2,64,2048]{2,1,0:T(8,128)}), f32[2,64,2048]{2,1,0:T(8,128)}, u32[]{:S(2)}, u32[]{:S(2)}) async-start(f32[2,64,2048]{2,1,0:T(8,128)} %bitcast.167), calls=%async_computation.6 | async-start | bytes 2097152 | tf_op jit(solution)/shard_map/all_to_all | solution.py:254
  754.9 24.4 %copy-start.3 = (bf16[4,2,128,128]{3,2,1,0:T(8,128)(2,1)}, bf16[4,2,128,128]{3,2,1,0:T(8,128)(2,1)S(1)}, u32[]{:S(2)}) copy-start(bf16[4,2,128,128]{3,2,1,0:T(8,128)(2,1)S(1)} %scatter_fusion) | copy-start | bytes 786436
Sparse Core Ops, SparseCore 0:
  9.8 45.1 all-gather.4
  57.6 94.3 all-gather.6

commit v2 on v1

--- a/solution.py
+++ b/solution.py
@@ -103,43 +103,65 @@
     *,
     n_zh,
     n_sub,
+    n_core,
     n_tp,
 ):
     zh = lax.axis_index("zh")
+    core = lax.axis_index("core")
     tp_place = lax.axis_index("tp")
+    everyone = ("zh", "sub2", "core", "tp")
+    group = ("sub2", "tp")
+    n_group = n_sub * n_tp
     quarter = hidden_in.shape[0]
     width = hidden_in.shape[1]
     experts_all = router_weight.shape[1]
     half_experts = experts_all // n_zh
     heads_here = QUERY_HEADS // n_tp
     key_value_local = KEY_VALUE_HEADS // n_tp
-    ff_half = FF // 2
     ff_quarter = FF // n_tp
-    capacity = 2 * 8
-    within = ("sub", "tp")
-    n_within = n_sub * n_tp
-
-    gate_up_half = gate_up_master.astype(jnp.bfloat16)
-    trainer_block = gate_up_half.shape[1]
-    gate_up_half = gate_up_half.reshape(n_zh, half_experts, trainer_block, 2 * FF)
+    capacity = 16
+
+    def flat(a, b, c, d):
+        return ((a * n_sub + b) * n_core + c) * n_tp + d
+
+    primary = (tp_place % 2) == core
+    slots = [lax.dynamic_index_in_dim(down_weight, tp_place // 2, 0, keepdims=False)]
+    for shift in range(1, n_tp):
+        pairs = []
+        for a in range(n_zh):
+            for b in range(n_sub):
+                for c in range(n_core):
+                    for q in range(n_tp):
+                        dest = (q - shift) % n_tp
+                        if dest % 2 == c:
+                            pairs.append((flat(a, b, c, q), flat(a, b, c, dest)))
+        sent = lax.dynamic_index_in_dim(
+            down_weight, ((tp_place - shift) % n_tp) // 2, 0, keepdims=False
+        )
+        slots.append(lax.ppermute(sent, everyone, perm=pairs))
+    slots = jnp.stack(slots)
+    share = []
+    for a in range(n_zh):
+        for b in range(n_sub):
+            for d in range(n_tp):
+                share.append((flat(a, b, d % 2, d), flat(a, b, 1 - d % 2, d)))
+    slots = jnp.where(primary, slots, lax.ppermute(slots, everyone, perm=share))
+
+    trainer_block = gate_up_master.shape[1]
+    gate_up_half = gate_up_master.astype(jnp.bfloat16).reshape(
+        n_zh, half_experts, trainer_block, 2 * FF
+    )
     gate_up_half = lax.all_to_all(gate_up_half, "zh", 0, 0, tiled=True)
-    pieces = gate_up_half.reshape(n_zh, n_sub, 2, trainer_block, 2 * FF)
-    gate_part = pieces[..., :FF].reshape(n_zh, n_sub, 2, trainer_block, 2, ff_half)
-    up_part = pieces[..., FF:].reshape(n_zh, n_sub, 2, trainer_block, 2, ff_half)
-    pieces = jnp.concatenate([gate_part, up_part], axis=-1)
-    pieces = pieces.transpose(1, 4, 2, 0, 3, 5).reshape(n_within, n_zh * trainer_block, FF)
-    pieces = lax.all_to_all(pieces, within, 0, 0, tiled=True)
-    expert_gate_up = (
-        pieces.reshape(n_sub, n_tp, n_zh, trainer_block, FF)
-        .transpose(2, 0, 1, 3, 4)
+    pieces = gate_up_half.reshape(n_zh, n_sub, n_tp, trainer_block, n_core, FF)
+    pieces = jnp.stack([pieces[:, :, 2 * (d % 2) + d // 2] for d in range(n_tp)], axis=2)
+    pieces = pieces.transpose(1, 4, 2, 0, 3, 5).reshape(n_sub * n_core * n_tp, -1, FF)
+    pieces = lax.all_to_all(pieces, ("sub2", "core", "tp"), 0, 0, tiled=True)
+    column_half = (
+        pieces.reshape(n_sub, n_core, n_tp, n_zh, trainer_block, FF)
+        .transpose(3, 0, 1, 2, 4, 5)
         .reshape(-1, FF)
     )
-    parity = tp_place % 2
-    kept = lax.dynamic_index_in_dim(down_weight, parity, 0, keepdims=False)
-    given = lax.dynamic_index_in_dim(down_weight, 1 - parity, 0, keepdims=False)
-    got = lax.ppermute(given, "tp", perm=[(i, i ^ 1) for i in range(n_tp)])
-    down_first = jnp.where(parity == 0, kept, got)
-    down_second = jnp.where(parity == 0, got, kept)
+    expert_gate_up = lax.all_gather(column_half, "core", axis=1, tiled=True)
 
     prompt_rows = lax.all_gather(hidden_in, "tp", axis=0, tiled=True)
     column_span = prompt_rows.shape[0]
@@ -161,11 +183,12 @@
     )
     head_rows = lax.all_to_all(joined, "tp", split_axis=1, concat_axis=0, tiled=True)
     head_rows = lax.all_gather(head_rows, "zh", axis=0, tiled=True)
-    head_rows = lax.all_gather(head_rows, "sub", axis=0, tiled=True)
-    seq_block = head_rows.shape[0] // (n_zh * n_sub)
+    head_rows = lax.all_gather(head_rows, "sub2", axis=0, tiled=True)
+    head_rows = lax.all_gather(head_rows, "core", axis=0, tiled=True)
+    seq_block = head_rows.shape[0] // (n_zh * n_sub * n_core)
     normed_order = (
-        normed.reshape(column_span, n_zh, n_sub, seq_block)
-        .transpose(0, 2, 1, 3)
+        normed.reshape(column_span, n_zh, n_sub, n_core, seq_block)
+        .transpose(0, 3, 2, 1, 4)
         .reshape(column_span, -1)
     )
     projected_rows = jnp.dot(normed_order, head_rows, preferred_element_type=jnp.float32)
@@ -197,55 +220,51 @@
     )
     after_attn = hidden_in.astype(jnp.float32) + attention_sums
     mixed = rms_scale(after_attn, post_gain).astype(jnp.bfloat16)
-    logits = jnp.dot(mixed, router_weight, preferred_element_type=jnp.float32)
-    chosen = jnp.take_along_axis(logits, routes, axis=1)
+
+    both_routes = lax.all_gather(routes, "zh", axis=0, tiled=True)
+    both_rows = lax.all_gather(mixed, "zh", axis=0, tiled=True)
+    row_count = both_rows.shape[0]
+    logits = jnp.dot(both_rows, router_weight, preferred_element_type=jnp.float32)
+    chosen = jnp.take_along_axis(logits, both_routes, axis=1)
     raised = jnp.exp(chosen)
     gates = raised / jnp.sum(raised, axis=1, keepdims=True)
-
-    both_rows = lax.all_gather(mixed, "zh", axis=0, tiled=True)
-    both_routes = lax.all_gather(routes, "zh", axis=0, tiled=True)
-    both_gates = lax.all_gather(gates, "zh", axis=0, tiled=True)
-    row_count = both_rows.shape[0]
     pair_expert = both_routes.reshape(-1)
     local_pair = (pair_expert // half_experts) == zh
     local_expert = pair_expert % half_experts
+    within_line = local_expert % n_tp
+    place = (local_expert // n_tp) * n_tp + 2 * (within_line % 2) + within_line // 2
     hits = (
-        (local_expert[:, None] == jnp.arange(half_experts, dtype=jnp.int32)[None, :])
+        (place[:, None] == jnp.arange(half_experts, dtype=jnp.int32)[None, :])
         & local_pair[:, None]
     ).astype(jnp.int32)
     before = jnp.cumsum(hits, axis=0) - hits
     slot_index = jnp.sum(before * hits, axis=1)
-    target = jnp.where(local_pair, local_expert * capacity + slot_index, half_experts * capacity)
+    target = jnp.where(local_pair, place * capacity + slot_index, half_experts * capacity)
     outgoing = (
         jnp.zeros((half_experts * capacity, width), jnp.bfloat16)
         .at[target]
         .set(jnp.repeat(both_rows, TOPK, axis=0), mode="drop")
     )
-    outgoing = jnp.broadcast_to(
-        outgoing.reshape(n_sub, 1, 2, capacity, width), (n_sub, 2, 2, capacity, width)
-    ).reshape(n_within, capacity, width)
-    incoming = lax.all_to_all(outgoing, within, 0, 0, tiled=True)
+    incoming = lax.all_to_all(
+        outgoing.reshape(n_group, capacity, width), group, 0, 0, tiled=True
+    )
     flat_rows = incoming.reshape(-1, width)
     both = jnp.dot(flat_rows, expert_gate_up, preferred_element_type=jnp.float32)
-    units = (jax.nn.silu(both[:, :ff_half]) * both[:, ff_half:]).astype(jnp.bfloat16)
-    produced_first = jnp.dot(
-        units[:, :ff_quarter], down_first, preferred_element_type=jnp.float32
-    ).astype(jnp.bfloat16)
-    produced_second = jnp.dot(
-        units[:, ff_quarter:], down_second, preferred_element_type=jnp.float32
-    ).astype(jnp.bfloat16)
-    half_sum = (produced_first.astype(jnp.float32) + produced_second.astype(jnp.float32)).astype(
-        jnp.bfloat16
-    )
-    returned = lax.all_to_all(
-        half_sum.reshape(n_within, capacity, width), within, 0, 0, tiled=True
-    ).reshape(n_sub, 2, 2, capacity, width)
-    expert_out = (returned[:, 0].astype(jnp.float32) + returned[:, 1].astype(jnp.float32)).astype(
-        jnp.bfloat16
-    )
-    expert_out = expert_out.reshape(half_experts * capacity, width)
-    pair_out = expert_out[jnp.minimum(target, half_experts * capacity - 1)]
-    pair_gates = jnp.where(local_pair, both_gates.reshape(-1), 0.0)
+    units = (jax.nn.silu(both[:, :FF]) * both[:, FF:]).astype(jnp.bfloat16)
+    summed = jnp.zeros((flat_rows.shape[0], width), jnp.float32)
+    for slot in range(n_tp):
+        lower = ((tp_place + slot) % n_tp) * ff_quarter
+        block = lax.dynamic_slice_in_dim(units, lower, ff_quarter, axis=1)
+        produced = jnp.dot(block, slots[slot], preferred_element_type=jnp.float32)
+        summed = summed + lax.optimization_barrier(produced.astype(jnp.bfloat16)).astype(
+            jnp.float32
+        )
+    expert_result = summed.astype(jnp.bfloat16).reshape(n_group, capacity, width)
+    returned = lax.all_to_all(expert_result, group, 0, 0, tiled=True)
+    pair_out = returned.reshape(half_experts * capacity, width)[
+        jnp.minimum(target, half_experts * capacity - 1)
+    ]
+    pair_gates = jnp.where(local_pair, gates.reshape(-1), 0.0)
     partial = jnp.sum(
         (pair_gates[:, None] * pair_out.astype(jnp.float32)).reshape(row_count, TOPK, width),
         axis=1,
@@ -275,12 +294,15 @@
 def solution(mesh):
     n_seq, n_tp = mesh.devices.shape
     n_zh = 2
-    n_sub = n_seq // n_zh
-    split_mesh = Mesh(mesh.devices.reshape(n_zh, n_sub, n_tp), ("zh", "sub", "tp"))
-    rows = ("zh", "sub", "tp")
-    seq = ("zh", "sub")
+    n_core = 2
+    n_sub = n_seq // (n_zh * n_core)
+    split_mesh = Mesh(
+        mesh.devices.reshape(n_zh, n_sub, n_core, n_tp), ("zh", "sub2", "core", "tp")
+    )
+    rows = ("zh", "sub2", "core", "tp")
+    seq = ("zh", "sub2", "core")
     return jax.shard_map(
-        functools.partial(on_device, n_zh=n_zh, n_sub=n_sub, n_tp=n_tp),
+        functools.partial(on_device, n_zh=n_zh, n_sub=n_sub, n_core=n_core, n_tp=n_tp),
         mesh=split_mesh,
         in_specs=(
             P(rows, None),

time: 796 us -> 689 us (0.87)
  blocking collectives: 221 us -> 88.9 us
  waiting for transfers between devices: 368 us -> 392 us
  starting transfers between devices: 47.6 us -> 55.8 us
    all_to_all x3, waiting for transfers between devices: 230 us -> 89.7 us  [the longest x1 89.7 us: on_device(): returned = lax.all_to_all(expert_result, group, 0, 0, tiled=True)]
    all_gather x1 -> x0, blocking collectives: 131 us -> none  [on_device(): both_gates = lax.all_gather(gates, 'zh', axis=0, tiled=True)]
    ppermute x1 -> x4, waiting for transfers between devices: 0.01 us -> 115 us  [the longest x3 112 us: on_device(): slots.append(lax.ppermute(sent, everyone, perm=pairs))]
    all_gather x1, waiting for transfers between devices: 11.5 us -> 45.9 us  [on_device(): prompt_rows = lax.all_gather(hidden_in, 'tp', axis=0, tiled=True)]
    all_gather x1 -> x3, waiting for transfers between devices: 94.7 us -> 105 us  [the longest x1 55.6 us: on_device(): head_rows = lax.all_gather(head_rows, 'core', axis=0, tiled=True)]
    ppermute x1 -> x4, starting transfers between devices: 1.61 us -> 10 us  [the longest x3 6.86 us: on_device(): slots.append(lax.ppermute(sent, everyone, perm=pairs))]
    another operation x6 -> x7, other arithmetic: 20.1 us -> 22.1 us
  transfers between devices with their start and end apart: 9 -> 14, of which waited for: 6 -> 10; matrix products, arithmetic and copies ran while one was open for 11% -> 12% of each run, Pallas kernels for 0% -> 0%
where the time goes in v2:
time: 689 us; the launch traced here: 682 us
  waiting for transfers between devices  392 us (57%)
  blocking collectives  88.9 us (13%)
  starting transfers between devices  55.8 us (8%)
  local copies, waits for them, and re-layouts  53.2 us (8%)
  other arithmetic  53.2 us (8%)
  matrix products  23.3 us (3%)
  between operations  15.8 us (2%)
    ppermute x3, waiting for transfers between devices, on_device(): slots.append(lax.ppermute(sent, everyone, perm=pairs))  112 us
    all_to_all x1, waiting for transfers between devices, on_device(): returned = lax.all_to_all(expert_result, group, 0, 0, tiled=True)  89.7 us
    all_gather x1, waiting for transfers between devices, on_device(): head_rows = lax.all_gather(head_rows, 'core', axis=0, tiled=True)  55.6 us
    all_gather x1, blocking collectives, on_device(): both_routes = lax.all_gather(routes, 'zh', axis=0, tiled=True)  55.4 us
    all_gather x1, waiting for transfers between devices, on_device(): head_rows = lax.all_gather(head_rows, 'sub2', axis=0, tiled=True)  49.7 us
    all_gather x1, waiting for transfers between devices, on_device(): prompt_rows = lax.all_gather(hidden_in, 'tp', axis=0, tiled=True)  45.9 us
    all_to_all x1, waiting for transfers between devices, on_device(): lax.all_to_all(partial.reshape(n_zh, quarter, width), 'zh', 0, 0, tiled=T...  26.8 us
    another operation x6, other arithmetic  20.2 us
  transfers between devices with their start and end apart: 14, of which 10 were waited for; matrix products, arithmetic and copies ran while one was open for 12% of the time, Pallas kernels for 0%

profile of v2, /device:TPU:2, one launch (start us, length us, event | category | flops | bytes accessed | tf_op | source)
XLA Modules:
  0.0 682.0 jit_solution(12399408086061135520)
XLA Ops:
  8.2 11.5 %all_to_all.46 = bf16[8,4,1280]{2,0,1:T(8,128)(2,1)S(1)} all-to-all(bf16[8,4,1280]{2,0,1:T(8,128)(2,1)S(1)} %pad_maximum_fusion.1), channel_id=1, replica_groups=mesh['zh'=2,'sub2'=16,'core'=2,'tp'=4] {'tp'}, dimensions={1} | all-to-all | bytes 163840 | tf_op jit(solution)/shard_map/all_to_all | solution.py:184
  19.7 10.0 %all_gather.22 = bf16[64,1280]{1,0:T(8,128)(2,1)} all-gather(bf16[32,1280]{1,0:T(8,128)(2,1)S(1)} %bitcast.173), channel_id=1, replica_groups=mesh['zh'=2,'sub2'=16,'core'=2,'tp'=4] {'zh'}, dimensions={0}, use_global_device_ids=true | all-gather | bytes 245760 | tf_op jit(solution)/shard_map/all_gather | solution.py:185
  30.5 49.7 %all-gather.8.cloned.1.call-done = bf16[1024,1280]{1,0:T(8,128)(2,1)} async-done(((bf16[64,1280]{1,0:T(8,128)(2,1)}), bf16[1024,1280]{1,0:T(8,128)(2,1)}) %all-gather.8.cloned.1.call-update) | async-done | bytes 2621456 | tf_op jit(solution)/shard_map/all_gather | solution.py:186
  85.2 7.0 %all-to-all-start.3 = ((bf16[2,64,8,1536]{3,2,1,0:T(8,128)(2,1)}), bf16[2,64,8,1536]{3,2,1,0:T(8,128)(2,1)}, u32[]{:S(2)}, u32[]{:S(2)}) async-start(bf16[2,64,8,1536]{3,2,1,0:T(8,128)(2,1)} %bitcast.161), calls=%async_computation.3 | async-start | bytes 6291456 | tf_op jit(solution)/shard_map/all_to_all | solution.py:154
  93.5 45.9 %all-gather.6.cloned.1.call-done = bf16[256,2048]{1,0:T(8,128)(2,1)} async-done(((bf16[64,2048]{1,0:T(8,128)(2,1)}), bf16[256,2048]{1,0:T(8,128)(2,1)}) %all-gather.6.cloned.1.call-update) | async-done | bytes 1048592 | tf_op jit(solution)/shard_map/all_gather | solution.py:166
  141.7 55.6 %all-gather.10.cloned.1.call-done = bf16[2048,1280]{1,0:T(8,128)(2,1)} async-done(((bf16[1024,1280]{1,0:T(8,128)(2,1)}), bf16[2048,1280]{1,0:T(8,128)(2,1)}) %all-gather.10.cloned.1.call-update) | async-done | bytes 5242896 | tf_op jit(solution)/shard_map/all_gather | solution.py:187
  214.2 7.5 %reshape.763 = bf16[2,16,4,8,2,768]{5,4,3,2,1,0:T(2,128)(2,1)} reshape(bf16[2,64,8,1536]{3,2,1,0:T(8,128)(2,1)} %all-to-all-done.3) | data formatting | bytes 6291456 | tf_op jit(solution)/shard_map/reshape | solution.py:155
  232.5 7.9 %all-to-all-done.1 = bf16[4,64,2048]{2,1,0:T(8,128)(2,1)S(1)} async-done(((bf16[4,64,2048]{2,1,0:T(8,128)(2,1)}), bf16[4,64,2048]{2,1,0:T(8,128)(2,1)S(1)}, u32[]{:S(2)}, u32[]{:S(2)}) %all-to-all-start.1) | async-done | bytes 1048608 | tf_op jit(solution)/shard_map/all_to_all | solution.py:46
  240.4 10.0 %all-to-all-start.4 = ((bf16[128,16,768]{2,1,0:T(8,128)(2,1)}), bf16[128,16,768]{2,1,0:T(8,128)(2,1)}, u32[]{:S(2)}, u32[]{:S(2)}) async-start(bf16[128,16,768]{2,1,0:T(8,128)(2,1)} %bitcast.160), calls=%async_computation.4 | async-start | bytes 6291456 | tf_op jit(solution)/shard_map/all_to_all | solution.py:158
  250.5 55.4 %all-gather = s32[2,64,8]{1,2,0:T(8,128)S(1)} all-gather(s32[1,64,8]{1,2,0:T(8,128)S(1)} %bitcast.183), channel_id=1, replica_groups=mesh['zh'=2,'sub2'=16,'core'=2,'tp'=4] {'zh'}, dimensions={0}, use_global_device_ids=true | all-gather | bytes 6144 | tf_op jit(solution)/shard_map/all_gather | solution.py:224
  306.3 18.0 %reduce-window.6 = s32[64,8,128]{2,1,0:T(8,128)S(1)} reduce-window(s32[64,8,128]{2,1,0:T(8,128)S(1)} %fusion.27, s32[]{:T(128)} %constant.208.clone.1), window={size=1x1x128 pad=0_0x0_0x127_0}, to_apply=%region_7.8 | reduce-window | flops 8323072 | bytes 524292 | tf_op jit(solution)/shard_map/reduce-window
  325.6 12.0 %all_gather.26 = bf16[128,2048]{1,0:T(8,128)(2,1)S(1)} all-gather(bf16[64,2048]{1,0:T(8,128)(2,1)S(1)} %multiply_convert_fusion), channel_id=1, replica_groups=mesh['zh'=2,'sub2'=16,'core'=2,'tp'=4] {'zh'}, dimensions={0}, use_global_device_ids=true | all-gather | bytes 786432 | tf_op jit(solution)/shard_map/all_gather | solution.py:225
  337.7 9.1 %scatter_custom_fusion = bf16[1024,2048]{1,0:T(8,128)(2,1)} fusion(s32[1024]{0:T(1024)S(1)} %bitcast.184, bf16[128,2048]{1,0:T(8,128)(2,1)S(1)} %all_gather.26, bf16[]{:T(256)} %constant.217.clone.1), kind=kCustom, calls=%fused_computation.7 | custom fusion | bytes 4718594 | tf_op jit(solution)/shard_map/scatter | solution.py:246
  346.8 11.2 %all-to-all-start.2 = ((bf16[64,16,2048]{2,1,0:T(8,128)(2,1)}), bf16[64,16,2048]{2,1,0:T(8,128)(2,1)}, u32[]{:S(2)}, u32[]{:S(2)}) async-start(bf16[64,16,2048]{2,1,0:T(8,128)(2,1)} %bitcast.158), calls=%async_computation.2 | async-start | bytes 8388608 | tf_op jit(solution)/shard_map/all_to_all | solution.py:248
  370.7 49.0 %collective-permute-done = bf16[192,2048]{1,0:T(8,128)(2,1)S(1)} collective-permute-done((bf16[192,2048]{1,0:T(8,128)(2,1)S(1)}, bf16[192,2048]{1,0:T(8,128)(2,1)S(1)}, u32[]{:S(2)}, u32[]{:S(2)}) %collective-permute-start) | collective-permute-done | bytes 786464 | tf_op jit(solution)/shard_map/ppermute | solution.py:141
  419.6 33.0 %collective-permute-done.2 = bf16[192,2048]{1,0:T(8,128)(2,1)S(1)} collective-permute-done((bf16[192,2048]{1,0:T(8,128)(2,1)S(1)}, bf16[192,2048]{1,0:T(8,128)(2,1)S(1)}, u32[]{:S(2)}, u32[]{:S(2)}) %collective-permute-start.2) | collective-permute-done | bytes 786464 | tf_op jit(solution)/shard_map/ppermute | solution.py:141
  452.7 29.7 %collective-permute-done.1 = bf16[192,2048]{1,0:T(8,128)(2,1)S(1)} collective-permute-done((bf16[192,2048]{1,0:T(8,128)(2,1)S(1)}, bf16[192,2048]{1,0:T(8,128)(2,1)S(1)}, u32[]{:S(2)}, u32[]{:S(2)}) %collective-permute-start.1) | collective-permute-done | bytes 786464 | tf_op jit(solution)/shard_map/ppermute | solution.py:141
  494.1 10.0 %fusion.83 = f32[1024,1536]{1,0:T(8,128)S(1)} fusion(bf16[1024,2048]{1,0:T(8,128)(2,1)} %bitcast.29, bf16[2048,1536]{1,0:T(8,128)(2,1)} %all-gather.12.cloned.1.call-done), kind=kOutput, calls=%fused_computation.215 | convolution fusion | flops 6442450944 | bytes 16777216 | tf_op jit(solution)/shard_map/dot_general | solution.py:252
  516.4 8.8 %all-to-all-start.5 = ((bf16[64,16,2048]{2,1,0:T(8,128)(2,1)}), bf16[64,16,2048]{2,1,0:T(8,128)(2,1)}, u32[]{:S(2)}, u32[]{:S(2)}) async-start(bf16[64,16,2048]{2,1,0:T(8,128)(2,1)} %bitcast.157), calls=%async_computation.5 | async-start | bytes 8388608 | tf_op jit(solution)/shard_map/all_to_all | solution.py:263
  525.8 6.8 gather_fusion.1
  532.9 89.7 %all-to-all-done.5 = bf16[64,16,2048]{2,1,0:T(8,128)(2,1)} async-done(((bf16[64,16,2048]{2,1,0:T(8,128)(2,1)}), bf16[64,16,2048]{2,1,0:T(8,128)(2,1)}, u32[]{:S(2)}, u32[]{:S(2)}) %all-to-all-start.5) | async-done | bytes 4194336 | tf_op jit(solution)/shard_map/all_to_all | solution.py:263
  622.6 11.6 %gather_fusion = bf16[1024,2048]{1,0:T(8,128)(2,1)} fusion(bf16[1024,2048]{1,0:T(8,128)(2,1)} %bitcast.47, s32[1024]{0:T(1024)S(1)} %broadcast_clamp_fusion), kind=kCustom, calls=%fused_computation | custom fusion | bytes 8392704 | tf_op jit(solution)/shard_map/gather | solution.py:264
  634.2 7.5 %fusion = f32[128,2048]{1,0:T(8,128)} fusion(bf16[1024,2048]{1,0:T(8,128)(2,1)} %gather_fusion, f32[128,8]{1,0:T(8,128)S(1)} %copy.112), kind=kLoop, calls=%fused_computation.5 | loop fusion | flops 6029312 | bytes 5246976 | tf_op jit(solution)/shard_map/reduce_sum | solution.py:268
  647.3 26.8 %all-to-all-done.6 = f32[2,64,2048]{2,1,0:T(8,128)S(1)} async-done(((f32[2,64,2048]{2,1,0:T(8,128)}), f32[2,64,2048]{2,1,0:T(8,128)S(1)}, u32[]{:S(2)}, u32[]{:S(2)}) %all-to-all-start.6) | async-done | bytes 1048608 | tf_op jit(solution)/shard_map/all_to_all | solution.py:273
  (148 shorter events, 82.5 us)
Async XLA Ops:
  7.2 518.3 %copy-start = (bf16[2048,128]{1,0:T(8,128)(2,1)S(1)}, bf16[2048,128]{1,0:T(8,128)(2,1)}, u32[]{:S(2)}) copy-start(bf16[2048,128]{1,0:T(8,128)(2,1)} %param.20) | copy-start | bytes 1572868
  7.2 73.1 %all-gather.8.cloned.1.call-start = ((), (), s32[]{:S(2)}) async-start(), calls=%async_computation.8 | async-start | bytes 2785280 | tf_op jit(solution)/shard_map/all_gather | solution.py:186
  29.7 109.7 %all-gather.6.cloned.1.call-start = ((), (), s32[]{:S(2)}) async-start(), calls=%async_computation.7 | async-start | bytes 1310720 | tf_op jit(solution)/shard_map/all_gather | solution.py:166
  30.5 166.8 %all-gather.10.cloned.1.call-start = ((), (), s32[]{:S(2)}) async-start(), calls=%async_computation.9 | async-start | bytes 7864320 | tf_op jit(solution)/shard_map/all_gather | solution.py:187
  85.2 124.1 %all-to-all-start.3 = ((bf16[2,64,8,1536]{3,2,1,0:T(8,128)(2,1)}), bf16[2,64,8,1536]{3,2,1,0:T(8,128)(2,1)}, u32[]{:S(2)}, u32[]{:S(2)}) async-start(bf16[2,64,8,1536]{3,2,1,0:T(8,128)(2,1)} %bitcast.161), calls=%async_computation.3 | async-start | bytes 6291456 | tf_op jit(solution)/shard_map/all_to_all | solution.py:154
  92.2 49.0 %copy-start.12 = (f32[2048]{0:T(1024)S(1)}, f32[2048]{0:T(1024)}, u32[]{:S(2)}) copy-start(f32[2048]{0:T(1024)} %param.14) | copy-start | bytes 24580
  92.9 48.0 %copy-start.15 = (pred[256]{0:T(512)(128)(4,1)}, pred[256]{0:T(512)(128)(4,1)S(1)}, u32[]{:S(2)}) copy-start(pred[256]{0:T(512)(128)(4,1)S(1)} %iota_compare_fusion.3) | copy-start | bytes 772
  209.2 31.1 %all-to-all-start.1 = ((bf16[4,64,2048]{2,1,0:T(8,128)(2,1)}), bf16[4,64,2048]{2,1,0:T(8,128)(2,1)S(1)}, u32[]{:S(2)}, u32[]{:S(2)}) async-start(bf16[4,64,2048]{2,1,0:T(8,128)(2,1)} %bitcast.20), calls=%async_computation.1 | async-start | bytes 2097152 | tf_op jit(solution)/shard_map/all_to_all | solution.py:46
  240.4 106.4 %all-to-all-start.4 = ((bf16[128,16,768]{2,1,0:T(8,128)(2,1)}), bf16[128,16,768]{2,1,0:T(8,128)(2,1)}, u32[]{:S(2)}, u32[]{:S(2)}) async-start(bf16[128,16,768]{2,1,0:T(8,128)(2,1)} %bitcast.160), calls=%async_computation.4 | async-start | bytes 6291456 | tf_op jit(solution)/shard_map/all_to_all | solution.py:158
  250.4 74.9 %copy-start.6 = (bf16[64,2048]{1,0:T(8,128)(2,1)S(1)}, bf16[64,2048]{1,0:T(8,128)(2,1)}, u32[]{:S(2)}) copy-start(bf16[64,2048]{1,0:T(8,128)(2,1)} %param.13) | copy-start | bytes 786436
  250.4 75.1 %copy-start.13 = (f32[2048]{0:T(1024)S(1)}, f32[2048]{0:T(1024)}, u32[]{:S(2)}) copy-start(f32[2048]{0:T(1024)} %param.19) | copy-start | bytes 24580
  346.8 147.3 %all-to-all-start.2 = ((bf16[64,16,2048]{2,1,0:T(8,128)(2,1)}), bf16[64,16,2048]{2,1,0:T(8,128)(2,1)}, u32[]{:S(2)}, u32[]{:S(2)}) async-start(bf16[64,16,2048]{2,1,0:T(8,128)(2,1)} %bitcast.158), calls=%async_computation.2 | async-start | bytes 8388608 | tf_op jit(solution)/shard_map/all_to_all | solution.py:248
  358.0 136.1 %all-gather.12.cloned.1.call-start = ((), (), s32[]{:S(2)}) async-start(), calls=%async_computation.10 | async-start | bytes 9437184 | tf_op jit(solution)/shard_map/all_gather | solution.py:164
  363.8 55.8 %collective-permute-start = (bf16[192,2048]{1,0:T(8,128)(2,1)S(1)}, bf16[192,2048]{1,0:T(8,128)(2,1)S(1)}, u32[]{:S(2)}, u32[]{:S(2)}) collective-permute-start(bf16[192,2048]{1,0:T(8,128)(2,1)S(1)} %get-tuple-element.21), channel_id=1, source_target_pairs={{1,0},{3,2},{4,7},{6,5},{9,8},{11,10},{12,15},{14,13},{17,16},{19,... | collective-permute-start | bytes 2359304 | tf_op jit(solution)/shard_map/ppermute | solution.py:141
  365.1 87.6 %collective-permute-start.2 = (bf16[192,2048]{1,0:T(8,128)(2,1)S(1)}, bf16[192,2048]{1,0:T(8,128)(2,1)S(1)}, u32[]{:S(2)}, u32[]{:S(2)}) collective-permute-start(bf16[192,2048]{1,0:T(8,128)(2,1)S(1)} %get-tuple-element.22), channel_id=1, source_target_pairs={{1,2},{3,0},{4,5},{6,7},{9,10},{11,8},{12,13},{14,15},{17,18},{19,... | collective-permute-start | bytes 2359304 | tf_op jit(solution)/shard_map/ppermute | solution.py:141
  366.4 115.9 %collective-permute-start.1 = (bf16[192,2048]{1,0:T(8,128)(2,1)S(1)}, bf16[192,2048]{1,0:T(8,128)(2,1)S(1)}, u32[]{:S(2)}, u32[]{:S(2)}) collective-permute-start(bf16[192,2048]{1,0:T(8,128)(2,1)S(1)} %get-tuple-element.23), channel_id=1, source_target_pairs={{0,2},{2,0},{5,7},{7,5},{8,10},{10,8},{13,15},{15,13},{16,18},{18,... | collective-permute-start | bytes 2359304 | tf_op jit(solution)/shard_map/ppermute | solution.py:141
  484.3 6.9 %collective-permute-start.3 = (bf16[4,192,2048]{2,1,0:T(8,128)(2,1)}, bf16[4,192,2048]{2,1,0:T(8,128)(2,1)}, u32[]{:S(2)}, u32[]{:S(2)}) collective-permute-start(bf16[4,192,2048]{2,1,0:T(8,128)(2,1)} %pad_maximum_fusion), channel_id=1, source_target_pairs={{0,4},{5,1},{2,6},{7,3},{8,12},{13,9},{10,14},{15,11},{16,20},{21,... | collective-permute-start | bytes 9437192 | tf_op jit(solution)/shard_map/ppermute | solution.py:148
  516.4 106.3 %all-to-all-start.5 = ((bf16[64,16,2048]{2,1,0:T(8,128)(2,1)}), bf16[64,16,2048]{2,1,0:T(8,128)(2,1)}, u32[]{:S(2)}, u32[]{:S(2)}) async-start(bf16[64,16,2048]{2,1,0:T(8,128)(2,1)} %bitcast.157), calls=%async_computation.5 | async-start | bytes 8388608 | tf_op jit(solution)/shard_map/all_to_all | solution.py:263
  634.2 11.2 %copy-start.20 = (s32[1,2]{1,0:T(1,128)S(1)}, s32[1,2]{1,0:T(1,128)}, u32[]{:S(2)}) copy-start(s32[1,2]{1,0:T(1,128)} %param.25) | copy-start | bytes 28
  634.2 11.2 %copy-start.11 = (bf16[256,1,64]{2,0,1:T(8,128)(2,1)S(1)}, bf16[256,1,64]{2,0,1:T(8,128)(2,1)}, u32[]{:S(2)}) copy-start(bf16[256,1,64]{2,0,1:T(8,128)(2,1)} %copy-done.10) | copy-start | bytes 98308
  634.2 11.4 %copy-start.16 = (pred[256]{0:T(512)(128)(4,1)S(1)}, pred[256]{0:T(512)(128)(4,1)}, u32[]{:S(2)}) copy-start(pred[256]{0:T(512)(128)(4,1)} %copy-done.15) | copy-start | bytes 772
  641.7 32.6 %copy-start.7 = (bf16[64,2048]{1,0:T(8,128)(2,1)S(1)}, bf16[64,2048]{1,0:T(8,128)(2,1)}, u32[]{:S(2)}) copy-start(bf16[64,2048]{1,0:T(8,128)(2,1)} %param.13) | copy-start | bytes 786436
  641.7 32.5 %all-to-all-start.6 = ((f32[2,64,2048]{2,1,0:T(8,128)}), f32[2,64,2048]{2,1,0:T(8,128)S(1)}, u32[]{:S(2)}, u32[]{:S(2)}) async-start(f32[2,64,2048]{2,1,0:T(8,128)} %bitcast.50), calls=%async_computation.6 | async-start | bytes 2097152 | tf_op jit(solution)/shard_map/all_to_all | solution.py:273
  647.3 27.7 %copy-start.9 = (bf16[4,2,128,128]{3,2,1,0:T(8,128)(2,1)}, bf16[4,2,128,128]{3,2,1,0:T(8,128)(2,1)S(1)}, u32[]{:S(2)}) copy-start(bf16[4,2,128,128]{3,2,1,0:T(8,128)(2,1)S(1)} %scatter_fusion) | copy-start | bytes 786436
  (11 other events, 43.7 us)
Sparse Core Ops, SparseCore 0:
  29.9 50.3 all-gather.7
  82.1 57.2 all-gather.5
  141.2 56.0 all-gather.9
  362.1 21.0 all-gather.11

commit v3 on v2

--- a/solution.py
+++ b/solution.py
@@ -146,6 +146,8 @@
             for d in range(n_tp):
                 share.append((flat(a, b, d % 2, d), flat(a, b, 1 - d % 2, d)))
     slots = jnp.where(primary, slots, lax.ppermute(slots, everyone, perm=share))
+    both_routes = lax.all_gather(routes, "zh", axis=0, tiled=True)
+    slots, both_routes, hidden_in = lax.optimization_barrier((slots, both_routes, hidden_in))
 
     trainer_block = gate_up_master.shape[1]
     gate_up_half = gate_up_master.astype(jnp.bfloat16).reshape(
@@ -221,7 +223,6 @@
     after_attn = hidden_in.astype(jnp.float32) + attention_sums
     mixed = rms_scale(after_attn, post_gain).astype(jnp.bfloat16)
 
-    both_routes = lax.all_gather(routes, "zh", axis=0, tiled=True)
     both_rows = lax.all_gather(mixed, "zh", axis=0, tiled=True)
     row_count = both_rows.shape[0]
     logits = jnp.dot(both_rows, router_weight, preferred_element_type=jnp.float32)
@@ -237,8 +238,12 @@
         (place[:, None] == jnp.arange(half_experts, dtype=jnp.int32)[None, :])
         & local_pair[:, None]
     ).astype(jnp.int32)
-    before = jnp.cumsum(hits, axis=0) - hits
-    slot_index = jnp.sum(before * hits, axis=1)
+    pair_count = hits.shape[0]
+    earlier = (
+        jnp.arange(pair_count)[:, None] > jnp.arange(pair_count)[None, :]
+    ).astype(jnp.bfloat16)
+    before = jnp.dot(earlier, hits.astype(jnp.bfloat16), preferred_element_type=jnp.float32)
+    slot_index = jnp.sum(before * hits.astype(jnp.float32), axis=1).astype(jnp.int32)
     target = jnp.where(local_pair, place * capacity + slot_index, half_experts * capacity)
     outgoing = (
         jnp.zeros((half_experts * capacity, width), jnp.bfloat16)

time: 689 us -> 642 us (0.932)
  waiting for transfers between devices: 392 us -> 363 us
  other arithmetic: 53.2 us -> 37.1 us
  blocking collectives: 88.9 us -> 81.8 us
    ppermute x3, waiting for transfers between devices: 112 us -> 31.4 us  [on_device(): slots.append(lax.ppermute(sent, everyone, perm=pairs))]
    all_to_all x1, waiting for transfers between devices: 0.01 us -> 69 us  [on_device(): lax.all_to_all(outgoing.reshape(n_group, capacity, width), group, 0, 0, t...]
    all_gather x1, blocking collectives: 12 us -> 63.5 us  [on_device(): both_rows = lax.all_gather(mixed, 'zh', axis=0, tiled=True)]
    all_gather x1, waiting for transfers between devices: 49.7 us -> 0.02 us  [on_device(): head_rows = lax.all_gather(head_rows, 'sub2', axis=0, tiled=True)]
    all_gather x1, blocking collectives: 55.4 us -> 8.25 us  [on_device(): both_routes = lax.all_gather(routes, 'zh', axis=0, tiled=True)]
    all_gather x1, waiting for transfers between devices: 0.01 us -> 22.7 us  [on_device(): expert_gate_up = lax.all_gather(column_half, 'core', axis=1, tiled=True)]
    another operation x6 -> x3, other arithmetic: 20.2 us -> 2.01 us
    all_to_all x1 -> x0, blocking collectives: 11.5 us -> none  [on_device(): lax.all_to_all(joined, 'tp', split_axis=1, concat_axis=0, tiled=True)]
  transfers between devices with their start and end apart: 14 -> 15, of which waited for: 10 -> 12; matrix products, arithmetic and copies ran while one was open for 12% -> 11% of each run, Pallas kernels for 0% -> 0%
where the time goes in v3:
time: 642 us; the launch traced here: 631 us
  waiting for transfers between devices  363 us (57%)
  blocking collectives  81.8 us (13%)
  starting transfers between devices  55.4 us (9%)
  local copies, waits for them, and re-layouts  54.2 us (8%)
  other arithmetic  37.1 us (6%)
  matrix products  23.9 us (4%)
  between operations  15.5 us (2%)
    all_to_all x1, waiting for transfers between devices, on_device(): returned = lax.all_to_all(expert_result, group, 0, 0, tiled=True)  87.7 us
    all_to_all x1, waiting for transfers between devices, on_device(): lax.all_to_all(outgoing.reshape(n_group, capacity, width), group, 0, 0, t...  69 us
    all_gather x1, blocking collectives, on_device(): both_rows = lax.all_gather(mixed, 'zh', axis=0, tiled=True)  63.5 us
    all_gather x1, waiting for transfers between devices, on_device(): head_rows = lax.all_gather(head_rows, 'core', axis=0, tiled=True)  52.1 us
    all_gather x1, waiting for transfers between devices, on_device(): prompt_rows = lax.all_gather(hidden_in, 'tp', axis=0, tiled=True)  52 us
    ppermute x3, waiting for transfers between devices, on_device(): slots.append(lax.ppermute(sent, everyone, perm=pairs))  31.4 us
    all_to_all x1, waiting for transfers between devices, on_device(): lax.all_to_all(partial.reshape(n_zh, quarter, width), 'zh', 0, 0, tiled=T...  24.1 us
    all_gather x1, waiting for transfers between devices, on_device(): expert_gate_up = lax.all_gather(column_half, 'core', axis=1, tiled=True)  22.7 us
  transfers between devices with their start and end apart: 15, of which 12 were waited for; matrix products, arithmetic and copies ran while one was open for 11% of the time, Pallas kernels for 0%

profile of v3, /device:TPU:2, one launch (start us, length us, event | category | flops | bytes accessed | tf_op | source)
XLA Modules:
  0.0 630.6 jit_solution(5236516604695556332)
XLA Ops:
  20.5 10.0 %all_gather.23 = bf16[64,1280]{1,0:T(8,128)(2,1)} all-gather(bf16[32,1280]{1,0:T(8,128)(2,1)S(1)} %bitcast.156), channel_id=1, replica_groups=mesh['zh'=2,'sub2'=16,'core'=2,'tp'=4] {'zh'}, dimensions={0}, use_global_device_ids=true | all-gather | bytes 245760 | tf_op jit(solution)/shard_map/all_gather | solution.py:187
  37.2 11.0 %collective-permute-done = bf16[192,2048]{1,0:T(8,128)(2,1)S(1)} collective-permute-done((bf16[192,2048]{1,0:T(8,128)(2,1)S(1)}, bf16[192,2048]{1,0:T(8,128)(2,1)S(1)}, u32[]{:S(2)}, u32[]{:S(2)}) %collective-permute-start) | collective-permute-done | bytes 786464 | tf_op jit(solution)/shard_map/ppermute | solution.py:141
  48.2 14.7 %collective-permute-done.2 = bf16[192,2048]{1,0:T(8,128)(2,1)S(1)} collective-permute-done((bf16[192,2048]{1,0:T(8,128)(2,1)S(1)}, bf16[192,2048]{1,0:T(8,128)(2,1)S(1)}, u32[]{:S(2)}, u32[]{:S(2)}) %collective-permute-start.2) | collective-permute-done | bytes 786464 | tf_op jit(solution)/shard_map/ppermute | solution.py:141
  73.5 8.3 %all-gather = s32[2,64,8]{1,2,0:T(8,128)S(1)} all-gather(s32[1,64,8]{1,2,0:T(8,128)S(1)} %bitcast.165), channel_id=1, replica_groups=mesh['zh'=2,'sub2'=16,'core'=2,'tp'=4] {'zh'}, dimensions={0}, use_global_device_ids=true | all-gather | bytes 6144 | tf_op jit(solution)/shard_map/all_gather | solution.py:149
  90.4 6.2 all-to-all-start.3
  97.9 52.0 %all-gather.6.cloned.1.call-done = bf16[256,2048]{1,0:T(8,128)(2,1)} async-done(((bf16[64,2048]{1,0:T(8,128)(2,1)}), bf16[256,2048]{1,0:T(8,128)(2,1)}) %all-gather.6.cloned.1.call-update) | async-done | bytes 1048592 | tf_op jit(solution)/shard_map/all_gather | solution.py:168
  152.2 52.1 %all-gather.10.cloned.1.call-done = bf16[2048,1280]{1,0:T(8,128)(2,1)} async-done(((bf16[1024,1280]{1,0:T(8,128)(2,1)}), bf16[2048,1280]{1,0:T(8,128)(2,1)}) %all-gather.10.cloned.1.call-update) | async-done | bytes 5242896 | tf_op jit(solution)/shard_map/all_gather | solution.py:189
  221.1 7.5 %reshape.735 = bf16[2,16,4,8,2,768]{5,4,3,2,1,0:T(2,128)(2,1)} reshape(bf16[2,64,8,1536]{3,2,1,0:T(8,128)(2,1)} %all-to-all-done.3) | data formatting | bytes 6291456 | tf_op jit(solution)/shard_map/reshape | solution.py:157
  239.4 7.9 %all-to-all-done.1 = bf16[4,64,2048]{2,1,0:T(8,128)(2,1)S(1)} async-done(((bf16[4,64,2048]{2,1,0:T(8,128)(2,1)}), bf16[4,64,2048]{2,1,0:T(8,128)(2,1)S(1)}, u32[]{:S(2)}, u32[]{:S(2)}) %all-to-all-start.1) | async-done | bytes 1048608 | tf_op jit(solution)/shard_map/all_to_all | solution.py:46
  248.3 9.9 %all-to-all-start.4 = ((bf16[128,16,768]{2,1,0:T(8,128)(2,1)}), bf16[128,16,768]{2,1,0:T(8,128)(2,1)}, u32[]{:S(2)}, u32[]{:S(2)}) async-start(bf16[128,16,768]{2,1,0:T(8,128)(2,1)} %bitcast.142), calls=%async_computation.4 | async-start | bytes 6291456 | tf_op jit(solution)/shard_map/all_to_all | solution.py:160
  261.0 63.5 %all_gather.26 = bf16[128,2048]{1,0:T(8,128)(2,1)S(1)} all-gather(bf16[64,2048]{1,0:T(8,128)(2,1)S(1)} %multiply_convert_fusion), channel_id=1, replica_groups=mesh['zh'=2,'sub2'=16,'core'=2,'tp'=4] {'zh'}, dimensions={0}, use_global_device_ids=true | all-gather | bytes 786432 | tf_op jit(solution)/shard_map/all_gather | solution.py:226
  324.6 9.1 %scatter_custom_fusion = bf16[1024,2048]{1,0:T(8,128)(2,1)} fusion(s32[1024]{0:T(1024)S(1)} %bitcast.166, bf16[128,2048]{1,0:T(8,128)(2,1)S(1)} %all_gather.26, bf16[]{:T(256)} %constant.219.clone.1), kind=kCustom, calls=%fused_computation.7 | custom fusion | bytes 4718594 | tf_op jit(solution)/shard_map/scatter | solution.py:251
  333.7 9.4 %all-to-all-done.4 = bf16[128,16,768]{2,1,0:T(8,128)(2,1)} async-done(((bf16[128,16,768]{2,1,0:T(8,128)(2,1)}), bf16[128,16,768]{2,1,0:T(8,128)(2,1)}, u32[]{:S(2)}, u32[]{:S(2)}) %all-to-all-start.4) | async-done | bytes 3145760 | tf_op jit(solution)/shard_map/all_to_all | solution.py:160
  343.0 6.5 %all-to-all-start.2 = ((bf16[64,16,2048]{2,1,0:T(8,128)(2,1)}), bf16[64,16,2048]{2,1,0:T(8,128)(2,1)}, u32[]{:S(2)}, u32[]{:S(2)}) async-start(bf16[64,16,2048]{2,1,0:T(8,128)(2,1)} %bitcast.140), calls=%async_computation.2 | async-start | bytes 8388608 | tf_op jit(solution)/shard_map/all_to_all | solution.py:253
  353.8 22.7 %all-gather.12.cloned.1.call-done = bf16[2048,1536]{1,0:T(8,128)(2,1)} async-done(((bf16[2048,768]{1,0:T(8,128)(2,1)}), bf16[2048,1536]{1,0:T(8,128)(2,1)}) %all-gather.12.cloned.1.call-update) | async-done | bytes 6291472 | tf_op jit(solution)/shard_map/all_gather | solution.py:166
  376.5 69.0 %all-to-all-done.2 = bf16[64,16,2048]{2,1,0:T(8,128)(2,1)} async-done(((bf16[64,16,2048]{2,1,0:T(8,128)(2,1)}), bf16[64,16,2048]{2,1,0:T(8,128)(2,1)}, u32[]{:S(2)}, u32[]{:S(2)}) %all-to-all-start.2) | async-done | bytes 4194336 | tf_op jit(solution)/shard_map/all_to_all | solution.py:253
  445.5 10.0 %fusion.78 = f32[1024,1536]{1,0:T(8,128)S(1)} fusion(bf16[1024,2048]{1,0:T(8,128)(2,1)} %bitcast.33, bf16[2048,1536]{1,0:T(8,128)(2,1)} %all-gather.12.cloned.1.call-done), kind=kOutput, calls=%fused_computation.188 | convolution fusion | flops 6442450944 | bytes 16777216 | tf_op jit(solution)/shard_map/dot_general | solution.py:257
  467.8 8.2 %all-to-all-start.5 = ((bf16[64,16,2048]{2,1,0:T(8,128)(2,1)}), bf16[64,16,2048]{2,1,0:T(8,128)(2,1)}, u32[]{:S(2)}, u32[]{:S(2)}) async-start(bf16[64,16,2048]{2,1,0:T(8,128)(2,1)} %bitcast.139), calls=%async_computation.5 | async-start | bytes 8388608 | tf_op jit(solution)/shard_map/all_to_all | solution.py:268
  476.5 6.8 %gather_fusion.1 = f32[1024]{0:T(1024)S(1)} fusion(f32[128,128]{1,0:T(8,128)S(1)} %fusion.77, s32[1024]{0:T(1024)S(1)} %reshape.751), kind=kCustom, calls=%fused_computation.1 | custom fusion | bytes 16384 | tf_op jit(solution)/shard_map/jit(take_along_axis)/gather | solution.py:229
  483.6 87.7 %all-to-all-done.5 = bf16[64,16,2048]{2,1,0:T(8,128)(2,1)} async-done(((bf16[64,16,2048]{2,1,0:T(8,128)(2,1)}), bf16[64,16,2048]{2,1,0:T(8,128)(2,1)}, u32[]{:S(2)}, u32[]{:S(2)}) %all-to-all-start.5) | async-done | bytes 4194336 | tf_op jit(solution)/shard_map/all_to_all | solution.py:268
  571.3 11.6 %gather_fusion = bf16[1024,2048]{1,0:T(8,128)(2,1)} fusion(bf16[1024,2048]{1,0:T(8,128)(2,1)} %bitcast.45, s32[1024]{0:T(1024)S(1)} %broadcast_clamp_fusion), kind=kCustom, calls=%fused_computation | custom fusion | bytes 8392704 | tf_op jit(solution)/shard_map/gather | solution.py:269
  582.9 7.5 %fusion = f32[128,2048]{1,0:T(8,128)} fusion(bf16[1024,2048]{1,0:T(8,128)(2,1)} %gather_fusion, f32[128,8]{1,0:T(8,128)S(1)} %copy.100), kind=kLoop, calls=%fused_computation.5 | loop fusion | flops 6029312 | bytes 5246976 | tf_op jit(solution)/shard_map/reduce_sum | solution.py:273
  590.4 6.0 all-to-all-start.6
  597.3 24.1 %all-to-all-done.6 = f32[2,64,2048]{2,1,0:T(8,128)} async-done(((f32[2,64,2048]{2,1,0:T(8,128)}), f32[2,64,2048]{2,1,0:T(8,128)}, u32[]{:S(2)}, u32[]{:S(2)}) %all-to-all-start.6) | async-done | bytes 1048608 | tf_op jit(solution)/shard_map/all_to_all | solution.py:278
  (123 shorter events, 93.6 us)
Async XLA Ops:
  7.2 469.1 %copy-start = (bf16[2048,128]{1,0:T(8,128)(2,1)S(1)}, bf16[2048,128]{1,0:T(8,128)(2,1)}, u32[]{:S(2)}) copy-start(bf16[2048,128]{1,0:T(8,128)(2,1)} %param.20) | copy-start | bytes 1572868
  8.8 11.7 %all-to-all-start = ((bf16[8,4,1280]{2,0,1:T(8,128)(2,1)}), bf16[8,4,1280]{2,0,1:T(8,128)(2,1)S(1)}, u32[]{:S(2)}, u32[]{:S(2)}) async-start(bf16[8,4,1280]{2,0,1:T(8,128)(2,1)} %pad_maximum_fusion.1), calls=%async_computation | async-start | bytes 163840 | tf_op jit(solution)/shard_map/all_to_all | solution.py:186
  14.7 70.1 %all-gather.8.cloned.1.call-start = ((), (), s32[]{:S(2)}) async-start(), calls=%async_computation.8 | async-start | bytes 2785280 | tf_op jit(solution)/shard_map/all_gather | solution.py:188
  30.5 119.4 %all-gather.6.cloned.1.call-start = ((), (), s32[]{:S(2)}) async-start(), calls=%async_computation.7 | async-start | bytes 1310720 | tf_op jit(solution)/shard_map/all_gather | solution.py:168
  32.7 15.5 %collective-permute-start = (bf16[192,2048]{1,0:T(8,128)(2,1)S(1)}, bf16[192,2048]{1,0:T(8,128)(2,1)S(1)}, u32[]{:S(2)}, u32[]{:S(2)}) collective-permute-start(bf16[192,2048]{1,0:T(8,128)(2,1)S(1)} %get-tuple-element.27), channel_id=1, source_target_pairs={{1,0},{3,2},{4,7},{6,5},{9,8},{11,10},{12,15},{14,13},{17,16},{19,... | collective-permute-start | bytes 2359304 | tf_op jit(solution)/shard_map/ppermute | solution.py:141
  34.0 28.9 %collective-permute-start.2 = (bf16[192,2048]{1,0:T(8,128)(2,1)S(1)}, bf16[192,2048]{1,0:T(8,128)(2,1)S(1)}, u32[]{:S(2)}, u32[]{:S(2)}) collective-permute-start(bf16[192,2048]{1,0:T(8,128)(2,1)S(1)} %get-tuple-element.28), channel_id=1, source_target_pairs={{1,2},{3,0},{4,5},{6,7},{9,10},{11,8},{12,13},{14,15},{17,18},{19,... | collective-permute-start | bytes 2359304 | tf_op jit(solution)/shard_map/ppermute | solution.py:141
  35.3 33.3 %collective-permute-start.1 = (bf16[192,2048]{1,0:T(8,128)(2,1)S(1)}, bf16[192,2048]{1,0:T(8,128)(2,1)S(1)}, u32[]{:S(2)}, u32[]{:S(2)}) collective-permute-start(bf16[192,2048]{1,0:T(8,128)(2,1)S(1)} %get-tuple-element.29), channel_id=1, source_target_pairs={{0,2},{2,0},{5,7},{7,5},{8,10},{10,8},{13,15},{15,13},{16,18},{18,... | collective-permute-start | bytes 2359304 | tf_op jit(solution)/shard_map/ppermute | solution.py:141
  68.6 1.9 copy-start.4
  68.6 4.9 copy-start.8
  70.5 11.3 %collective-permute-start.3 = (bf16[4,192,2048]{2,1,0:T(8,128)(2,1)}, bf16[4,192,2048]{2,1,0:T(8,128)(2,1)}, u32[]{:S(2)}, u32[]{:S(2)}) collective-permute-start(bf16[4,192,2048]{2,1,0:T(8,128)(2,1)} %pad_maximum_fusion), channel_id=1, source_target_pairs={{0,4},{5,1},{2,6},{7,3},{8,12},{13,9},{10,14},{15,11},{16,20},{21,... | collective-permute-start | bytes 9437192 | tf_op jit(solution)/shard_map/ppermute | solution.py:148
  84.7 119.5 %all-gather.10.cloned.1.call-start = ((), (), s32[]{:S(2)}) async-start(), calls=%async_computation.9 | async-start | bytes 7864320 | tf_op jit(solution)/shard_map/all_gather | solution.py:189
  90.4 125.8 %all-to-all-start.3 = ((bf16[2,64,8,1536]{3,2,1,0:T(8,128)(2,1)}), bf16[2,64,8,1536]{3,2,1,0:T(8,128)(2,1)}, u32[]{:S(2)}, u32[]{:S(2)}) async-start(bf16[2,64,8,1536]{3,2,1,0:T(8,128)(2,1)} %bitcast.143), calls=%async_computation.3 | async-start | bytes 6291456 | tf_op jit(solution)/shard_map/all_to_all | solution.py:156
  96.5 55.2 %copy-start.6 = (f32[2048]{0:T(1024)S(1)}, f32[2048]{0:T(1024)}, u32[]{:S(2)}) copy-start(f32[2048]{0:T(1024)} %param.14) | copy-start | bytes 24580
  211.7 2.2 copy-start.11
  216.1 31.2 %all-to-all-start.1 = ((bf16[4,64,2048]{2,1,0:T(8,128)(2,1)}), bf16[4,64,2048]{2,1,0:T(8,128)(2,1)S(1)}, u32[]{:S(2)}, u32[]{:S(2)}) async-start(bf16[4,64,2048]{2,1,0:T(8,128)(2,1)} %bitcast.154), calls=%async_computation.1 | async-start | bytes 2097152 | tf_op jit(solution)/shard_map/all_to_all | solution.py:46
  248.3 94.8 %all-to-all-start.4 = ((bf16[128,16,768]{2,1,0:T(8,128)(2,1)}), bf16[128,16,768]{2,1,0:T(8,128)(2,1)}, u32[]{:S(2)}, u32[]{:S(2)}) async-start(bf16[128,16,768]{2,1,0:T(8,128)(2,1)} %bitcast.142), calls=%async_computation.4 | async-start | bytes 6291456 | tf_op jit(solution)/shard_map/all_to_all | solution.py:160
  258.2 2.5 copy-start.3
  258.2 2.7 copy-start.7
  343.0 102.5 %all-to-all-start.2 = ((bf16[64,16,2048]{2,1,0:T(8,128)(2,1)}), bf16[64,16,2048]{2,1,0:T(8,128)(2,1)}, u32[]{:S(2)}, u32[]{:S(2)}) async-start(bf16[64,16,2048]{2,1,0:T(8,128)(2,1)} %bitcast.140), calls=%async_computation.2 | async-start | bytes 8388608 | tf_op jit(solution)/shard_map/all_to_all | solution.py:253
  349.5 27.0 %all-gather.12.cloned.1.call-start = ((), (), s32[]{:S(2)}) async-start(), calls=%async_computation.10 | async-start | bytes 9437184 | tf_op jit(solution)/shard_map/all_gather | solution.py:166
  467.8 103.5 %all-to-all-start.5 = ((bf16[64,16,2048]{2,1,0:T(8,128)(2,1)}), bf16[64,16,2048]{2,1,0:T(8,128)(2,1)}, u32[]{:S(2)}, u32[]{:S(2)}) async-start(bf16[64,16,2048]{2,1,0:T(8,128)(2,1)} %bitcast.139), calls=%async_computation.5 | async-start | bytes 8388608 | tf_op jit(solution)/shard_map/all_to_all | solution.py:268
  582.9 13.5 %copy-start.12 = (s32[1,2]{1,0:T(1,128)S(1)}, s32[1,2]{1,0:T(1,128)}, u32[]{:S(2)}) copy-start(s32[1,2]{1,0:T(1,128)} %param.25) | copy-start | bytes 28
  590.4 31.1 %all-to-all-start.6 = ((f32[2,64,2048]{2,1,0:T(8,128)}), f32[2,64,2048]{2,1,0:T(8,128)}, u32[]{:S(2)}, u32[]{:S(2)}) async-start(f32[2,64,2048]{2,1,0:T(8,128)} %bitcast.147), calls=%async_computation.6 | async-start | bytes 2097152 | tf_op jit(solution)/shard_map/all_to_all | solution.py:278
  597.3 26.3 %copy-start.5 = (bf16[4,2,128,128]{3,2,1,0:T(8,128)(2,1)}, bf16[4,2,128,128]{3,2,1,0:T(8,128)(2,1)S(1)}, u32[]{:S(2)}) copy-start(bf16[4,2,128,128]{3,2,1,0:T(8,128)(2,1)S(1)} %scatter_fusion) | copy-start | bytes 786436
  (4 other events, 5.7 us)
Sparse Core Ops, SparseCore 0:
  30.7 50.4 all-gather.7
  84.8 65.0 all-gather.5
  151.7 52.4 all-gather.9
  353.9 22.5 all-gather.11

commit v4 on v3

--- a/solution.py
+++ b/solution.py
@@ -168,6 +168,7 @@
     prompt_rows = lax.all_gather(hidden_in, "tp", axis=0, tiled=True)
     column_span = prompt_rows.shape[0]
     normed = rms_scale(prompt_rows.astype(jnp.float32), attention_gain).astype(jnp.bfloat16)
+    expert_gate_up, normed = lax.optimization_barrier((expert_gate_up, normed))
     trainer_rows = attention_trainer_copy.shape[0]
     query_cols = attention_trainer_copy[:, : QUERY_HEADS * HEAD_SIZE].reshape(
         trainer_rows, n_tp, heads_here * HEAD_SIZE
@@ -223,7 +224,7 @@
     after_attn = hidden_in.astype(jnp.float32) + attention_sums
     mixed = rms_scale(after_attn, post_gain).astype(jnp.bfloat16)
 
-    both_rows = lax.all_gather(mixed, "zh", axis=0, tiled=True)
+    both_rows = collect(mixed, "zh", 0)
     row_count = both_rows.shape[0]
     logits = jnp.dot(both_rows, router_weight, preferred_element_type=jnp.float32)
     chosen = jnp.take_along_axis(logits, both_routes, axis=1)

time: 642 us -> 663 us (1.033)
  blocking collectives: 81.8 us -> 133 us
  waiting for transfers between devices: 363 us -> 315 us
  starting transfers between devices: 55.4 us -> 72.8 us
    all_gather x1, blocking collectives: 9.99 us -> 87.5 us  [on_device(): head_rows = lax.all_gather(head_rows, 'zh', axis=0, tiled=True)]
    all_gather x1 -> x0, blocking collectives: 63.5 us -> none  [on_device(): both_rows = lax.all_gather(mixed, 'zh', axis=0, tiled=True)]
    all_gather x1, waiting for transfers between devices: 52 us -> 10 us  [on_device(): prompt_rows = lax.all_gather(hidden_in, 'tp', axis=0, tiled=True)]
    all_gather x1, blocking collectives: 8.25 us -> 45.9 us  [on_device(): both_routes = lax.all_gather(routes, 'zh', axis=0, tiled=True)]
    ppermute x3, waiting for transfers between devices: 31.4 us -> 0.01 us  [on_device(): slots.append(lax.ppermute(sent, everyone, perm=pairs))]
    all_gather x1, waiting for transfers between devices: 52.1 us -> 23.4 us  [on_device(): head_rows = lax.all_gather(head_rows, 'core', axis=0, tiled=True)]
    all_to_all x1, waiting for transfers between devices: 69 us -> 93.5 us  [on_device(): lax.all_to_all(outgoing.reshape(n_group, capacity, width), group, 0, 0, t...]
    all_to_all x1, waiting for transfers between devices: 7.92 us -> 26 us  [summed_on_arrival(): lax.all_to_all(in_blocks(array, dim, peers), axis, 0, 0, tiled=True)]
  transfers between devices with their start and end apart: 15 -> 16, of which waited for: 12 -> 10; matrix products, arithmetic and copies ran while one was open for 11% -> 7% of each run, Pallas kernels for 0% -> 0%
where the time goes in v4:
time: 663 us; the launch traced here: 653 us
  waiting for transfers between devices  315 us (48%)
  blocking collectives  133 us (20%)
  starting transfers between devices  72.8 us (11%)
  local copies, waits for them, and re-layouts  53.8 us (8%)
  other arithmetic  38.1 us (6%)
  matrix products  23.9 us (4%)
  between operations  15.3 us (2%)
    all_to_all x1, waiting for transfers between devices, on_device(): lax.all_to_all(outgoing.reshape(n_group, capacity, width), group, 0, 0, t...  93.5 us
    all_gather x1, blocking collectives, on_device(): head_rows = lax.all_gather(head_rows, 'zh', axis=0, tiled=True)  87.5 us
    all_to_all x1, waiting for transfers between devices, on_device(): returned = lax.all_to_all(expert_result, group, 0, 0, tiled=True)  85.8 us
    all_gather x1, blocking collectives, on_device(): both_routes = lax.all_gather(routes, 'zh', axis=0, tiled=True)  45.9 us
    all_to_all x1, waiting for transfers between devices, summed_on_arrival(): lax.all_to_all(in_blocks(array, dim, peers), axis, 0, 0, tiled=True)  26 us
    all_gather x1, waiting for transfers between devices, on_device(): head_rows = lax.all_gather(head_rows, 'core', axis=0, tiled=True)  23.4 us
    all_to_all x1, waiting for transfers between devices, on_device(): lax.all_to_all(partial.reshape(n_zh, quarter, width), 'zh', 0, 0, tiled=T...  23.2 us
    all_gather x1, waiting for transfers between devices, on_device(): expert_gate_up = lax.all_gather(column_half, 'core', axis=1, tiled=True)  20.7 us
  transfers between devices with their start and end apart: 16, of which 10 were waited for; matrix products, arithmetic and copies ran while one was open for 7% of the time, Pallas kernels for 0%

profile of v4, /device:TPU:2, one launch (start us, length us, event | category | flops | bytes accessed | tf_op | source)
XLA Modules:
  0.0 652.8 jit_solution(3116576256500550206)
XLA Ops:
  8.8 5.9 all-to-all-start.2
  20.5 6.0 all-to-all-start
  34.5 87.5 %all_gather.21 = bf16[64,1280]{1,0:T(8,128)(2,1)} all-gather(bf16[32,1280]{1,0:T(8,128)(2,1)S(1)} %bitcast.157), channel_id=1, replica_groups=mesh['zh'=2,'sub2'=16,'core'=2,'tp'=4] {'zh'}, dimensions={0}, use_global_device_ids=true | all-gather | bytes 245760 | tf_op jit(solution)/shard_map/all_gather | solution.py:188
  122.0 7.5 %reshape.724 = bf16[2,16,4,8,2,768]{5,4,3,2,1,0:T(2,128)(2,1)} reshape(bf16[2,64,8,1536]{3,2,1,0:T(8,128)(2,1)} %all-to-all-done) | data formatting | bytes 6291456 | tf_op jit(solution)/shard_map/reshape | solution.py:157
  140.3 17.2 %all-to-all-start.1 = ((bf16[128,16,768]{2,1,0:T(8,128)(2,1)}), bf16[128,16,768]{2,1,0:T(8,128)(2,1)}, u32[]{:S(2)}, u32[]{:S(2)}) async-start(bf16[128,16,768]{2,1,0:T(8,128)(2,1)} %bitcast.142), calls=%async_computation.1 | async-start | bytes 6291456 | tf_op jit(solution)/shard_map/all_to_all | solution.py:160
  164.2 45.9 %all-gather = s32[2,64,8]{1,2,0:T(8,128)S(1)} all-gather(s32[1,64,8]{1,2,0:T(8,128)S(1)} %bitcast.166), channel_id=1, replica_groups=mesh['zh'=2,'sub2'=16,'core'=2,'tp'=4] {'zh'}, dimensions={0}, use_global_device_ids=true | all-gather | bytes 6144 | tf_op jit(solution)/shard_map/all_gather | solution.py:149
  213.2 18.2 %all-to-all-done.1 = bf16[128,16,768]{2,1,0:T(8,128)(2,1)} async-done(((bf16[128,16,768]{2,1,0:T(8,128)(2,1)}), bf16[128,16,768]{2,1,0:T(8,128)(2,1)}, u32[]{:S(2)}, u32[]{:S(2)}) %all-to-all-start.1) | async-done | bytes 3145760 | tf_op jit(solution)/shard_map/all_to_all | solution.py:160
  237.4 10.0 %all-gather.8.cloned.1.call-done = bf16[256,2048]{1,0:T(8,128)(2,1)} async-done(((bf16[64,2048]{1,0:T(8,128)(2,1)}), bf16[256,2048]{1,0:T(8,128)(2,1)}) %all-gather.8.cloned.1.call-update) | async-done | bytes 1048592 | tf_op jit(solution)/shard_map/all_gather | solution.py:168
  249.6 20.7 %all-gather.6.cloned.1.call-done = bf16[2048,1536]{1,0:T(8,128)(2,1)} async-done(((bf16[2048,768]{1,0:T(8,128)(2,1)}), bf16[2048,1536]{1,0:T(8,128)(2,1)}) %all-gather.6.cloned.1.call-update) | async-done | bytes 6291472 | tf_op jit(solution)/shard_map/all_gather | solution.py:166
  270.4 23.4 %all-gather.12.cloned.1.call-done = bf16[2048,1280]{1,0:T(8,128)(2,1)} async-done(((bf16[1024,1280]{1,0:T(8,128)(2,1)}), bf16[2048,1280]{1,0:T(8,128)(2,1)}) %all-gather.12.cloned.1.call-update) | async-done | bytes 5242896 | tf_op jit(solution)/shard_map/all_gather | solution.py:190
  311.2 26.0 %all-to-all-done.3 = bf16[4,64,2048]{2,1,0:T(8,128)(2,1)} async-done(((bf16[4,64,2048]{2,1,0:T(8,128)(2,1)}), bf16[4,64,2048]{2,1,0:T(8,128)(2,1)}, u32[]{:S(2)}, u32[]{:S(2)}) %all-to-all-start.3) | async-done | bytes 1048608 | tf_op jit(solution)/shard_map/all_to_all | solution.py:46
  339.8 6.8 %all-to-all-start.4 = ((bf16[2,64,2048]{2,1,0:T(8,128)(2,1)}), bf16[2,64,2048]{2,1,0:T(8,128)(2,1)S(1)}, u32[]{:S(2)}, u32[]{:S(2)}) async-start(bf16[2,64,2048]{2,1,0:T(8,128)(2,1)} %broadcast_in_dim.59), calls=%async_computation.4 | async-start | bytes 1048576 | tf_op jit(solution)/shard_map/all_to_all | solution.py:29
  347.5 13.5 %all-to-all-done.4 = bf16[2,64,2048]{2,1,0:T(8,128)(2,1)S(1)} async-done(((bf16[2,64,2048]{2,1,0:T(8,128)(2,1)}), bf16[2,64,2048]{2,1,0:T(8,128)(2,1)S(1)}, u32[]{:S(2)}, u32[]{:S(2)}) %all-to-all-start.4) | async-done | bytes 524320 | tf_op jit(solution)/shard_map/all_to_all | solution.py:29
  361.0 9.1 %scatter_custom_fusion = bf16[1024,2048]{1,0:T(8,128)(2,1)} fusion(s32[1024]{0:T(1024)S(1)} %bitcast.167, bf16[128,2048]{1,0:T(8,128)(2,1)S(1)} %bitcast.146, bf16[]{:T(256)} %constant.219.clone.1), kind=kCustom, calls=%fused_computation.7 | custom fusion | bytes 4718594 | tf_op jit(solution)/shard_map/scatter | solution.py:252
  370.2 9.3 %all-to-all-start.5 = ((bf16[64,16,2048]{2,1,0:T(8,128)(2,1)}), bf16[64,16,2048]{2,1,0:T(8,128)(2,1)}, u32[]{:S(2)}, u32[]{:S(2)}) async-start(bf16[64,16,2048]{2,1,0:T(8,128)(2,1)} %bitcast.141), calls=%async_computation.5 | async-start | bytes 8388608 | tf_op jit(solution)/shard_map/all_to_all | solution.py:254
  379.5 93.5 %all-to-all-done.5 = bf16[64,16,2048]{2,1,0:T(8,128)(2,1)} async-done(((bf16[64,16,2048]{2,1,0:T(8,128)(2,1)}), bf16[64,16,2048]{2,1,0:T(8,128)(2,1)}, u32[]{:S(2)}, u32[]{:S(2)}) %all-to-all-start.5) | async-done | bytes 4194336 | tf_op jit(solution)/shard_map/all_to_all | solution.py:254
  473.0 10.0 %fusion.78 = f32[1024,1536]{1,0:T(8,128)S(1)} fusion(bf16[1024,2048]{1,0:T(8,128)(2,1)} %bitcast.40, bf16[2048,1536]{1,0:T(8,128)(2,1)} %all-gather.6.cloned.1.call-done), kind=kOutput, calls=%fused_computation.188 | convolution fusion | flops 6442450944 | bytes 16777216 | tf_op jit(solution)/shard_map/dot_general | solution.py:258
  490.2 5.1 add_convert_fusion
  495.3 7.4 %all-to-all-start.6 = ((bf16[64,16,2048]{2,1,0:T(8,128)(2,1)}), bf16[64,16,2048]{2,1,0:T(8,128)(2,1)}, u32[]{:S(2)}, u32[]{:S(2)}) async-start(bf16[64,16,2048]{2,1,0:T(8,128)(2,1)} %bitcast.140), calls=%async_computation.6 | async-start | bytes 8388608 | tf_op jit(solution)/shard_map/all_to_all | solution.py:269
  503.2 6.8 %gather_fusion.1 = f32[1024]{0:T(1024)S(1)} fusion(f32[128,128]{1,0:T(8,128)S(1)} %fusion.77, s32[1024]{0:T(1024)S(1)} %reshape.756), kind=kCustom, calls=%fused_computation.1 | custom fusion | bytes 16384 | tf_op jit(solution)/shard_map/jit(take_along_axis)/gather | solution.py:230
  510.3 85.8 %all-to-all-done.6 = bf16[64,16,2048]{2,1,0:T(8,128)(2,1)} async-done(((bf16[64,16,2048]{2,1,0:T(8,128)(2,1)}), bf16[64,16,2048]{2,1,0:T(8,128)(2,1)}, u32[]{:S(2)}, u32[]{:S(2)}) %all-to-all-start.6) | async-done | bytes 4194336 | tf_op jit(solution)/shard_map/all_to_all | solution.py:269
  596.1 11.6 %gather_fusion = bf16[1024,2048]{1,0:T(8,128)(2,1)} fusion(bf16[1024,2048]{1,0:T(8,128)(2,1)} %bitcast.46, s32[1024]{0:T(1024)S(1)} %broadcast_clamp_fusion), kind=kCustom, calls=%fused_computation | custom fusion | bytes 8392704 | tf_op jit(solution)/shard_map/gather | solution.py:270
  607.7 7.5 %fusion = f32[128,2048]{1,0:T(8,128)} fusion(bf16[1024,2048]{1,0:T(8,128)(2,1)} %gather_fusion, f32[128,8]{1,0:T(8,128)S(1)} %copy.102), kind=kLoop, calls=%fused_computation.5 | loop fusion | flops 6029312 | bytes 5246976 | tf_op jit(solution)/shard_map/reduce_sum | solution.py:274
  620.6 23.2 %all-to-all-done.7 = f32[2,64,2048]{2,1,0:T(8,128)} async-done(((f32[2,64,2048]{2,1,0:T(8,128)}), f32[2,64,2048]{2,1,0:T(8,128)}, u32[]{:S(2)}, u32[]{:S(2)}) %all-to-all-start.7) | async-done | bytes 1048608 | tf_op jit(solution)/shard_map/all_to_all | solution.py:279
  (123 shorter events, 79.5 us)
Async XLA Ops:
  7.2 495.7 %copy-start = (bf16[2048,128]{1,0:T(8,128)(2,1)S(1)}, bf16[2048,128]{1,0:T(8,128)(2,1)}, u32[]{:S(2)}) copy-start(bf16[2048,128]{1,0:T(8,128)(2,1)} %param.20) | copy-start | bytes 1572868
  8.8 11.7 %all-to-all-start.2 = ((bf16[8,4,1280]{2,0,1:T(8,128)(2,1)}), bf16[8,4,1280]{2,0,1:T(8,128)(2,1)S(1)}, u32[]{:S(2)}, u32[]{:S(2)}) async-start(bf16[8,4,1280]{2,0,1:T(8,128)(2,1)} %pad_maximum_fusion.1), calls=%async_computation.2 | async-start | bytes 163840 | tf_op jit(solution)/shard_map/all_to_all | solution.py:187
  20.5 6.0 copy-start.2
  20.5 101.5 %all-to-all-start = ((bf16[2,64,8,1536]{3,2,1,0:T(8,128)(2,1)}), bf16[2,64,8,1536]{3,2,1,0:T(8,128)(2,1)}, u32[]{:S(2)}, u32[]{:S(2)}) async-start(bf16[2,64,8,1536]{3,2,1,0:T(8,128)(2,1)} %bitcast.144), calls=%async_computation | async-start | bytes 6291456 | tf_op jit(solution)/shard_map/all_to_all | solution.py:156
  26.5 209.6 %all-gather.10.cloned.1.call-start = ((), (), s32[]{:S(2)}) async-start(), calls=%async_computation.10 | async-start | bytes 2785280 | tf_op jit(solution)/shard_map/all_gather | solution.py:189
  27.9 129.6 %collective-permute-start = (bf16[192,2048]{1,0:T(8,128)(2,1)}, bf16[192,2048]{1,0:T(8,128)(2,1)S(1)}, u32[]{:S(2)}, u32[]{:S(2)}) collective-permute-start(bf16[192,2048]{1,0:T(8,128)(2,1)} %get-tuple-element.31), channel_id=1, source_target_pairs={{1,0},{3,2},{4,7},{6,5},{9,8},{11,10},{12,15},{14,13},{17,16},{19,... | collective-permute-start | bytes 2359304 | tf_op jit(solution)/shard_map/ppermute | solution.py:141
  29.2 128.4 %collective-permute-start.2 = (bf16[192,2048]{1,0:T(8,128)(2,1)}, bf16[192,2048]{1,0:T(8,128)(2,1)S(1)}, u32[]{:S(2)}, u32[]{:S(2)}) collective-permute-start(bf16[192,2048]{1,0:T(8,128)(2,1)} %get-tuple-element.32), channel_id=1, source_target_pairs={{1,2},{3,0},{4,5},{6,7},{9,10},{11,8},{12,13},{14,15},{17,18},{19,... | collective-permute-start | bytes 2359304 | tf_op jit(solution)/shard_map/ppermute | solution.py:141
  30.5 127.1 %collective-permute-start.1 = (bf16[192,2048]{1,0:T(8,128)(2,1)}, bf16[192,2048]{1,0:T(8,128)(2,1)}, u32[]{:S(2)}, u32[]{:S(2)}) collective-permute-start(bf16[192,2048]{1,0:T(8,128)(2,1)} %get-tuple-element.33), channel_id=1, source_target_pairs={{0,2},{2,0},{5,7},{7,5},{8,10},{10,8},{13,15},{15,13},{16,18},{18,... | collective-permute-start | bytes 2359304 | tf_op jit(solution)/shard_map/ppermute | solution.py:141
  140.3 91.1 %all-to-all-start.1 = ((bf16[128,16,768]{2,1,0:T(8,128)(2,1)}), bf16[128,16,768]{2,1,0:T(8,128)(2,1)}, u32[]{:S(2)}, u32[]{:S(2)}) async-start(bf16[128,16,768]{2,1,0:T(8,128)(2,1)} %bitcast.142), calls=%async_computation.1 | async-start | bytes 6291456 | tf_op jit(solution)/shard_map/all_to_all | solution.py:160
  157.5 89.9 %all-gather.8.cloned.1.call-start = ((), (), s32[]{:S(2)}) async-start(), calls=%async_computation.9 | async-start | bytes 1310720 | tf_op jit(solution)/shard_map/all_gather | solution.py:168
  157.6 6.6 %copy-start.7 = (s32[64,8]{0,1:T(8,128)S(1)}, s32[64,8]{0,1:T(8,128)}, u32[]{:S(2)}) copy-start(s32[64,8]{0,1:T(8,128)} %param.23) | copy-start | bytes 6148
  160.5 49.7 %collective-permute-start.3 = (bf16[4,192,2048]{2,1,0:T(8,128)(2,1)}, bf16[4,192,2048]{2,1,0:T(8,128)(2,1)}, u32[]{:S(2)}, u32[]{:S(2)}) collective-permute-start(bf16[4,192,2048]{2,1,0:T(8,128)(2,1)} %pad_maximum_fusion), channel_id=1, source_target_pairs={{0,4},{5,1},{2,6},{7,3},{8,12},{13,9},{10,14},{15,11},{16,20},{21,... | collective-permute-start | bytes 9437192 | tf_op jit(solution)/shard_map/ppermute | solution.py:148
  213.1 57.1 %all-gather.6.cloned.1.call-start = ((), (), s32[]{:S(2)}) async-start(), calls=%async_computation.8 | async-start | bytes 9437184 | tf_op jit(solution)/shard_map/all_gather | solution.py:166
  235.5 13.8 %copy-start.5 = (f32[2048]{0:T(1024)S(1)}, f32[2048]{0:T(1024)}, u32[]{:S(2)}) copy-start(f32[2048]{0:T(1024)} %param.14) | copy-start | bytes 24580
  235.5 58.3 %all-gather.12.cloned.1.call-start = ((), (), s32[]{:S(2)}) async-start(), calls=%async_computation.11 | async-start | bytes 7864320 | tf_op jit(solution)/shard_map/all_gather | solution.py:190
  306.0 32.7 %copy-start.3 = (bf16[64,2048]{1,0:T(8,128)(2,1)S(1)}, bf16[64,2048]{1,0:T(8,128)(2,1)}, u32[]{:S(2)}) copy-start(bf16[64,2048]{1,0:T(8,128)(2,1)} %param.13) | copy-start | bytes 786436
  306.0 32.9 %copy-start.6 = (f32[2048]{0:T(1024)S(1)}, f32[2048]{0:T(1024)}, u32[]{:S(2)}) copy-start(f32[2048]{0:T(1024)} %param.19) | copy-start | bytes 24580
  306.0 31.2 %all-to-all-start.3 = ((bf16[4,64,2048]{2,1,0:T(8,128)(2,1)}), bf16[4,64,2048]{2,1,0:T(8,128)(2,1)}, u32[]{:S(2)}, u32[]{:S(2)}) async-start(bf16[4,64,2048]{2,1,0:T(8,128)(2,1)} %bitcast.155), calls=%async_computation.3 | async-start | bytes 2097152 | tf_op jit(solution)/shard_map/all_to_all | solution.py:46
  339.8 21.2 %all-to-all-start.4 = ((bf16[2,64,2048]{2,1,0:T(8,128)(2,1)}), bf16[2,64,2048]{2,1,0:T(8,128)(2,1)S(1)}, u32[]{:S(2)}, u32[]{:S(2)}) async-start(bf16[2,64,2048]{2,1,0:T(8,128)(2,1)} %broadcast_in_dim.59), calls=%async_computation.4 | async-start | bytes 1048576 | tf_op jit(solution)/shard_map/all_to_all | solution.py:29
  370.2 102.8 %all-to-all-start.5 = ((bf16[64,16,2048]{2,1,0:T(8,128)(2,1)}), bf16[64,16,2048]{2,1,0:T(8,128)(2,1)}, u32[]{:S(2)}, u32[]{:S(2)}) async-start(bf16[64,16,2048]{2,1,0:T(8,128)(2,1)} %bitcast.141), calls=%async_computation.5 | async-start | bytes 8388608 | tf_op jit(solution)/shard_map/all_to_all | solution.py:254
  495.3 100.9 %all-to-all-start.6 = ((bf16[64,16,2048]{2,1,0:T(8,128)(2,1)}), bf16[64,16,2048]{2,1,0:T(8,128)(2,1)}, u32[]{:S(2)}, u32[]{:S(2)}) async-start(bf16[64,16,2048]{2,1,0:T(8,128)(2,1)} %bitcast.140), calls=%async_computation.6 | async-start | bytes 8388608 | tf_op jit(solution)/shard_map/all_to_all | solution.py:269
  607.7 11.9 %copy-start.11 = (s32[1,2]{1,0:T(1,128)S(1)}, s32[1,2]{1,0:T(1,128)}, u32[]{:S(2)}) copy-start(s32[1,2]{1,0:T(1,128)} %param.25) | copy-start | bytes 28
  615.2 28.6 %all-to-all-start.7 = ((f32[2,64,2048]{2,1,0:T(8,128)}), f32[2,64,2048]{2,1,0:T(8,128)}, u32[]{:S(2)}, u32[]{:S(2)}) async-start(f32[2,64,2048]{2,1,0:T(8,128)} %bitcast.150), calls=%async_computation.7 | async-start | bytes 2097152 | tf_op jit(solution)/shard_map/all_to_all | solution.py:279
  620.6 25.4 %copy-start.4 = (bf16[4,2,128,128]{3,2,1,0:T(8,128)(2,1)}, bf16[4,2,128,128]{3,2,1,0:T(8,128)(2,1)S(1)}, u32[]{:S(2)}) copy-start(bf16[4,2,128,128]{3,2,1,0:T(8,128)(2,1)S(1)} %scatter_fusion) | copy-start | bytes 786436
  (4 other events, 6.6 us)
Sparse Core Ops, SparseCore 0:
  122.1 74.8 all-gather.9
  213.3 34.1 all-gather.7
  249.3 20.9 all-gather.5
  271.9 21.8 all-gather.11

commit v5 on v4

--- a/solution.py
+++ b/solution.py
@@ -165,10 +165,9 @@
     )
     expert_gate_up = lax.all_gather(column_half, "core", axis=1, tiled=True)
 
-    prompt_rows = lax.all_gather(hidden_in, "tp", axis=0, tiled=True)
+    prompt_rows = collect(hidden_in, "tp", 0)
     column_span = prompt_rows.shape[0]
     normed = rms_scale(prompt_rows.astype(jnp.float32), attention_gain).astype(jnp.bfloat16)
-    expert_gate_up, normed = lax.optimization_barrier((expert_gate_up, normed))
     trainer_rows = attention_trainer_copy.shape[0]
     query_cols = attention_trainer_copy[:, : QUERY_HEADS * HEAD_SIZE].reshape(
         trainer_rows, n_tp, heads_here * HEAD_SIZE

time: 663 us -> 628 us (0.947)
  blocking collectives: 133 us -> 29.7 us
  waiting for transfers between devices: 315 us -> 388 us
  starting transfers between devices: 72.8 us -> 55.6 us
  local copies, waits for them, and re-layouts: 53.8 us -> 62 us
    all_gather x1, blocking collectives: 87.5 us -> 9.99 us  [on_device(): head_rows = lax.all_gather(head_rows, 'zh', axis=0, tiled=True)]
    all_to_all x1, waiting for transfers between devices: 0.01 us -> 49 us  [on_device(): gate_up_half = lax.all_to_all(gate_up_half, 'zh', 0, 0, tiled=True)]
    all_to_all x1, waiting for transfers between devices: 18.2 us -> 63.6 us  [on_device(): pieces = lax.all_to_all(pieces, ('sub2', 'core', 'tp'), 0, 0, tiled=True)]
    all_gather x1, blocking collectives: 45.9 us -> 8.27 us  [on_device(): both_routes = lax.all_gather(routes, 'zh', axis=0, tiled=True)]
    ppermute x3, waiting for transfers between devices: 0.01 us -> 31.4 us  [on_device(): slots.append(lax.ppermute(sent, everyone, perm=pairs))]
    all_gather x1, waiting for transfers between devices: 23.4 us -> 0.02 us  [on_device(): head_rows = lax.all_gather(head_rows, 'core', axis=0, tiled=True)]
    all_to_all x1, waiting for transfers between devices: 93.5 us -> 70.5 us  [on_device(): lax.all_to_all(outgoing.reshape(n_group, capacity, width), group, 0, 0, t...]
    all_to_all x1, waiting for transfers between devices: 26 us -> 11.8 us  [summed_on_arrival(): lax.all_to_all(in_blocks(array, dim, peers), axis, 0, 0, tiled=True)]
  transfers between devices with their start and end apart: 16 -> 15, of which waited for: 10 -> 13; matrix products, arithmetic and copies ran while one was open for 7% -> 13% of each run, Pallas kernels for 0% -> 0%
where the time goes in v5:
time: 628 us; the launch traced here: 615 us
  waiting for transfers between devices  388 us (62%)
  local copies, waits for them, and re-layouts  62 us (10%)
  starting transfers between devices  55.6 us (9%)
  other arithmetic  40.8 us (6%)
  blocking collectives  29.7 us (5%)
  matrix products  23.9 us (4%)
  between operations  15.5 us (2%)
    all_to_all x1, waiting for transfers between devices, on_device(): returned = lax.all_to_all(expert_result, group, 0, 0, tiled=True)  87.7 us
    all_to_all x1, waiting for transfers between devices, on_device(): lax.all_to_all(outgoing.reshape(n_group, capacity, width), group, 0, 0, t...  70.5 us
    all_to_all x1, waiting for transfers between devices, on_device(): pieces = lax.all_to_all(pieces, ('sub2', 'core', 'tp'), 0, 0, tiled=True)  63.6 us
    all_to_all x1, waiting for transfers between devices, on_device(): gate_up_half = lax.all_to_all(gate_up_half, 'zh', 0, 0, tiled=True)  49 us
    ppermute x3, waiting for transfers between devices, on_device(): slots.append(lax.ppermute(sent, everyone, perm=pairs))  31.4 us
    all_to_all x1, waiting for transfers between devices, on_device(): lax.all_to_all(partial.reshape(n_zh, quarter, width), 'zh', 0, 0, tiled=T...  24.3 us
    all_gather x1, waiting for transfers between devices, on_device(): expert_gate_up = lax.all_gather(column_half, 'core', axis=1, tiled=True)  21.2 us
    all_to_all x2, waiting for transfers between devices, from_everyone(): lax.all_to_all(jnp.broadcast_to(array[None], (peers, *array.shape)), axis...  20.9 us
  transfers between devices with their start and end apart: 15, of which 13 were waited for; matrix products, arithmetic and copies ran while one was open for 13% of the time, Pallas kernels for 0%

profile of v5, /device:TPU:2, one launch (start us, length us, event | category | flops | bytes accessed | tf_op | source)
XLA Modules:
  0.0 615.5 jit_solution(16798864063756449822)
XLA Ops:
  8.2 11.5 %all_to_all.56 = bf16[8,4,1280]{2,0,1:T(8,128)(2,1)S(1)} all-to-all(bf16[8,4,1280]{2,0,1:T(8,128)(2,1)S(1)} %pad_maximum_fusion.1), channel_id=1, replica_groups=mesh['zh'=2,'sub2'=16,'core'=2,'tp'=4] {'tp'}, dimensions={1} | all-to-all | bytes 163840 | tf_op jit(solution)/shard_map/all_to_all | solution.py:186
  19.7 10.0 %all_gather.16 = bf16[64,1280]{1,0:T(8,128)(2,1)} all-gather(bf16[32,1280]{1,0:T(8,128)(2,1)S(1)} %bitcast.158), channel_id=1, replica_groups=mesh['zh'=2,'sub2'=16,'core'=2,'tp'=4] {'zh'}, dimensions={0}, use_global_device_ids=true | all-gather | bytes 245760 | tf_op jit(solution)/shard_map/all_gather | solution.py:187
  36.6 11.0 %collective-permute-done = bf16[192,2048]{1,0:T(8,128)(2,1)S(1)} collective-permute-done((bf16[192,2048]{1,0:T(8,128)(2,1)S(1)}, bf16[192,2048]{1,0:T(8,128)(2,1)S(1)}, u32[]{:S(2)}, u32[]{:S(2)}) %collective-permute-start) | collective-permute-done | bytes 786464 | tf_op jit(solution)/shard_map/ppermute | solution.py:141
  47.6 14.7 %collective-permute-done.2 = bf16[192,2048]{1,0:T(8,128)(2,1)S(1)} collective-permute-done((bf16[192,2048]{1,0:T(8,128)(2,1)S(1)}, bf16[192,2048]{1,0:T(8,128)(2,1)S(1)}, u32[]{:S(2)}, u32[]{:S(2)}) %collective-permute-start.2) | collective-permute-done | bytes 786464 | tf_op jit(solution)/shard_map/ppermute | solution.py:141
  72.8 7.5 %all-gather.5.cloned.1.call-done = bf16[1024,1280]{1,0:T(8,128)(2,1)} async-done(((bf16[64,1280]{1,0:T(8,128)(2,1)}), bf16[1024,1280]{1,0:T(8,128)(2,1)}) %all-gather.5.cloned.1.call-update) | async-done | bytes 2621456 | tf_op jit(solution)/shard_map/all_gather | solution.py:188
  80.3 8.3 %all-gather = s32[2,64,8]{1,2,0:T(8,128)S(1)} all-gather(s32[1,64,8]{1,2,0:T(8,128)S(1)} %bitcast.167), channel_id=1, replica_groups=mesh['zh'=2,'sub2'=16,'core'=2,'tp'=4] {'zh'}, dimensions={0}, use_global_device_ids=true | all-gather | bytes 6144 | tf_op jit(solution)/shard_map/all_gather | solution.py:149
  105.0 15.7 %all-to-all-done = bf16[4,64,2048]{2,1,0:T(8,128)(2,1)S(1)} async-done(((bf16[4,64,2048]{2,1,0:T(8,128)(2,1)}), bf16[4,64,2048]{2,1,0:T(8,128)(2,1)S(1)}, u32[]{:S(2)}, u32[]{:S(2)}) %all-to-all-start) | async-done | bytes 1048608 | tf_op jit(solution)/shard_map/all_to_all | solution.py:29
  120.7 6.6 %all-to-all-start.5 = ((bf16[2,64,8,1536]{3,2,1,0:T(8,128)(2,1)}), bf16[2,64,8,1536]{3,2,1,0:T(8,128)(2,1)}, u32[]{:S(2)}, u32[]{:S(2)}) async-start(bf16[2,64,8,1536]{3,2,1,0:T(8,128)(2,1)} %bitcast.145), calls=%async_computation.5 | async-start | bytes 6291456 | tf_op jit(solution)/shard_map/all_to_all | solution.py:156
  149.1 49.0 %all-to-all-done.5 = bf16[2,64,8,1536]{3,2,1,0:T(8,128)(2,1)} async-done(((bf16[2,64,8,1536]{3,2,1,0:T(8,128)(2,1)}), bf16[2,64,8,1536]{3,2,1,0:T(8,128)(2,1)}, u32[]{:S(2)}, u32[]{:S(2)}) %all-to-all-start.5) | async-done | bytes 3145760 | tf_op jit(solution)/shard_map/all_to_all | solution.py:156
  202.7 7.5 %reshape.761 = bf16[2,16,4,8,2,768]{5,4,3,2,1,0:T(2,128)(2,1)} reshape(bf16[2,64,8,1536]{3,2,1,0:T(8,128)(2,1)} %all-to-all-done.5) | data formatting | bytes 6291456 | tf_op jit(solution)/shard_map/reshape | solution.py:157
  215.1 11.8 %all-to-all-done.2 = bf16[4,64,2048]{2,1,0:T(8,128)(2,1)} async-done(((bf16[4,64,2048]{2,1,0:T(8,128)(2,1)}), bf16[4,64,2048]{2,1,0:T(8,128)(2,1)}, u32[]{:S(2)}, u32[]{:S(2)}) %all-to-all-start.2) | async-done | bytes 1048608 | tf_op jit(solution)/shard_map/all_to_all | solution.py:46
  234.2 6.5 %maximum_bitcast_fusion = bf16[16,2,4,2,8,768]{5,1,4,2,0,3:T(2,128)(2,1)S(1)} fusion(bf16[2,16,1,8,2,768]{5,4,3,2,1,0:T(2,128)(2,1)} %get-tuple-element.23, bf16[2,16,1,8,2,768]{5,4,3,2,1,0:T(2,128)(2,1)} %get-tuple-element.24, bf16[2,16,1,8,2,768]{5,4,3,2,1,0:T(2,128)(2,1)} %get-tuple-element.25, bf16[2,16,1,8,2,768]{5,4,3,2,1,0:T(2,128)(2,1)} %get-tuple-element.22), kind=kLoop, calls=%fused_computation.18 | loop fusion | flops 4718592 | bytes 6291456 | tf_op jit(solution)/shard_map/transpose | solution.py:159
  248.3 7.4 %all-to-all-start.6 = ((bf16[128,16,768]{2,1,0:T(8,128)(2,1)}), bf16[128,16,768]{2,1,0:T(8,128)(2,1)}, u32[]{:S(2)}, u32[]{:S(2)}) async-start(bf16[128,16,768]{2,1,0:T(8,128)(2,1)} %bitcast.144), calls=%async_computation.6 | async-start | bytes 6291456 | tf_op jit(solution)/shard_map/all_to_all | solution.py:160
  256.8 9.1 %scatter_custom_fusion = bf16[1024,2048]{1,0:T(8,128)(2,1)} fusion(s32[1024]{0:T(1024)S(1)} %bitcast.168, bf16[128,2048]{1,0:T(8,128)(2,1)S(1)} %bitcast.147, bf16[]{:T(256)} %constant.219.clone.1), kind=kCustom, calls=%fused_computation.7 | custom fusion | bytes 4718594 | tf_op jit(solution)/shard_map/scatter | solution.py:251
  265.8 63.6 %all-to-all-done.6 = bf16[128,16,768]{2,1,0:T(8,128)(2,1)} async-done(((bf16[128,16,768]{2,1,0:T(8,128)(2,1)}), bf16[128,16,768]{2,1,0:T(8,128)(2,1)}, u32[]{:S(2)}, u32[]{:S(2)}) %all-to-all-start.6) | async-done | bytes 3145760 | tf_op jit(solution)/shard_map/all_to_all | solution.py:160
  340.1 21.2 %all-gather.9.cloned.1.call-done = bf16[2048,1536]{1,0:T(8,128)(2,1)} async-done(((bf16[2048,768]{1,0:T(8,128)(2,1)}), bf16[2048,1536]{1,0:T(8,128)(2,1)}) %all-gather.9.cloned.1.call-update) | async-done | bytes 6291472 | tf_op jit(solution)/shard_map/all_gather | solution.py:166
  361.3 70.5 %all-to-all-done.4 = bf16[64,16,2048]{2,1,0:T(8,128)(2,1)} async-done(((bf16[64,16,2048]{2,1,0:T(8,128)(2,1)}), bf16[64,16,2048]{2,1,0:T(8,128)(2,1)}, u32[]{:S(2)}, u32[]{:S(2)}) %all-to-all-start.4) | async-done | bytes 4194336 | tf_op jit(solution)/shard_map/all_to_all | solution.py:253
  431.9 10.0 %fusion.76 = f32[1024,1536]{1,0:T(8,128)S(1)} fusion(bf16[1024,2048]{1,0:T(8,128)(2,1)} %bitcast.33, bf16[2048,1536]{1,0:T(8,128)(2,1)} %all-gather.9.cloned.1.call-done), kind=kOutput, calls=%fused_computation.186 | convolution fusion | flops 6442450944 | bytes 16777216 | tf_op jit(solution)/shard_map/dot_general | solution.py:257
  454.1 8.2 %all-to-all-start.7 = ((bf16[64,16,2048]{2,1,0:T(8,128)(2,1)}), bf16[64,16,2048]{2,1,0:T(8,128)(2,1)}, u32[]{:S(2)}, u32[]{:S(2)}) async-start(bf16[64,16,2048]{2,1,0:T(8,128)(2,1)} %bitcast.141), calls=%async_computation.7 | async-start | bytes 8388608 | tf_op jit(solution)/shard_map/all_to_all | solution.py:268
  462.8 6.8 %gather_fusion.1 = f32[1024]{0:T(1024)S(1)} fusion(f32[128,128]{1,0:T(8,128)S(1)} %fusion.75, s32[1024]{0:T(1024)S(1)} %reshape.778), kind=kCustom, calls=%fused_computation.1 | custom fusion | bytes 16384 | tf_op jit(solution)/shard_map/jit(take_along_axis)/gather | solution.py:229
  469.9 87.7 %all-to-all-done.7 = bf16[64,16,2048]{2,1,0:T(8,128)(2,1)} async-done(((bf16[64,16,2048]{2,1,0:T(8,128)(2,1)}), bf16[64,16,2048]{2,1,0:T(8,128)(2,1)}, u32[]{:S(2)}, u32[]{:S(2)}) %all-to-all-start.7) | async-done | bytes 4194336 | tf_op jit(solution)/shard_map/all_to_all | solution.py:268
  557.6 11.5 %gather_fusion = bf16[1024,2048]{1,0:T(8,128)(2,1)} fusion(bf16[1024,2048]{1,0:T(8,128)(2,1)} %bitcast.45, s32[1024]{0:T(1024)S(1)} %broadcast_clamp_fusion), kind=kCustom, calls=%fused_computation | custom fusion | bytes 8392704 | tf_op jit(solution)/shard_map/gather | solution.py:269
  569.1 7.5 %fusion = f32[128,2048]{1,0:T(8,128)} fusion(bf16[1024,2048]{1,0:T(8,128)(2,1)} %gather_fusion, f32[128,8]{1,0:T(8,128)S(1)} %copy.100), kind=kLoop, calls=%fused_computation.5 | loop fusion | flops 6029312 | bytes 5246976 | tf_op jit(solution)/shard_map/reduce_sum | solution.py:273
  582.2 24.3 %all-to-all-done.8 = f32[2,64,2048]{2,1,0:T(8,128)} async-done(((f32[2,64,2048]{2,1,0:T(8,128)}), f32[2,64,2048]{2,1,0:T(8,128)}, u32[]{:S(2)}, u32[]{:S(2)}) %all-to-all-start.8) | async-done | bytes 1048608 | tf_op jit(solution)/shard_map/all_to_all | solution.py:278
  (139 shorter events, 112.3 us)
Async XLA Ops:
  7.2 455.3 %copy-start = (bf16[2048,128]{1,0:T(8,128)(2,1)S(1)}, bf16[2048,128]{1,0:T(8,128)(2,1)}, u32[]{:S(2)}) copy-start(bf16[2048,128]{1,0:T(8,128)(2,1)} %param.20) | copy-start | bytes 1572868
  7.2 73.1 %all-gather.5.cloned.1.call-start = ((), (), s32[]{:S(2)}) async-start(), calls=%async_computation.9 | async-start | bytes 2785280 | tf_op jit(solution)/shard_map/all_gather | solution.py:188
  29.7 105.5 %all-gather.7.cloned.1.call-start = ((), (), s32[]{:S(2)}) async-start(), calls=%async_computation.10 | async-start | bytes 7864320 | tf_op jit(solution)/shard_map/all_gather | solution.py:189
  32.0 15.5 %collective-permute-start = (bf16[192,2048]{1,0:T(8,128)(2,1)S(1)}, bf16[192,2048]{1,0:T(8,128)(2,1)S(1)}, u32[]{:S(2)}, u32[]{:S(2)}) collective-permute-start(bf16[192,2048]{1,0:T(8,128)(2,1)S(1)} %get-tuple-element.27), channel_id=1, source_target_pairs={{1,0},{3,2},{4,7},{6,5},{9,8},{11,10},{12,15},{14,13},{17,16},{19,... | collective-permute-start | bytes 2359304 | tf_op jit(solution)/shard_map/ppermute | solution.py:141
  33.3 28.9 %collective-permute-start.2 = (bf16[192,2048]{1,0:T(8,128)(2,1)S(1)}, bf16[192,2048]{1,0:T(8,128)(2,1)S(1)}, u32[]{:S(2)}, u32[]{:S(2)}) collective-permute-start(bf16[192,2048]{1,0:T(8,128)(2,1)S(1)} %get-tuple-element.28), channel_id=1, source_target_pairs={{1,2},{3,0},{4,5},{6,7},{9,10},{11,8},{12,13},{14,15},{17,18},{19,... | collective-permute-start | bytes 2359304 | tf_op jit(solution)/shard_map/ppermute | solution.py:141
  34.6 33.3 %collective-permute-start.1 = (bf16[192,2048]{1,0:T(8,128)(2,1)S(1)}, bf16[192,2048]{1,0:T(8,128)(2,1)S(1)}, u32[]{:S(2)}, u32[]{:S(2)}) collective-permute-start(bf16[192,2048]{1,0:T(8,128)(2,1)S(1)} %get-tuple-element.29), channel_id=1, source_target_pairs={{0,2},{2,0},{5,7},{7,5},{8,10},{10,8},{13,15},{15,13},{16,18},{18,... | collective-permute-start | bytes 2359304 | tf_op jit(solution)/shard_map/ppermute | solution.py:141
  68.0 12.4 %copy-start.13 = (s32[64,8]{0,1:T(8,128)S(1)}, s32[64,8]{0,1:T(8,128)}, u32[]{:S(2)}) copy-start(s32[64,8]{0,1:T(8,128)} %param.23) | copy-start | bytes 6148
  69.8 18.9 %collective-permute-start.3 = (bf16[4,192,2048]{2,1,0:T(8,128)(2,1)}, bf16[4,192,2048]{2,1,0:T(8,128)(2,1)}, u32[]{:S(2)}, u32[]{:S(2)}) collective-permute-start(bf16[4,192,2048]{2,1,0:T(8,128)(2,1)} %pad_maximum_fusion), channel_id=1, source_target_pairs={{0,4},{5,1},{2,6},{7,3},{8,12},{13,9},{10,14},{15,11},{16,20},{21,... | collective-permute-start | bytes 9437192 | tf_op jit(solution)/shard_map/ppermute | solution.py:148
  92.7 28.1 %all-to-all-start = ((bf16[4,64,2048]{2,1,0:T(8,128)(2,1)}), bf16[4,64,2048]{2,1,0:T(8,128)(2,1)S(1)}, u32[]{:S(2)}, u32[]{:S(2)}) async-start(bf16[4,64,2048]{2,1,0:T(8,128)(2,1)} %broadcast_in_dim.59), calls=%async_computation | async-start | bytes 2097152 | tf_op jit(solution)/shard_map/all_to_all | solution.py:29
  103.7 17.0 %copy-start.16 = (f32[64]{0:T(128)}, f32[64]{0:T(128)S(1)}, u32[]{:S(2)}) copy-start(f32[64]{0:T(128)S(1)} %multiply_power_fusion) | copy-start | bytes 772
  103.8 17.0 %copy-start.14 = (pred[256]{0:T(512)(128)(4,1)}, pred[256]{0:T(512)(128)(4,1)S(1)}, u32[]{:S(2)}) copy-start(pred[256]{0:T(512)(128)(4,1)S(1)} %iota_compare_fusion.8) | copy-start | bytes 772
  120.7 77.4 %all-to-all-start.5 = ((bf16[2,64,8,1536]{3,2,1,0:T(8,128)(2,1)}), bf16[2,64,8,1536]{3,2,1,0:T(8,128)(2,1)}, u32[]{:S(2)}, u32[]{:S(2)}) async-start(bf16[2,64,8,1536]{3,2,1,0:T(8,128)(2,1)} %bitcast.145), calls=%async_computation.5 | async-start | bytes 6291456 | tf_op jit(solution)/shard_map/all_to_all | solution.py:156
  198.1 28.7 %all-to-all-start.2 = ((bf16[4,64,2048]{2,1,0:T(8,128)(2,1)}), bf16[4,64,2048]{2,1,0:T(8,128)(2,1)}, u32[]{:S(2)}, u32[]{:S(2)}) async-start(bf16[4,64,2048]{2,1,0:T(8,128)(2,1)} %bitcast.26), calls=%async_computation.2 | async-start | bytes 2097152 | tf_op jit(solution)/shard_map/all_to_all | solution.py:46
  210.2 18.3 %copy-start.11 = (f32[2048]{0:T(1024)S(1)}, f32[2048]{0:T(1024)}, u32[]{:S(2)}) copy-start(f32[2048]{0:T(1024)} %param.19) | copy-start | bytes 24580
  229.5 18.8 %all-to-all-start.3 = ((bf16[2,64,2048]{2,1,0:T(8,128)(2,1)}), bf16[2,64,2048]{2,1,0:T(8,128)(2,1)S(1)}, u32[]{:S(2)}, u32[]{:S(2)}) async-start(bf16[2,64,2048]{2,1,0:T(8,128)(2,1)} %broadcast_in_dim.62), calls=%async_computation.3 | async-start | bytes 1048576 | tf_op jit(solution)/shard_map/all_to_all | solution.py:29
  248.3 81.1 %all-to-all-start.6 = ((bf16[128,16,768]{2,1,0:T(8,128)(2,1)}), bf16[128,16,768]{2,1,0:T(8,128)(2,1)}, u32[]{:S(2)}, u32[]{:S(2)}) async-start(bf16[128,16,768]{2,1,0:T(8,128)(2,1)} %bitcast.144), calls=%async_computation.6 | async-start | bytes 6291456 | tf_op jit(solution)/shard_map/all_to_all | solution.py:160
  329.4 102.5 %all-to-all-start.4 = ((bf16[64,16,2048]{2,1,0:T(8,128)(2,1)}), bf16[64,16,2048]{2,1,0:T(8,128)(2,1)}, u32[]{:S(2)}, u32[]{:S(2)}) async-start(bf16[64,16,2048]{2,1,0:T(8,128)(2,1)} %bitcast.142), calls=%async_computation.4 | async-start | bytes 8388608 | tf_op jit(solution)/shard_map/all_to_all | solution.py:253
  335.9 25.5 %all-gather.9.cloned.1.call-start = ((), (), s32[]{:S(2)}) async-start(), calls=%async_computation.11 | async-start | bytes 9437184 | tf_op jit(solution)/shard_map/all_gather | solution.py:166
  454.1 103.5 %all-to-all-start.7 = ((bf16[64,16,2048]{2,1,0:T(8,128)(2,1)}), bf16[64,16,2048]{2,1,0:T(8,128)(2,1)}, u32[]{:S(2)}, u32[]{:S(2)}) async-start(bf16[64,16,2048]{2,1,0:T(8,128)(2,1)} %bitcast.141), calls=%async_computation.7 | async-start | bytes 8388608 | tf_op jit(solution)/shard_map/all_to_all | solution.py:268
  569.1 12.1 %copy-start.9 = (bf16[256,1,64]{2,0,1:T(8,128)(2,1)S(1)}, bf16[256,1,64]{2,0,1:T(8,128)(2,1)}, u32[]{:S(2)}) copy-start(bf16[256,1,64]{2,0,1:T(8,128)(2,1)} %copy-done.8) | copy-start | bytes 98308
  569.1 12.3 %copy-start.15 = (pred[256]{0:T(512)(128)(4,1)S(1)}, pred[256]{0:T(512)(128)(4,1)}, u32[]{:S(2)}) copy-start(pred[256]{0:T(512)(128)(4,1)} %copy-done.14) | copy-start | bytes 772
  576.6 31.3 %copy-start.3 = (bf16[64,2048]{1,0:T(8,128)(2,1)S(1)}, bf16[64,2048]{1,0:T(8,128)(2,1)}, u32[]{:S(2)}) copy-start(bf16[64,2048]{1,0:T(8,128)(2,1)} %param.13) | copy-start | bytes 786436
  576.6 29.9 %all-to-all-start.8 = ((f32[2,64,2048]{2,1,0:T(8,128)}), f32[2,64,2048]{2,1,0:T(8,128)}, u32[]{:S(2)}, u32[]{:S(2)}) async-start(f32[2,64,2048]{2,1,0:T(8,128)} %bitcast.150), calls=%async_computation.8 | async-start | bytes 2097152 | tf_op jit(solution)/shard_map/all_to_all | solution.py:278
  582.2 26.5 %copy-start.5 = (bf16[4,2,128,128]{3,2,1,0:T(8,128)(2,1)}, bf16[4,2,128,128]{3,2,1,0:T(8,128)(2,1)S(1)}, u32[]{:S(2)}) copy-start(bf16[4,2,128,128]{3,2,1,0:T(8,128)(2,1)S(1)} %scatter_fusion) | copy-start | bytes 786436
  (10 other events, 48.6 us)
Sparse Core Ops, SparseCore 0:
  29.9 50.3 all-gather.4
  82.1 20.3 all-gather.6
  340.2 21.1 all-gather.8

commit v6 on v5

--- a/solution.py
+++ b/solution.py
@@ -147,27 +147,11 @@
                 share.append((flat(a, b, d % 2, d), flat(a, b, 1 - d % 2, d)))
     slots = jnp.where(primary, slots, lax.ppermute(slots, everyone, perm=share))
     both_routes = lax.all_gather(routes, "zh", axis=0, tiled=True)
-    slots, both_routes, hidden_in = lax.optimization_barrier((slots, both_routes, hidden_in))
-
     trainer_block = gate_up_master.shape[1]
     gate_up_half = gate_up_master.astype(jnp.bfloat16).reshape(
         n_zh, half_experts, trainer_block, 2 * FF
     )
     gate_up_half = lax.all_to_all(gate_up_half, "zh", 0, 0, tiled=True)
-    pieces = gate_up_half.reshape(n_zh, n_sub, n_tp, trainer_block, n_core, FF)
-    pieces = jnp.stack([pieces[:, :, 2 * (d % 2) + d // 2] for d in range(n_tp)], axis=2)
-    pieces = pieces.transpose(1, 4, 2, 0, 3, 5).reshape(n_sub * n_core * n_tp, -1, FF)
-    pieces = lax.all_to_all(pieces, ("sub2", "core", "tp"), 0, 0, tiled=True)
-    column_half = (
-        pieces.reshape(n_sub, n_core, n_tp, n_zh, trainer_block, FF)
-        .transpose(3, 0, 1, 2, 4, 5)
-        .reshape(-1, FF)
-    )
-    expert_gate_up = lax.all_gather(column_half, "core", axis=1, tiled=True)
-
-    prompt_rows = collect(hidden_in, "tp", 0)
-    column_span = prompt_rows.shape[0]
-    normed = rms_scale(prompt_rows.astype(jnp.float32), attention_gain).astype(jnp.bfloat16)
     trainer_rows = attention_trainer_copy.shape[0]
     query_cols = attention_trainer_copy[:, : QUERY_HEADS * HEAD_SIZE].reshape(
         trainer_rows, n_tp, heads_here * HEAD_SIZE
@@ -186,6 +170,23 @@
     head_rows = lax.all_to_all(joined, "tp", split_axis=1, concat_axis=0, tiled=True)
     head_rows = lax.all_gather(head_rows, "zh", axis=0, tiled=True)
     head_rows = lax.all_gather(head_rows, "sub2", axis=0, tiled=True)
+    slots, both_routes, gate_up_half, head_rows, hidden_in = lax.optimization_barrier(
+        (slots, both_routes, gate_up_half, head_rows, hidden_in)
+    )
+
+    pieces = gate_up_half.reshape(n_zh, n_sub, n_tp, trainer_block, n_core, FF)
+    pieces = jnp.stack([pieces[:, :, 2 * (d % 2) + d // 2] for d in range(n_tp)], axis=2)
+    pieces = pieces.transpose(1, 4, 2, 0, 3, 5).reshape(n_sub * n_core * n_tp, -1, FF)
+    pieces = lax.all_to_all(pieces, ("sub2", "core", "tp"), 0, 0, tiled=True)
+    column_half = (
+        pieces.reshape(n_sub, n_core, n_tp, n_zh, trainer_block, FF)
+        .transpose(3, 0, 1, 2, 4, 5)
+        .reshape(-1, FF)
+    )
+
+    prompt_rows = collect(hidden_in, "tp", 0)
+    column_span = prompt_rows.shape[0]
+    normed = rms_scale(prompt_rows.astype(jnp.float32), attention_gain).astype(jnp.bfloat16)
     head_rows = lax.all_gather(head_rows, "core", axis=0, tiled=True)
     seq_block = head_rows.shape[0] // (n_zh * n_sub * n_core)
     normed_order = (
@@ -215,6 +216,8 @@
         values_local_rows,
         prompt_length,
     )
+    column_half, context_rows = lax.optimization_barrier((column_half, context_rows))
+    expert_gate_up = lax.all_gather(column_half, "core", axis=1, tiled=True)
     attention_sums = summed_on_arrival(
         jnp.dot(context_rows, output_proj, preferred_element_type=jnp.float32).astype(jnp.bfloat16),
         "tp",

time: 628 us -> 628 us (level)
  waiting for transfers between devices: 388 us -> 339 us
  blocking collectives: 29.7 us -> 72 us
  starting transfers between devices: 55.6 us -> 65.7 us
    all_gather x1, blocking collectives: 8.27 us -> 62 us  [on_device(): both_routes = lax.all_gather(routes, 'zh', axis=0, tiled=True)]
    all_to_all x1, waiting for transfers between devices: 49 us -> 0.01 us  [on_device(): gate_up_half = lax.all_to_all(gate_up_half, 'zh', 0, 0, tiled=True)]
    all_to_all x1, waiting for transfers between devices: 11.8 us -> 24.9 us  [summed_on_arrival(): lax.all_to_all(in_blocks(array, dim, peers), axis, 0, 0, tiled=True)]
    all_to_all x1 -> x0, blocking collectives: 11.5 us -> none  [on_device(): lax.all_to_all(joined, 'tp', split_axis=1, concat_axis=0, tiled=True)]
    all_to_all x1, waiting for transfers between devices: 63.6 us -> 53.3 us  [on_device(): pieces = lax.all_to_all(pieces, ('sub2', 'core', 'tp'), 0, 0, tiled=True)]
    all_gather x1, waiting for transfers between devices: 7.48 us -> 0.01 us  [on_device(): head_rows = lax.all_gather(head_rows, 'sub2', axis=0, tiled=True)]
  transfers between devices with their start and end apart: 15 -> 16, of which waited for: 13 -> 12; matrix products, arithmetic and copies ran while one was open for 13% -> 10% of each run, Pallas kernels for 0% -> 0%
where the time goes in v6:
time: 628 us; the launch traced here: 617 us
  waiting for transfers between devices  339 us (54%)
  blocking collectives  72 us (11%)
  starting transfers between devices  65.7 us (10%)
  local copies, waits for them, and re-layouts  59.5 us (9%)
  other arithmetic  39.7 us (6%)
  matrix products  26.2 us (4%)
  between operations  15.3 us (2%)
    all_to_all x1, waiting for transfers between devices, on_device(): returned = lax.all_to_all(expert_result, group, 0, 0, tiled=True)  85.8 us
    all_to_all x1, waiting for transfers between devices, on_device(): lax.all_to_all(outgoing.reshape(n_group, capacity, width), group, 0, 0, t...  70.4 us
    all_gather x1, blocking collectives, on_device(): both_routes = lax.all_gather(routes, 'zh', axis=0, tiled=True)  62 us
    all_to_all x1, waiting for transfers between devices, on_device(): pieces = lax.all_to_all(pieces, ('sub2', 'core', 'tp'), 0, 0, tiled=True)  53.3 us
    ppermute x3, waiting for transfers between devices, on_device(): slots.append(lax.ppermute(sent, everyone, perm=pairs))  31.4 us
    all_to_all x1, waiting for transfers between devices, summed_on_arrival(): lax.all_to_all(in_blocks(array, dim, peers), axis, 0, 0, tiled=True)  24.9 us
    all_to_all x1, waiting for transfers between devices, on_device(): lax.all_to_all(partial.reshape(n_zh, quarter, width), 'zh', 0, 0, tiled=T...  23.1 us
    all_gather x1, waiting for transfers between devices, on_device(): expert_gate_up = lax.all_gather(column_half, 'core', axis=1, tiled=True)  23 us
  transfers between devices with their start and end apart: 16, of which 12 were waited for; matrix products, arithmetic and copies ran while one was open for 10% of the time, Pallas kernels for 0%

profile of v6, /device:TPU:2, one launch (start us, length us, event | category | flops | bytes accessed | tf_op | source)
XLA Modules:
  0.0 617.4 jit_solution(10315052507494036723)
XLA Ops:
  8.8 5.9 all-to-all-start.1
  20.5 10.0 %all_gather.16 = bf16[64,1280]{1,0:T(8,128)(2,1)} all-gather(bf16[32,1280]{1,0:T(8,128)(2,1)S(1)} %bitcast.158), channel_id=1, replica_groups=mesh['zh'=2,'sub2'=16,'core'=2,'tp'=4] {'zh'}, dimensions={0}, use_global_device_ids=true | all-gather | bytes 245760 | tf_op jit(solution)/shard_map/all_gather | solution.py:171
  37.2 11.0 %collective-permute-done = bf16[192,2048]{1,0:T(8,128)(2,1)S(1)} collective-permute-done((bf16[192,2048]{1,0:T(8,128)(2,1)S(1)}, bf16[192,2048]{1,0:T(8,128)(2,1)S(1)}, u32[]{:S(2)}, u32[]{:S(2)}) %collective-permute-start) | collective-permute-done | bytes 786464 | tf_op jit(solution)/shard_map/ppermute | solution.py:141
  48.2 14.7 %collective-permute-done.2 = bf16[192,2048]{1,0:T(8,128)(2,1)S(1)} collective-permute-done((bf16[192,2048]{1,0:T(8,128)(2,1)S(1)}, bf16[192,2048]{1,0:T(8,128)(2,1)S(1)}, u32[]{:S(2)}, u32[]{:S(2)}) %collective-permute-start.2) | collective-permute-done | bytes 786464 | tf_op jit(solution)/shard_map/ppermute | solution.py:141
  78.3 6.3 %all-to-all-start = ((bf16[2,64,8,1536]{3,2,1,0:T(8,128)(2,1)}), bf16[2,64,8,1536]{3,2,1,0:T(8,128)(2,1)}, u32[]{:S(2)}, u32[]{:S(2)}) async-start(bf16[2,64,8,1536]{3,2,1,0:T(8,128)(2,1)} %bitcast.145), calls=%async_computation | async-start | bytes 6291456 | tf_op jit(solution)/shard_map/all_to_all | solution.py:154
  84.6 62.0 %all-gather = s32[2,64,8]{1,2,0:T(8,128)S(1)} all-gather(s32[1,64,8]{1,2,0:T(8,128)S(1)} %bitcast.167), channel_id=1, replica_groups=mesh['zh'=2,'sub2'=16,'core'=2,'tp'=4] {'zh'}, dimensions={0}, use_global_device_ids=true | all-gather | bytes 6144 | tf_op jit(solution)/shard_map/all_gather | solution.py:149
  150.8 6.8 %all-to-all-start.3 = ((bf16[4,64,2048]{2,1,0:T(8,128)(2,1)}), bf16[4,64,2048]{2,1,0:T(8,128)(2,1)S(1)}, u32[]{:S(2)}, u32[]{:S(2)}) async-start(bf16[4,64,2048]{2,1,0:T(8,128)(2,1)} %broadcast_in_dim.59), calls=%async_computation.3 | async-start | bytes 2097152 | tf_op jit(solution)/shard_map/all_to_all | solution.py:29
  157.6 7.5 %reshape.749 = bf16[2,16,4,8,2,768]{5,4,3,2,1,0:T(2,128)(2,1)} reshape(bf16[2,64,8,1536]{3,2,1,0:T(8,128)(2,1)} %all-to-all-done) | data formatting | bytes 6291456 | tf_op jit(solution)/shard_map/reshape | solution.py:177
  175.9 7.4 %all-to-all-done.3 = bf16[4,64,2048]{2,1,0:T(8,128)(2,1)S(1)} async-done(((bf16[4,64,2048]{2,1,0:T(8,128)(2,1)}), bf16[4,64,2048]{2,1,0:T(8,128)(2,1)S(1)}, u32[]{:S(2)}, u32[]{:S(2)}) %all-to-all-start.3) | async-done | bytes 1048608 | tf_op jit(solution)/shard_map/all_to_all | solution.py:29
  183.3 11.1 %all-to-all-start.2 = ((bf16[128,16,768]{2,1,0:T(8,128)(2,1)}), bf16[128,16,768]{2,1,0:T(8,128)(2,1)}, u32[]{:S(2)}, u32[]{:S(2)}) async-start(bf16[128,16,768]{2,1,0:T(8,128)(2,1)} %bitcast.144), calls=%async_computation.2 | async-start | bytes 6291456 | tf_op jit(solution)/shard_map/all_to_all | solution.py:180
  214.5 53.3 %all-to-all-done.2 = bf16[128,16,768]{2,1,0:T(8,128)(2,1)} async-done(((bf16[128,16,768]{2,1,0:T(8,128)(2,1)}), bf16[128,16,768]{2,1,0:T(8,128)(2,1)}, u32[]{:S(2)}, u32[]{:S(2)}) %all-to-all-start.2) | async-done | bytes 3145760 | tf_op jit(solution)/shard_map/all_to_all | solution.py:180
  281.0 24.9 %all-to-all-done.4 = bf16[4,64,2048]{2,1,0:T(8,128)(2,1)} async-done(((bf16[4,64,2048]{2,1,0:T(8,128)(2,1)}), bf16[4,64,2048]{2,1,0:T(8,128)(2,1)}, u32[]{:S(2)}, u32[]{:S(2)}) %all-to-all-start.4) | async-done | bytes 1048608 | tf_op jit(solution)/shard_map/all_to_all | solution.py:46
  313.3 13.5 %all-to-all-done.5 = bf16[2,64,2048]{2,1,0:T(8,128)(2,1)S(1)} async-done(((bf16[2,64,2048]{2,1,0:T(8,128)(2,1)}), bf16[2,64,2048]{2,1,0:T(8,128)(2,1)S(1)}, u32[]{:S(2)}, u32[]{:S(2)}) %all-to-all-start.5) | async-done | bytes 524320 | tf_op jit(solution)/shard_map/all_to_all | solution.py:29
  326.8 9.0 %scatter_custom_fusion = bf16[1024,2048]{1,0:T(8,128)(2,1)} fusion(s32[1024]{0:T(1024)S(1)} %bitcast.168, bf16[128,2048]{1,0:T(8,128)(2,1)S(1)} %bitcast.147, bf16[]{:T(256)} %constant.219.clone.1), kind=kCustom, calls=%fused_computation.7 | custom fusion | bytes 4718594 | tf_op jit(solution)/shard_map/scatter | solution.py:254
  335.8 7.8 %all-to-all-start.6 = ((bf16[64,16,2048]{2,1,0:T(8,128)(2,1)}), bf16[64,16,2048]{2,1,0:T(8,128)(2,1)}, u32[]{:S(2)}, u32[]{:S(2)}) async-start(bf16[64,16,2048]{2,1,0:T(8,128)(2,1)} %bitcast.142), calls=%async_computation.6 | async-start | bytes 8388608 | tf_op jit(solution)/shard_map/all_to_all | solution.py:256
  344.4 23.0 %all-gather.9.cloned.1.call-done = bf16[2048,1536]{1,0:T(8,128)(2,1)} async-done(((bf16[2048,768]{1,0:T(8,128)(2,1)}), bf16[2048,1536]{1,0:T(8,128)(2,1)}) %all-gather.9.cloned.1.call-update) | async-done | bytes 6291472 | tf_op jit(solution)/shard_map/all_gather | solution.py:220
  367.4 70.4 %all-to-all-done.6 = bf16[64,16,2048]{2,1,0:T(8,128)(2,1)} async-done(((bf16[64,16,2048]{2,1,0:T(8,128)(2,1)}), bf16[64,16,2048]{2,1,0:T(8,128)(2,1)}, u32[]{:S(2)}, u32[]{:S(2)}) %all-to-all-start.6) | async-done | bytes 4194336 | tf_op jit(solution)/shard_map/all_to_all | solution.py:256
  437.8 10.0 %fusion.76 = f32[1024,1536]{1,0:T(8,128)S(1)} fusion(bf16[1024,2048]{1,0:T(8,128)(2,1)} %bitcast.39, bf16[2048,1536]{1,0:T(8,128)(2,1)} %all-gather.9.cloned.1.call-done), kind=kOutput, calls=%fused_computation.186 | convolution fusion | flops 6442450944 | bytes 16777216 | tf_op jit(solution)/shard_map/dot_general | solution.py:260
  460.0 7.3 %all-to-all-start.7 = ((bf16[64,16,2048]{2,1,0:T(8,128)(2,1)}), bf16[64,16,2048]{2,1,0:T(8,128)(2,1)}, u32[]{:S(2)}, u32[]{:S(2)}) async-start(bf16[64,16,2048]{2,1,0:T(8,128)(2,1)} %bitcast.141), calls=%async_computation.7 | async-start | bytes 8388608 | tf_op jit(solution)/shard_map/all_to_all | solution.py:271
  467.8 6.8 %gather_fusion.1 = f32[1024]{0:T(1024)S(1)} fusion(f32[128,128]{1,0:T(8,128)S(1)} %fusion.75, s32[1024]{0:T(1024)S(1)} %reshape.778), kind=kCustom, calls=%fused_computation.1 | custom fusion | bytes 16384 | tf_op jit(solution)/shard_map/jit(take_along_axis)/gather | solution.py:232
  474.9 85.8 %all-to-all-done.7 = bf16[64,16,2048]{2,1,0:T(8,128)(2,1)} async-done(((bf16[64,16,2048]{2,1,0:T(8,128)(2,1)}), bf16[64,16,2048]{2,1,0:T(8,128)(2,1)}, u32[]{:S(2)}, u32[]{:S(2)}) %all-to-all-start.7) | async-done | bytes 4194336 | tf_op jit(solution)/shard_map/all_to_all | solution.py:271
  560.7 11.5 %gather_fusion = bf16[1024,2048]{1,0:T(8,128)(2,1)} fusion(bf16[1024,2048]{1,0:T(8,128)(2,1)} %bitcast.45, s32[1024]{0:T(1024)S(1)} %broadcast_clamp_fusion), kind=kCustom, calls=%fused_computation | custom fusion | bytes 8392704 | tf_op jit(solution)/shard_map/gather | solution.py:272
  572.3 7.5 %fusion = f32[128,2048]{1,0:T(8,128)} fusion(bf16[1024,2048]{1,0:T(8,128)(2,1)} %gather_fusion, f32[128,8]{1,0:T(8,128)S(1)} %copy.102), kind=kLoop, calls=%fused_computation.5 | loop fusion | flops 6029312 | bytes 5246976 | tf_op jit(solution)/shard_map/reduce_sum | solution.py:276
  585.3 23.1 %all-to-all-done.8 = f32[2,64,2048]{2,1,0:T(8,128)} async-done(((f32[2,64,2048]{2,1,0:T(8,128)}), f32[2,64,2048]{2,1,0:T(8,128)}, u32[]{:S(2)}, u32[]{:S(2)}) %all-to-all-start.8) | async-done | bytes 1048608 | tf_op jit(solution)/shard_map/all_to_all | solution.py:281
  (138 shorter events, 105.6 us)
Async XLA Ops:
  7.2 460.3 %copy-start = (bf16[2048,128]{1,0:T(8,128)(2,1)S(1)}, bf16[2048,128]{1,0:T(8,128)(2,1)}, u32[]{:S(2)}) copy-start(bf16[2048,128]{1,0:T(8,128)(2,1)} %param.20) | copy-start | bytes 1572868
  8.8 11.7 %all-to-all-start.1 = ((bf16[8,4,1280]{2,0,1:T(8,128)(2,1)}), bf16[8,4,1280]{2,0,1:T(8,128)(2,1)S(1)}, u32[]{:S(2)}, u32[]{:S(2)}) async-start(bf16[8,4,1280]{2,0,1:T(8,128)(2,1)} %pad_maximum_fusion.1), calls=%async_computation.1 | async-start | bytes 163840 | tf_op jit(solution)/shard_map/all_to_all | solution.py:170
  14.7 134.9 %all-gather.5.cloned.1.call-start = ((), (), s32[]{:S(2)}) async-start(), calls=%async_computation.9 | async-start | bytes 2785280 | tf_op jit(solution)/shard_map/all_gather | solution.py:172
  32.6 15.5 %collective-permute-start = (bf16[192,2048]{1,0:T(8,128)(2,1)S(1)}, bf16[192,2048]{1,0:T(8,128)(2,1)S(1)}, u32[]{:S(2)}, u32[]{:S(2)}) collective-permute-start(bf16[192,2048]{1,0:T(8,128)(2,1)S(1)} %get-tuple-element.35), channel_id=1, source_target_pairs={{1,0},{3,2},{4,7},{6,5},{9,8},{11,10},{12,15},{14,13},{17,16},{19,... | collective-permute-start | bytes 2359304 | tf_op jit(solution)/shard_map/ppermute | solution.py:141
  33.9 28.9 %collective-permute-start.2 = (bf16[192,2048]{1,0:T(8,128)(2,1)S(1)}, bf16[192,2048]{1,0:T(8,128)(2,1)S(1)}, u32[]{:S(2)}, u32[]{:S(2)}) collective-permute-start(bf16[192,2048]{1,0:T(8,128)(2,1)S(1)} %get-tuple-element.36), channel_id=1, source_target_pairs={{1,2},{3,0},{4,5},{6,7},{9,10},{11,8},{12,13},{14,15},{17,18},{19,... | collective-permute-start | bytes 2359304 | tf_op jit(solution)/shard_map/ppermute | solution.py:141
  35.2 33.3 %collective-permute-start.1 = (bf16[192,2048]{1,0:T(8,128)(2,1)S(1)}, bf16[192,2048]{1,0:T(8,128)(2,1)S(1)}, u32[]{:S(2)}, u32[]{:S(2)}) collective-permute-start(bf16[192,2048]{1,0:T(8,128)(2,1)S(1)} %get-tuple-element.37), channel_id=1, source_target_pairs={{0,2},{2,0},{5,7},{7,5},{8,10},{10,8},{13,15},{15,13},{16,18},{18,... | collective-permute-start | bytes 2359304 | tf_op jit(solution)/shard_map/ppermute | solution.py:141
  70.4 76.3 %collective-permute-start.3 = (bf16[4,192,2048]{2,1,0:T(8,128)(2,1)}, bf16[4,192,2048]{2,1,0:T(8,128)(2,1)}, u32[]{:S(2)}, u32[]{:S(2)}) collective-permute-start(bf16[4,192,2048]{2,1,0:T(8,128)(2,1)} %pad_maximum_fusion), channel_id=1, source_target_pairs={{0,4},{5,1},{2,6},{7,3},{8,12},{13,9},{10,14},{15,11},{16,20},{21,... | collective-permute-start | bytes 9437192 | tf_op jit(solution)/shard_map/ppermute | solution.py:148
  78.3 71.3 %all-to-all-start = ((bf16[2,64,8,1536]{3,2,1,0:T(8,128)(2,1)}), bf16[2,64,8,1536]{3,2,1,0:T(8,128)(2,1)}, u32[]{:S(2)}, u32[]{:S(2)}) async-start(bf16[2,64,8,1536]{3,2,1,0:T(8,128)(2,1)} %bitcast.145), calls=%async_computation | async-start | bytes 6291456 | tf_op jit(solution)/shard_map/all_to_all | solution.py:154
  84.6 119.8 %all-gather.7.cloned.1.call-start = ((), (), s32[]{:S(2)}) async-start(), calls=%async_computation.10 | async-start | bytes 7864320 | tf_op jit(solution)/shard_map/all_gather | solution.py:190
  150.8 32.5 %all-to-all-start.3 = ((bf16[4,64,2048]{2,1,0:T(8,128)(2,1)}), bf16[4,64,2048]{2,1,0:T(8,128)(2,1)S(1)}, u32[]{:S(2)}, u32[]{:S(2)}) async-start(bf16[4,64,2048]{2,1,0:T(8,128)(2,1)} %broadcast_in_dim.59), calls=%async_computation.3 | async-start | bytes 2097152 | tf_op jit(solution)/shard_map/all_to_all | solution.py:29
  183.3 84.5 %all-to-all-start.2 = ((bf16[128,16,768]{2,1,0:T(8,128)(2,1)}), bf16[128,16,768]{2,1,0:T(8,128)(2,1)}, u32[]{:S(2)}, u32[]{:S(2)}) async-start(bf16[128,16,768]{2,1,0:T(8,128)(2,1)} %bitcast.144), calls=%async_computation.2 | async-start | bytes 6291456 | tf_op jit(solution)/shard_map/all_to_all | solution.py:180
  276.4 31.2 %copy-start.11 = (f32[2048]{0:T(1024)S(1)}, f32[2048]{0:T(1024)}, u32[]{:S(2)}) copy-start(f32[2048]{0:T(1024)} %param.19) | copy-start | bytes 24580
  276.4 29.5 %all-to-all-start.4 = ((bf16[4,64,2048]{2,1,0:T(8,128)(2,1)}), bf16[4,64,2048]{2,1,0:T(8,128)(2,1)}, u32[]{:S(2)}, u32[]{:S(2)}) async-start(bf16[4,64,2048]{2,1,0:T(8,128)(2,1)} %bitcast.32), calls=%async_computation.4 | async-start | bytes 2097152 | tf_op jit(solution)/shard_map/all_to_all | solution.py:46
  308.6 18.2 %all-to-all-start.5 = ((bf16[2,64,2048]{2,1,0:T(8,128)(2,1)}), bf16[2,64,2048]{2,1,0:T(8,128)(2,1)S(1)}, u32[]{:S(2)}, u32[]{:S(2)}) async-start(bf16[2,64,2048]{2,1,0:T(8,128)(2,1)} %broadcast_in_dim.62), calls=%async_computation.5 | async-start | bytes 1048576 | tf_op jit(solution)/shard_map/all_to_all | solution.py:29
  335.8 102.0 %all-to-all-start.6 = ((bf16[64,16,2048]{2,1,0:T(8,128)(2,1)}), bf16[64,16,2048]{2,1,0:T(8,128)(2,1)}, u32[]{:S(2)}, u32[]{:S(2)}) async-start(bf16[64,16,2048]{2,1,0:T(8,128)(2,1)} %bitcast.142), calls=%async_computation.6 | async-start | bytes 8388608 | tf_op jit(solution)/shard_map/all_to_all | solution.py:256
  343.6 23.8 %all-gather.9.cloned.1.call-start = ((), (), s32[]{:S(2)}) async-start(), calls=%async_computation.11 | async-start | bytes 9437184 | tf_op jit(solution)/shard_map/all_gather | solution.py:220
  460.0 100.7 %all-to-all-start.7 = ((bf16[64,16,2048]{2,1,0:T(8,128)(2,1)}), bf16[64,16,2048]{2,1,0:T(8,128)(2,1)}, u32[]{:S(2)}, u32[]{:S(2)}) async-start(bf16[64,16,2048]{2,1,0:T(8,128)(2,1)} %bitcast.141), calls=%async_computation.7 | async-start | bytes 8388608 | tf_op jit(solution)/shard_map/all_to_all | solution.py:271
  572.3 12.1 %copy-start.17 = (s32[1,2]{1,0:T(1,128)S(1)}, s32[1,2]{1,0:T(1,128)}, u32[]{:S(2)}) copy-start(s32[1,2]{1,0:T(1,128)} %param.25) | copy-start | bytes 28
  572.3 12.1 %copy-start.7 = (bf16[256,1,64]{2,0,1:T(8,128)(2,1)S(1)}, bf16[256,1,64]{2,0,1:T(8,128)(2,1)}, u32[]{:S(2)}) copy-start(bf16[256,1,64]{2,0,1:T(8,128)(2,1)} %copy-done.6) | copy-start | bytes 98308
  572.3 12.1 %copy-start.9 = (bf16[256,1,64]{2,0,1:T(8,128)(2,1)S(1)}, bf16[256,1,64]{2,0,1:T(8,128)(2,1)}, u32[]{:S(2)}) copy-start(bf16[256,1,64]{2,0,1:T(8,128)(2,1)} %copy-done.8) | copy-start | bytes 98308
  572.3 12.2 %copy-start.15 = (pred[256]{0:T(512)(128)(4,1)S(1)}, pred[256]{0:T(512)(128)(4,1)}, u32[]{:S(2)}) copy-start(pred[256]{0:T(512)(128)(4,1)} %copy-done.14) | copy-start | bytes 772
  579.8 30.1 %copy-start.3 = (bf16[64,2048]{1,0:T(8,128)(2,1)S(1)}, bf16[64,2048]{1,0:T(8,128)(2,1)}, u32[]{:S(2)}) copy-start(bf16[64,2048]{1,0:T(8,128)(2,1)} %param.13) | copy-start | bytes 786436
  579.8 28.7 %all-to-all-start.8 = ((f32[2,64,2048]{2,1,0:T(8,128)}), f32[2,64,2048]{2,1,0:T(8,128)}, u32[]{:S(2)}, u32[]{:S(2)}) async-start(f32[2,64,2048]{2,1,0:T(8,128)} %bitcast.150), calls=%async_computation.8 | async-start | bytes 2097152 | tf_op jit(solution)/shard_map/all_to_all | solution.py:281
  585.3 25.3 %copy-start.5 = (bf16[4,2,128,128]{3,2,1,0:T(8,128)(2,1)}, bf16[4,2,128,128]{3,2,1,0:T(8,128)(2,1)S(1)}, u32[]{:S(2)}) copy-start(bf16[4,2,128,128]{3,2,1,0:T(8,128)(2,1)S(1)} %scatter_fusion) | copy-start | bytes 786436
  (10 other events, 42.4 us)
Sparse Core Ops, SparseCore 0:
  30.7 50.4 all-gather.4
  149.8 21.8 all-gather.6
  346.2 21.1 all-gather.8

commit v7 on v6

--- a/solution.py
+++ b/solution.py
@@ -146,7 +146,7 @@
             for d in range(n_tp):
                 share.append((flat(a, b, d % 2, d), flat(a, b, 1 - d % 2, d)))
     slots = jnp.where(primary, slots, lax.ppermute(slots, everyone, perm=share))
-    both_routes = lax.all_gather(routes, "zh", axis=0, tiled=True)
+    both_routes = collect(routes, "zh", 0)
     trainer_block = gate_up_master.shape[1]
     gate_up_half = gate_up_master.astype(jnp.bfloat16).reshape(
         n_zh, half_experts, trainer_block, 2 * FF

time: 628 us -> 634 us (level)
  blocking collectives: 72 us -> 9.99 us
  waiting for transfers between devices: 339 us -> 400 us
    all_gather x1 -> x0, blocking collectives: 62 us -> none  [on_device(): both_routes = lax.all_gather(routes, 'zh', axis=0, tiled=True)]
    all_to_all x1, waiting for transfers between devices: 0.01 us -> 56.4 us  [on_device(): gate_up_half = lax.all_to_all(gate_up_half, 'zh', 0, 0, tiled=True)]
    all_to_all x2 -> x3, starting transfers between devices: 10.7 us -> 17.2 us  [from_everyone(): lax.all_to_all(jnp.broadcast_to(array[None], (peers, *array.shape)), axis...]
    all_to_all x2 -> x3, waiting for transfers between devices: 20.8 us -> 24.3 us  [from_everyone(): lax.all_to_all(jnp.broadcast_to(array[None], (peers, *array.shape)), axis...]
  transfers between devices with their start and end apart: 16 -> 17, of which waited for: 12 -> 14; matrix products, arithmetic and copies ran while one was open for 10% -> 10% of each run, Pallas kernels for 0% -> 0%
where the time goes in v7:
time: 634 us; the launch traced here: 623 us
  waiting for transfers between devices  400 us (63%)
  starting transfers between devices  71.2 us (11%)
  local copies, waits for them, and re-layouts  60.3 us (10%)
  other arithmetic  40.1 us (6%)
  matrix products  26.2 us (4%)
  between operations  15.3 us (2%)
  blocking collectives  9.99 us (2%)
    all_to_all x1, waiting for transfers between devices, on_device(): returned = lax.all_to_all(expert_result, group, 0, 0, tiled=True)  85.9 us
    all_to_all x1, waiting for transfers between devices, on_device(): lax.all_to_all(outgoing.reshape(n_group, capacity, width), group, 0, 0, t...  70.4 us
    all_to_all x1, waiting for transfers between devices, on_device(): gate_up_half = lax.all_to_all(gate_up_half, 'zh', 0, 0, tiled=True)  56.4 us
    all_to_all x1, waiting for transfers between devices, on_device(): pieces = lax.all_to_all(pieces, ('sub2', 'core', 'tp'), 0, 0, tiled=True)  53.8 us
    ppermute x3, waiting for transfers between devices, on_device(): slots.append(lax.ppermute(sent, everyone, perm=pairs))  31.4 us
    all_to_all x1, waiting for transfers between devices, summed_on_arrival(): lax.all_to_all(in_blocks(array, dim, peers), axis, 0, 0, tiled=True)  25 us
    all_to_all x3, waiting for transfers between devices, from_everyone(): lax.all_to_all(jnp.broadcast_to(array[None], (peers, *array.shape)), axis...  24.3 us
    all_to_all x1, waiting for transfers between devices, on_device(): lax.all_to_all(partial.reshape(n_zh, quarter, width), 'zh', 0, 0, tiled=T...  23.2 us
  transfers between devices with their start and end apart: 17, of which 14 were waited for; matrix products, arithmetic and copies ran while one was open for 10% of the time, Pallas kernels for 0%

profile of v7, /device:TPU:2, one launch (start us, length us, event | category | flops | bytes accessed | tf_op | source)
XLA Modules:
  0.0 622.8 jit_solution(8502387128194613790)
XLA Ops:
  8.8 5.9 all-to-all-start.2
  20.5 10.0 %all_gather.12 = bf16[64,1280]{1,0:T(8,128)(2,1)} all-gather(bf16[32,1280]{1,0:T(8,128)(2,1)S(1)} %bitcast.164), channel_id=1, replica_groups=mesh['zh'=2,'sub2'=16,'core'=2,'tp'=4] {'zh'}, dimensions={0}, use_global_device_ids=true | all-gather | bytes 245760 | tf_op jit(solution)/shard_map/all_gather | solution.py:171
  37.2 11.0 %collective-permute-done = bf16[192,2048]{1,0:T(8,128)(2,1)S(1)} collective-permute-done((bf16[192,2048]{1,0:T(8,128)(2,1)S(1)}, bf16[192,2048]{1,0:T(8,128)(2,1)S(1)}, u32[]{:S(2)}, u32[]{:S(2)}) %collective-permute-start) | collective-permute-done | bytes 786464 | tf_op jit(solution)/shard_map/ppermute | solution.py:141
  48.2 14.7 %collective-permute-done.2 = bf16[192,2048]{1,0:T(8,128)(2,1)S(1)} collective-permute-done((bf16[192,2048]{1,0:T(8,128)(2,1)S(1)}, bf16[192,2048]{1,0:T(8,128)(2,1)S(1)}, u32[]{:S(2)}, u32[]{:S(2)}) %collective-permute-start.2) | collective-permute-done | bytes 786464 | tf_op jit(solution)/shard_map/ppermute | solution.py:141
  74.1 6.2 all-to-all-start
  97.7 56.4 %all-to-all-done.1 = bf16[2,64,8,1536]{3,2,1,0:T(8,128)(2,1)} async-done(((bf16[2,64,8,1536]{3,2,1,0:T(8,128)(2,1)}), bf16[2,64,8,1536]{3,2,1,0:T(8,128)(2,1)}, u32[]{:S(2)}, u32[]{:S(2)}) %all-to-all-start.1) | async-done | bytes 3145760 | tf_op jit(solution)/shard_map/all_to_all | solution.py:154
  155.2 7.1 %all-to-all-start.4 = ((bf16[4,64,2048]{2,1,0:T(8,128)(2,1)}), bf16[4,64,2048]{2,1,0:T(8,128)(2,1)S(1)}, u32[]{:S(2)}, u32[]{:S(2)}) async-start(bf16[4,64,2048]{2,1,0:T(8,128)(2,1)} %broadcast_in_dim.58), calls=%async_computation.4 | async-start | bytes 2097152 | tf_op jit(solution)/shard_map/all_to_all | solution.py:29
  162.3 7.5 %reshape.754 = bf16[2,16,4,8,2,768]{5,4,3,2,1,0:T(2,128)(2,1)} reshape(bf16[2,64,8,1536]{3,2,1,0:T(8,128)(2,1)} %all-to-all-done.1) | data formatting | bytes 6291456 | tf_op jit(solution)/shard_map/reshape | solution.py:177
  180.7 7.9 %all-to-all-done.4 = bf16[4,64,2048]{2,1,0:T(8,128)(2,1)S(1)} async-done(((bf16[4,64,2048]{2,1,0:T(8,128)(2,1)}), bf16[4,64,2048]{2,1,0:T(8,128)(2,1)S(1)}, u32[]{:S(2)}, u32[]{:S(2)}) %all-to-all-start.4) | async-done | bytes 1048608 | tf_op jit(solution)/shard_map/all_to_all | solution.py:29
  188.6 11.1 %all-to-all-start.3 = ((bf16[128,16,768]{2,1,0:T(8,128)(2,1)}), bf16[128,16,768]{2,1,0:T(8,128)(2,1)}, u32[]{:S(2)}, u32[]{:S(2)}) async-start(bf16[128,16,768]{2,1,0:T(8,128)(2,1)} %bitcast.145), calls=%async_computation.3 | async-start | bytes 6291456 | tf_op jit(solution)/shard_map/all_to_all | solution.py:180
  219.4 53.8 %all-to-all-done.3 = bf16[128,16,768]{2,1,0:T(8,128)(2,1)} async-done(((bf16[128,16,768]{2,1,0:T(8,128)(2,1)}), bf16[128,16,768]{2,1,0:T(8,128)(2,1)}, u32[]{:S(2)}, u32[]{:S(2)}) %all-to-all-start.3) | async-done | bytes 3145760 | tf_op jit(solution)/shard_map/all_to_all | solution.py:180
  286.3 25.0 %all-to-all-done.5 = bf16[4,64,2048]{2,1,0:T(8,128)(2,1)} async-done(((bf16[4,64,2048]{2,1,0:T(8,128)(2,1)}), bf16[4,64,2048]{2,1,0:T(8,128)(2,1)}, u32[]{:S(2)}, u32[]{:S(2)}) %all-to-all-start.5) | async-done | bytes 1048608 | tf_op jit(solution)/shard_map/all_to_all | solution.py:46
  318.6 13.5 %all-to-all-done.6 = bf16[2,64,2048]{2,1,0:T(8,128)(2,1)S(1)} async-done(((bf16[2,64,2048]{2,1,0:T(8,128)(2,1)}), bf16[2,64,2048]{2,1,0:T(8,128)(2,1)S(1)}, u32[]{:S(2)}, u32[]{:S(2)}) %all-to-all-start.6) | async-done | bytes 524320 | tf_op jit(solution)/shard_map/all_to_all | solution.py:29
  332.1 9.0 %scatter_custom_fusion = bf16[1024,2048]{1,0:T(8,128)(2,1)} fusion(s32[1024]{0:T(1024)S(1)} %bitcast.174, bf16[128,2048]{1,0:T(8,128)(2,1)S(1)} %bitcast.148, bf16[]{:T(256)} %constant.219.clone.1), kind=kCustom, calls=%fused_computation.7 | custom fusion | bytes 4718594 | tf_op jit(solution)/shard_map/scatter | solution.py:254
  341.1 7.8 %all-to-all-start.7 = ((bf16[64,16,2048]{2,1,0:T(8,128)(2,1)}), bf16[64,16,2048]{2,1,0:T(8,128)(2,1)}, u32[]{:S(2)}, u32[]{:S(2)}) async-start(bf16[64,16,2048]{2,1,0:T(8,128)(2,1)} %bitcast.143), calls=%async_computation.7 | async-start | bytes 8388608 | tf_op jit(solution)/shard_map/all_to_all | solution.py:256
  349.7 23.0 %all-gather.8.cloned.1.call-done = bf16[2048,1536]{1,0:T(8,128)(2,1)} async-done(((bf16[2048,768]{1,0:T(8,128)(2,1)}), bf16[2048,1536]{1,0:T(8,128)(2,1)}) %all-gather.8.cloned.1.call-update) | async-done | bytes 6291472 | tf_op jit(solution)/shard_map/all_gather | solution.py:220
  372.7 70.4 %all-to-all-done.7 = bf16[64,16,2048]{2,1,0:T(8,128)(2,1)} async-done(((bf16[64,16,2048]{2,1,0:T(8,128)(2,1)}), bf16[64,16,2048]{2,1,0:T(8,128)(2,1)}, u32[]{:S(2)}, u32[]{:S(2)}) %all-to-all-start.7) | async-done | bytes 4194336 | tf_op jit(solution)/shard_map/all_to_all | solution.py:256
  443.1 10.0 %fusion.76 = f32[1024,1536]{1,0:T(8,128)S(1)} fusion(bf16[1024,2048]{1,0:T(8,128)(2,1)} %bitcast.39, bf16[2048,1536]{1,0:T(8,128)(2,1)} %all-gather.8.cloned.1.call-done), kind=kOutput, calls=%fused_computation.187 | convolution fusion | flops 6442450944 | bytes 16777216 | tf_op jit(solution)/shard_map/dot_general | solution.py:260
  465.3 7.3 %all-to-all-start.8 = ((bf16[64,16,2048]{2,1,0:T(8,128)(2,1)}), bf16[64,16,2048]{2,1,0:T(8,128)(2,1)}, u32[]{:S(2)}, u32[]{:S(2)}) async-start(bf16[64,16,2048]{2,1,0:T(8,128)(2,1)} %bitcast.142), calls=%async_computation.8 | async-start | bytes 8388608 | tf_op jit(solution)/shard_map/all_to_all | solution.py:271
  473.0 6.8 %gather_fusion.1 = f32[1024]{0:T(1024)S(1)} fusion(f32[128,128]{1,0:T(8,128)S(1)} %fusion.75, s32[1024]{0:T(1024)S(1)} %reshape.783), kind=kCustom, calls=%fused_computation.1 | custom fusion | bytes 16384 | tf_op jit(solution)/shard_map/jit(take_along_axis)/gather | solution.py:232
  480.1 85.9 %all-to-all-done.8 = bf16[64,16,2048]{2,1,0:T(8,128)(2,1)} async-done(((bf16[64,16,2048]{2,1,0:T(8,128)(2,1)}), bf16[64,16,2048]{2,1,0:T(8,128)(2,1)}, u32[]{:S(2)}, u32[]{:S(2)}) %all-to-all-start.8) | async-done | bytes 4194336 | tf_op jit(solution)/shard_map/all_to_all | solution.py:271
  566.1 11.5 %gather_fusion = bf16[1024,2048]{1,0:T(8,128)(2,1)} fusion(bf16[1024,2048]{1,0:T(8,128)(2,1)} %bitcast.45, s32[1024]{0:T(1024)S(1)} %broadcast_clamp_fusion), kind=kCustom, calls=%fused_computation | custom fusion | bytes 8392704 | tf_op jit(solution)/shard_map/gather | solution.py:272
  577.6 7.5 %fusion = f32[128,2048]{1,0:T(8,128)} fusion(bf16[1024,2048]{1,0:T(8,128)(2,1)} %gather_fusion, f32[128,8]{1,0:T(8,128)S(1)} %divide_select_fusion), kind=kLoop, calls=%fused_computation.5 | loop fusion | flops 6029312 | bytes 5246976 | tf_op jit(solution)/shard_map/reduce_sum | solution.py:276
  590.7 23.2 %all-to-all-done.9 = f32[2,64,2048]{2,1,0:T(8,128)} async-done(((f32[2,64,2048]{2,1,0:T(8,128)}), f32[2,64,2048]{2,1,0:T(8,128)}, u32[]{:S(2)}, u32[]{:S(2)}) %all-to-all-start.9) | async-done | bytes 1048608 | tf_op jit(solution)/shard_map/all_to_all | solution.py:281
  (133 shorter events, 115.1 us)
Async XLA Ops:
  7.2 465.6 %copy-start = (bf16[2048,128]{1,0:T(8,128)(2,1)S(1)}, bf16[2048,128]{1,0:T(8,128)(2,1)}, u32[]{:S(2)}) copy-start(bf16[2048,128]{1,0:T(8,128)(2,1)} %param.20) | copy-start | bytes 1572868
  8.8 11.7 %all-to-all-start.2 = ((bf16[8,4,1280]{2,0,1:T(8,128)(2,1)}), bf16[8,4,1280]{2,0,1:T(8,128)(2,1)S(1)}, u32[]{:S(2)}, u32[]{:S(2)}) async-start(bf16[8,4,1280]{2,0,1:T(8,128)(2,1)} %pad_maximum_fusion.1), calls=%async_computation.2 | async-start | bytes 163840 | tf_op jit(solution)/shard_map/all_to_all | solution.py:170
  14.7 139.3 %all-gather.4.cloned.1.call-start = ((), (), s32[]{:S(2)}) async-start(), calls=%async_computation.10 | async-start | bytes 2785280 | tf_op jit(solution)/shard_map/all_gather | solution.py:172
  32.6 15.5 %collective-permute-start = (bf16[192,2048]{1,0:T(8,128)(2,1)S(1)}, bf16[192,2048]{1,0:T(8,128)(2,1)S(1)}, u32[]{:S(2)}, u32[]{:S(2)}) collective-permute-start(bf16[192,2048]{1,0:T(8,128)(2,1)S(1)} %get-tuple-element.35), channel_id=1, source_target_pairs={{1,0},{3,2},{4,7},{6,5},{9,8},{11,10},{12,15},{14,13},{17,16},{19,... | collective-permute-start | bytes 2359304 | tf_op jit(solution)/shard_map/ppermute | solution.py:141
  33.9 28.9 %collective-permute-start.2 = (bf16[192,2048]{1,0:T(8,128)(2,1)S(1)}, bf16[192,2048]{1,0:T(8,128)(2,1)S(1)}, u32[]{:S(2)}, u32[]{:S(2)}) collective-permute-start(bf16[192,2048]{1,0:T(8,128)(2,1)S(1)} %get-tuple-element.36), channel_id=1, source_target_pairs={{1,2},{3,0},{4,5},{6,7},{9,10},{11,8},{12,13},{14,15},{17,18},{19,... | collective-permute-start | bytes 2359304 | tf_op jit(solution)/shard_map/ppermute | solution.py:141
  35.2 33.3 %collective-permute-start.1 = (bf16[192,2048]{1,0:T(8,128)(2,1)S(1)}, bf16[192,2048]{1,0:T(8,128)(2,1)S(1)}, u32[]{:S(2)}, u32[]{:S(2)}) collective-permute-start(bf16[192,2048]{1,0:T(8,128)(2,1)S(1)} %get-tuple-element.37), channel_id=1, source_target_pairs={{0,2},{2,0},{5,7},{7,5},{8,10},{10,8},{13,15},{15,13},{16,18},{18,... | collective-permute-start | bytes 2359304 | tf_op jit(solution)/shard_map/ppermute | solution.py:141
  70.4 24.3 %collective-permute-start.3 = (bf16[4,192,2048]{2,1,0:T(8,128)(2,1)}, bf16[4,192,2048]{2,1,0:T(8,128)(2,1)}, u32[]{:S(2)}, u32[]{:S(2)}) collective-permute-start(bf16[4,192,2048]{2,1,0:T(8,128)(2,1)} %pad_maximum_fusion), channel_id=1, source_target_pairs={{0,4},{5,1},{2,6},{7,3},{8,12},{13,9},{10,14},{15,11},{16,20},{21,... | collective-permute-start | bytes 9437192 | tf_op jit(solution)/shard_map/ppermute | solution.py:148
  74.1 13.9 %all-to-all-start = ((s32[2,1,512]{2,1,0:T(1,128)}), s32[2,1,512]{2,1,0:T(1,128)S(1)}, u32[]{:S(2)}, u32[]{:S(2)}) async-start(s32[2,1,512]{2,1,0:T(1,128)} %reshape.816), calls=%async_computation | async-start | bytes 8192 | tf_op jit(solution)/shard_map/all_to_all | solution.py:29
  88.0 66.0 %all-to-all-start.1 = ((bf16[2,64,8,1536]{3,2,1,0:T(8,128)(2,1)}), bf16[2,64,8,1536]{3,2,1,0:T(8,128)(2,1)}, u32[]{:S(2)}, u32[]{:S(2)}) async-start(bf16[2,64,8,1536]{3,2,1,0:T(8,128)(2,1)} %bitcast.146), calls=%async_computation.1 | async-start | bytes 6291456 | tf_op jit(solution)/shard_map/all_to_all | solution.py:154
  93.3 117.1 %all-gather.6.cloned.1.call-start = ((), (), s32[]{:S(2)}) async-start(), calls=%async_computation.11 | async-start | bytes 7864320 | tf_op jit(solution)/shard_map/all_gather | solution.py:190
  94.7 59.4 %copy-start.2 = (bf16[64,2048]{1,0:T(8,128)(2,1)S(1)}, bf16[64,2048]{1,0:T(8,128)(2,1)}, u32[]{:S(2)}) copy-start(bf16[64,2048]{1,0:T(8,128)(2,1)} %param.13) | copy-start | bytes 786436
  155.2 33.4 %all-to-all-start.4 = ((bf16[4,64,2048]{2,1,0:T(8,128)(2,1)}), bf16[4,64,2048]{2,1,0:T(8,128)(2,1)S(1)}, u32[]{:S(2)}, u32[]{:S(2)}) async-start(bf16[4,64,2048]{2,1,0:T(8,128)(2,1)} %broadcast_in_dim.58), calls=%async_computation.4 | async-start | bytes 2097152 | tf_op jit(solution)/shard_map/all_to_all | solution.py:29
  188.6 84.6 %all-to-all-start.3 = ((bf16[128,16,768]{2,1,0:T(8,128)(2,1)}), bf16[128,16,768]{2,1,0:T(8,128)(2,1)}, u32[]{:S(2)}, u32[]{:S(2)}) async-start(bf16[128,16,768]{2,1,0:T(8,128)(2,1)} %bitcast.145), calls=%async_computation.3 | async-start | bytes 6291456 | tf_op jit(solution)/shard_map/all_to_all | solution.py:180
  281.7 31.2 %copy-start.9 = (f32[2048]{0:T(1024)S(1)}, f32[2048]{0:T(1024)}, u32[]{:S(2)}) copy-start(f32[2048]{0:T(1024)} %param.19) | copy-start | bytes 24580
  281.7 29.5 %all-to-all-start.5 = ((bf16[4,64,2048]{2,1,0:T(8,128)(2,1)}), bf16[4,64,2048]{2,1,0:T(8,128)(2,1)}, u32[]{:S(2)}, u32[]{:S(2)}) async-start(bf16[4,64,2048]{2,1,0:T(8,128)(2,1)} %bitcast.32), calls=%async_computation.5 | async-start | bytes 2097152 | tf_op jit(solution)/shard_map/all_to_all | solution.py:46
  313.9 18.2 %all-to-all-start.6 = ((bf16[2,64,2048]{2,1,0:T(8,128)(2,1)}), bf16[2,64,2048]{2,1,0:T(8,128)(2,1)S(1)}, u32[]{:S(2)}, u32[]{:S(2)}) async-start(bf16[2,64,2048]{2,1,0:T(8,128)(2,1)} %broadcast_in_dim.65), calls=%async_computation.6 | async-start | bytes 1048576 | tf_op jit(solution)/shard_map/all_to_all | solution.py:29
  341.1 102.0 %all-to-all-start.7 = ((bf16[64,16,2048]{2,1,0:T(8,128)(2,1)}), bf16[64,16,2048]{2,1,0:T(8,128)(2,1)}, u32[]{:S(2)}, u32[]{:S(2)}) async-start(bf16[64,16,2048]{2,1,0:T(8,128)(2,1)} %bitcast.143), calls=%async_computation.7 | async-start | bytes 8388608 | tf_op jit(solution)/shard_map/all_to_all | solution.py:256
  348.9 23.8 %all-gather.8.cloned.1.call-start = ((), (), s32[]{:S(2)}) async-start(), calls=%async_computation.12 | async-start | bytes 9437184 | tf_op jit(solution)/shard_map/all_gather | solution.py:220
  465.3 100.7 %all-to-all-start.8 = ((bf16[64,16,2048]{2,1,0:T(8,128)(2,1)}), bf16[64,16,2048]{2,1,0:T(8,128)(2,1)}, u32[]{:S(2)}, u32[]{:S(2)}) async-start(bf16[64,16,2048]{2,1,0:T(8,128)(2,1)} %bitcast.142), calls=%async_computation.8 | async-start | bytes 8388608 | tf_op jit(solution)/shard_map/all_to_all | solution.py:271
  577.6 12.1 %copy-start.14 = (s32[1,2]{1,0:T(1,128)S(1)}, s32[1,2]{1,0:T(1,128)}, u32[]{:S(2)}) copy-start(s32[1,2]{1,0:T(1,128)} %param.25) | copy-start | bytes 28
  577.6 12.1 %copy-start.7 = (bf16[256,1,64]{2,0,1:T(8,128)(2,1)S(1)}, bf16[256,1,64]{2,0,1:T(8,128)(2,1)}, u32[]{:S(2)}) copy-start(bf16[256,1,64]{2,0,1:T(8,128)(2,1)} %copy-done.6) | copy-start | bytes 98308
  585.1 30.1 %copy-start.3 = (bf16[64,2048]{1,0:T(8,128)(2,1)S(1)}, bf16[64,2048]{1,0:T(8,128)(2,1)}, u32[]{:S(2)}) copy-start(bf16[64,2048]{1,0:T(8,128)(2,1)} %param.13) | copy-start | bytes 786436
  585.1 28.7 %all-to-all-start.9 = ((f32[2,64,2048]{2,1,0:T(8,128)}), f32[2,64,2048]{2,1,0:T(8,128)}, u32[]{:S(2)}, u32[]{:S(2)}) async-start(f32[2,64,2048]{2,1,0:T(8,128)} %bitcast.151), calls=%async_computation.9 | async-start | bytes 2097152 | tf_op jit(solution)/shard_map/all_to_all | solution.py:281
  590.7 25.3 %copy-start.5 = (bf16[4,2,128,128]{3,2,1,0:T(8,128)(2,1)}, bf16[4,2,128,128]{3,2,1,0:T(8,128)(2,1)S(1)}, u32[]{:S(2)}) copy-start(bf16[4,2,128,128]{3,2,1,0:T(8,128)(2,1)S(1)} %scatter_fusion) | copy-start | bytes 786436
  (8 other events, 28.5 us)
Sparse Core Ops, SparseCore 0:
  30.7 50.4 all-gather.3
  154.2 22.1 all-gather.5
  351.5 21.1 all-gather.7

commit v8 on v5

--- a/solution.py
+++ b/solution.py
@@ -266,17 +266,21 @@
         )
     expert_result = summed.astype(jnp.bfloat16).reshape(n_group, capacity, width)
     returned = lax.all_to_all(expert_result, group, 0, 0, tiled=True)
-    pair_out = returned.reshape(half_experts * capacity, width)[
-        jnp.minimum(target, half_experts * capacity - 1)
-    ]
-    pair_gates = jnp.where(local_pair, gates.reshape(-1), 0.0)
-    partial = jnp.sum(
-        (pair_gates[:, None] * pair_out.astype(jnp.float32)).reshape(row_count, TOPK, width),
-        axis=1,
-    )
-    combined = jnp.sum(
-        lax.all_to_all(partial.reshape(n_zh, quarter, width), "zh", 0, 0, tiled=True), axis=0
-    )
+    returned = returned.reshape(half_experts * capacity, width)
+    pair_gates = jnp.where(local_pair, gates.reshape(-1), 0.0).reshape(n_zh, -1)
+    pair_target = jnp.minimum(target, half_experts * capacity - 1).reshape(n_zh, -1)
+
+    def gated_sum(owner):
+        picked = returned[lax.dynamic_index_in_dim(pair_target, owner, 0, keepdims=False)]
+        weights = lax.dynamic_index_in_dim(pair_gates, owner, 0, keepdims=False)
+        return jnp.sum(
+            (weights[:, None] * picked.astype(jnp.float32)).reshape(quarter, TOPK, width), axis=1
+        )
+
+    from_partner = lax.ppermute(
+        gated_sum(1 - zh), "zh", perm=[(i, n_zh - 1 - i) for i in range(n_zh)]
+    )
+    combined = gated_sum(zh) + from_partner
     own_places = tp_place * quarter + jnp.arange(quarter)
     live_rows = own_places < prompt_length
     hidden_leaving = jnp.where(live_rows[:, None], after_attn + combined, 0.0).astype(jnp.bfloat16)

time: 628 us -> 613 us (0.976)
  waiting for transfers between devices: 388 us -> 372 us
    all_to_all x1 -> x0, waiting for transfers between devices: 24.3 us -> none  [on_device(): lax.all_to_all(partial.reshape(n_zh, quarter, width), 'zh', 0, 0, tiled=T...]
    ppermute x0 -> x1, waiting for transfers between devices: none -> 12.2 us  [on_device(): lax.ppermute(gated_sum(1 - zh), 'zh', perm=[(i, n_zh - 1 - i) for i in ra...]
    gather x1 -> x2, local copies, waits for them, and re-layouts: 11.5 us -> 14.3 us  [gated_sum(): returned[lax.dynamic_index_in_dim(pair_target, owner, 0, keepdims=False)]]
  transfers between devices with their start and end apart: 15 -> 15, of which waited for: 13 -> 13; matrix products, arithmetic and copies ran while one was open for 13% -> 15% of each run, Pallas kernels for 0% -> 0%
where the time goes in v8:
time: 613 us; the launch traced here: 602 us
  waiting for transfers between devices  372 us (61%)
  local copies, waits for them, and re-layouts  66.5 us (11%)
  starting transfers between devices  53.4 us (9%)
  other arithmetic  41.1 us (7%)
  blocking collectives  29.7 us (5%)
  matrix products  23.9 us (4%)
  between operations  15.5 us (3%)
    all_to_all x1, waiting for transfers between devices, on_device(): returned = lax.all_to_all(expert_result, group, 0, 0, tiled=True)  83.7 us
    all_to_all x1, waiting for transfers between devices, on_device(): lax.all_to_all(outgoing.reshape(n_group, capacity, width), group, 0, 0, t...  70.5 us
    all_to_all x1, waiting for transfers between devices, on_device(): pieces = lax.all_to_all(pieces, ('sub2', 'core', 'tp'), 0, 0, tiled=True)  63.5 us
    all_to_all x1, waiting for transfers between devices, on_device(): gate_up_half = lax.all_to_all(gate_up_half, 'zh', 0, 0, tiled=True)  49 us
    ppermute x3, waiting for transfers between devices, on_device(): slots.append(lax.ppermute(sent, everyone, perm=pairs))  31.4 us
    all_to_all x2, waiting for transfers between devices, from_everyone(): lax.all_to_all(jnp.broadcast_to(array[None], (peers, *array.shape)), axis...  21.3 us
    all_gather x1, waiting for transfers between devices, on_device(): expert_gate_up = lax.all_gather(column_half, 'core', axis=1, tiled=True)  21.2 us
    gather x2, local copies, waits for them, and re-layouts, gated_sum(): returned[lax.dynamic_index_in_dim(pair_target, owner, 0, keepdims=False)]  14.3 us
  transfers between devices with their start and end apart: 15, of which 13 were waited for; matrix products, arithmetic and copies ran while one was open for 15% of the time, Pallas kernels for 0%

profile of v8, /device:TPU:2, one launch (start us, length us, event | category | flops | bytes accessed | tf_op | source)
XLA Modules:
  0.0 602.2 jit_solution(18165560892266365476)
XLA Ops:
  8.2 11.5 %all_to_all.51 = bf16[8,4,1280]{2,0,1:T(8,128)(2,1)S(1)} all-to-all(bf16[8,4,1280]{2,0,1:T(8,128)(2,1)S(1)} %pad_maximum_fusion.1), channel_id=1, replica_groups=mesh['zh'=2,'sub2'=16,'core'=2,'tp'=4] {'tp'}, dimensions={1} | all-to-all | bytes 163840 | tf_op jit(solution)/shard_map/all_to_all | solution.py:186
  19.7 10.0 %all_gather.16 = bf16[64,1280]{1,0:T(8,128)(2,1)} all-gather(bf16[32,1280]{1,0:T(8,128)(2,1)S(1)} %bitcast.168), channel_id=1, replica_groups=mesh['zh'=2,'sub2'=16,'core'=2,'tp'=4] {'zh'}, dimensions={0}, use_global_device_ids=true | all-gather | bytes 245760 | tf_op jit(solution)/shard_map/all_gather | solution.py:187
  36.6 11.0 %collective-permute-done = bf16[192,2048]{1,0:T(8,128)(2,1)S(1)} collective-permute-done((bf16[192,2048]{1,0:T(8,128)(2,1)S(1)}, bf16[192,2048]{1,0:T(8,128)(2,1)S(1)}, u32[]{:S(2)}, u32[]{:S(2)}) %collective-permute-start) | collective-permute-done | bytes 786464 | tf_op jit(solution)/shard_map/ppermute | solution.py:141
  47.6 14.7 %collective-permute-done.2 = bf16[192,2048]{1,0:T(8,128)(2,1)S(1)} collective-permute-done((bf16[192,2048]{1,0:T(8,128)(2,1)S(1)}, bf16[192,2048]{1,0:T(8,128)(2,1)S(1)}, u32[]{:S(2)}, u32[]{:S(2)}) %collective-permute-start.2) | collective-permute-done | bytes 786464 | tf_op jit(solution)/shard_map/ppermute | solution.py:141
  72.8 7.5 %all-gather.5.cloned.1.call-done = bf16[1024,1280]{1,0:T(8,128)(2,1)} async-done(((bf16[64,1280]{1,0:T(8,128)(2,1)}), bf16[1024,1280]{1,0:T(8,128)(2,1)}) %all-gather.5.cloned.1.call-update) | async-done | bytes 2621456 | tf_op jit(solution)/shard_map/all_gather | solution.py:188
  80.3 8.3 %all-gather = s32[2,64,8]{1,2,0:T(8,128)S(1)} all-gather(s32[1,64,8]{1,2,0:T(8,128)S(1)} %bitcast.178), channel_id=1, replica_groups=mesh['zh'=2,'sub2'=16,'core'=2,'tp'=4] {'zh'}, dimensions={0}, use_global_device_ids=true | all-gather | bytes 6144 | tf_op jit(solution)/shard_map/all_gather | solution.py:149
  105.2 15.6 %all-to-all-done = bf16[4,64,2048]{2,1,0:T(8,128)(2,1)S(1)} async-done(((bf16[4,64,2048]{2,1,0:T(8,128)(2,1)}), bf16[4,64,2048]{2,1,0:T(8,128)(2,1)S(1)}, u32[]{:S(2)}, u32[]{:S(2)}) %all-to-all-start) | async-done | bytes 1048608 | tf_op jit(solution)/shard_map/all_to_all | solution.py:29
  120.8 6.6 %all-to-all-start.5 = ((bf16[2,64,8,1536]{3,2,1,0:T(8,128)(2,1)}), bf16[2,64,8,1536]{3,2,1,0:T(8,128)(2,1)}, u32[]{:S(2)}, u32[]{:S(2)}) async-start(bf16[2,64,8,1536]{3,2,1,0:T(8,128)(2,1)} %bitcast.156), calls=%async_computation.5 | async-start | bytes 6291456 | tf_op jit(solution)/shard_map/all_to_all | solution.py:156
  149.2 49.0 %all-to-all-done.5 = bf16[2,64,8,1536]{3,2,1,0:T(8,128)(2,1)} async-done(((bf16[2,64,8,1536]{3,2,1,0:T(8,128)(2,1)}), bf16[2,64,8,1536]{3,2,1,0:T(8,128)(2,1)}, u32[]{:S(2)}, u32[]{:S(2)}) %all-to-all-start.5) | async-done | bytes 3145760 | tf_op jit(solution)/shard_map/all_to_all | solution.py:156
  202.1 7.5 %reshape.795 = bf16[2,16,4,8,2,768]{5,4,3,2,1,0:T(2,128)(2,1)} reshape(bf16[2,64,8,1536]{3,2,1,0:T(8,128)(2,1)} %all-to-all-done.5) | data formatting | bytes 6291456 | tf_op jit(solution)/shard_map/reshape | solution.py:157
  214.2 11.9 %all-to-all-done.2 = bf16[4,64,2048]{2,1,0:T(8,128)(2,1)S(1)} async-done(((bf16[4,64,2048]{2,1,0:T(8,128)(2,1)}), bf16[4,64,2048]{2,1,0:T(8,128)(2,1)S(1)}, u32[]{:S(2)}, u32[]{:S(2)}) %all-to-all-start.2) | async-done | bytes 1048608 | tf_op jit(solution)/shard_map/all_to_all | solution.py:46
  246.3 7.4 %all-to-all-start.6 = ((bf16[128,16,768]{2,1,0:T(8,128)(2,1)}), bf16[128,16,768]{2,1,0:T(8,128)(2,1)}, u32[]{:S(2)}, u32[]{:S(2)}) async-start(bf16[128,16,768]{2,1,0:T(8,128)(2,1)} %bitcast.155), calls=%async_computation.6 | async-start | bytes 6291456 | tf_op jit(solution)/shard_map/all_to_all | solution.py:160
  254.8 9.1 %scatter_custom_fusion = bf16[1024,2048]{1,0:T(8,128)(2,1)} fusion(s32[1024]{0:T(1024)S(1)} %bitcast.179, bf16[128,2048]{1,0:T(8,128)(2,1)S(1)} %bitcast.158, bf16[]{:T(256)} %constant.240.clone.1), kind=kCustom, calls=%fused_computation.10 | custom fusion | bytes 4718594 | tf_op jit(solution)/shard_map/scatter | solution.py:251
  263.9 63.5 %all-to-all-done.6 = bf16[128,16,768]{2,1,0:T(8,128)(2,1)} async-done(((bf16[128,16,768]{2,1,0:T(8,128)(2,1)}), bf16[128,16,768]{2,1,0:T(8,128)(2,1)}, u32[]{:S(2)}, u32[]{:S(2)}) %all-to-all-start.6) | async-done | bytes 3145760 | tf_op jit(solution)/shard_map/all_to_all | solution.py:160
  327.5 6.5 %all-to-all-start.4 = ((bf16[64,16,2048]{2,1,0:T(8,128)(2,1)}), bf16[64,16,2048]{2,1,0:T(8,128)(2,1)}, u32[]{:S(2)}, u32[]{:S(2)}) async-start(bf16[64,16,2048]{2,1,0:T(8,128)(2,1)} %bitcast.153), calls=%async_computation.4 | async-start | bytes 8388608 | tf_op jit(solution)/shard_map/all_to_all | solution.py:253
  338.2 21.2 %all-gather.9.cloned.1.call-done = bf16[2048,1536]{1,0:T(8,128)(2,1)} async-done(((bf16[2048,768]{1,0:T(8,128)(2,1)}), bf16[2048,1536]{1,0:T(8,128)(2,1)}) %all-gather.9.cloned.1.call-update) | async-done | bytes 6291472 | tf_op jit(solution)/shard_map/all_gather | solution.py:166
  359.5 70.5 %all-to-all-done.4 = bf16[64,16,2048]{2,1,0:T(8,128)(2,1)} async-done(((bf16[64,16,2048]{2,1,0:T(8,128)(2,1)}), bf16[64,16,2048]{2,1,0:T(8,128)(2,1)}, u32[]{:S(2)}, u32[]{:S(2)}) %all-to-all-start.4) | async-done | bytes 4194336 | tf_op jit(solution)/shard_map/all_to_all | solution.py:253
  429.9 10.0 %fusion.83 = f32[1024,1536]{1,0:T(8,128)S(1)} fusion(bf16[1024,2048]{1,0:T(8,128)(2,1)} %bitcast.33, bf16[2048,1536]{1,0:T(8,128)(2,1)} %all-gather.9.cloned.1.call-done), kind=kOutput, calls=%fused_computation.213 | convolution fusion | flops 6442450944 | bytes 16777216 | tf_op jit(solution)/shard_map/dot_general | solution.py:257
  452.2 8.3 %all-to-all-start.7 = ((bf16[64,16,2048]{2,1,0:T(8,128)(2,1)}), bf16[64,16,2048]{2,1,0:T(8,128)(2,1)}, u32[]{:S(2)}, u32[]{:S(2)}) async-start(bf16[64,16,2048]{2,1,0:T(8,128)(2,1)} %bitcast.152), calls=%async_computation.7 | async-start | bytes 8388608 | tf_op jit(solution)/shard_map/all_to_all | solution.py:268
  463.9 6.8 %gather_fusion.2 = f32[1024]{0:T(1024)S(1)} fusion(f32[128,128]{1,0:T(8,128)S(1)} %fusion.82, s32[1024]{0:T(1024)S(1)} %reshape.820), kind=kCustom, calls=%fused_computation.2 | custom fusion | bytes 16384 | tf_op jit(solution)/shard_map/jit(take_along_axis)/gather | solution.py:229
  472.2 83.7 %all-to-all-done.7 = bf16[64,16,2048]{2,1,0:T(8,128)(2,1)} async-done(((bf16[64,16,2048]{2,1,0:T(8,128)(2,1)}), bf16[64,16,2048]{2,1,0:T(8,128)(2,1)}, u32[]{:S(2)}, u32[]{:S(2)}) %all-to-all-start.7) | async-done | bytes 4194336 | tf_op jit(solution)/shard_map/all_to_all | solution.py:268
  555.9 7.2 %gather_fusion.1 = bf16[512,2048]{1,0:T(8,128)(2,1)S(1)} fusion(bf16[1024,2048]{1,0:T(8,128)(2,1)} %bitcast.45, s32[1024]{0:T(1024)S(1)} %pad_clamp_fusion), kind=kCustom, calls=%fused_computation.1 | custom fusion | bytes 4196352 | tf_op jit(solution)/shard_map/gather | solution.py:274
  572.4 7.1 %gather_fusion = bf16[512,2048]{1,0:T(8,128)(2,1)S(1)} fusion(bf16[1024,2048]{1,0:T(8,128)(2,1)} %bitcast.45, s32[1024]{0:T(1024)S(1)} %pad_clamp_fusion.1), kind=kCustom, calls=%fused_computation | custom fusion | bytes 4196352 | tf_op jit(solution)/shard_map/gather | solution.py:274
  581.4 12.2 %collective-permute-done.4 = f32[64,2048]{1,0:T(8,128)} collective-permute-done((f32[64,2048]{1,0:T(8,128)}, f32[64,2048]{1,0:T(8,128)}, u32[]{:S(2)}, u32[]{:S(2)}) %collective-permute-start.4) | collective-permute-done | bytes 524320 | tf_op jit(solution)/shard_map/ppermute | solution.py:280
  (153 shorter events, 119.9 us)
Async XLA Ops:
  7.2 456.4 %copy-start = (bf16[2048,128]{1,0:T(8,128)(2,1)S(1)}, bf16[2048,128]{1,0:T(8,128)(2,1)}, u32[]{:S(2)}) copy-start(bf16[2048,128]{1,0:T(8,128)(2,1)} %param.20) | copy-start | bytes 1572868
  7.2 73.1 %all-gather.5.cloned.1.call-start = ((), (), s32[]{:S(2)}) async-start(), calls=%async_computation.8 | async-start | bytes 2785280 | tf_op jit(solution)/shard_map/all_gather | solution.py:188
  29.7 105.5 %all-gather.7.cloned.1.call-start = ((), (), s32[]{:S(2)}) async-start(), calls=%async_computation.9 | async-start | bytes 7864320 | tf_op jit(solution)/shard_map/all_gather | solution.py:189
  32.0 15.5 %collective-permute-start = (bf16[192,2048]{1,0:T(8,128)(2,1)S(1)}, bf16[192,2048]{1,0:T(8,128)(2,1)S(1)}, u32[]{:S(2)}, u32[]{:S(2)}) collective-permute-start(bf16[192,2048]{1,0:T(8,128)(2,1)S(1)} %get-tuple-element.29), channel_id=1, source_target_pairs={{1,0},{3,2},{4,7},{6,5},{9,8},{11,10},{12,15},{14,13},{17,16},{19,... | collective-permute-start | bytes 2359304 | tf_op jit(solution)/shard_map/ppermute | solution.py:141
  33.3 28.9 %collective-permute-start.2 = (bf16[192,2048]{1,0:T(8,128)(2,1)S(1)}, bf16[192,2048]{1,0:T(8,128)(2,1)S(1)}, u32[]{:S(2)}, u32[]{:S(2)}) collective-permute-start(bf16[192,2048]{1,0:T(8,128)(2,1)S(1)} %get-tuple-element.30), channel_id=1, source_target_pairs={{1,2},{3,0},{4,5},{6,7},{9,10},{11,8},{12,13},{14,15},{17,18},{19,... | collective-permute-start | bytes 2359304 | tf_op jit(solution)/shard_map/ppermute | solution.py:141
  34.6 33.3 %collective-permute-start.1 = (bf16[192,2048]{1,0:T(8,128)(2,1)S(1)}, bf16[192,2048]{1,0:T(8,128)(2,1)S(1)}, u32[]{:S(2)}, u32[]{:S(2)}) collective-permute-start(bf16[192,2048]{1,0:T(8,128)(2,1)S(1)} %get-tuple-element.31), channel_id=1, source_target_pairs={{0,2},{2,0},{5,7},{7,5},{8,10},{10,8},{13,15},{15,13},{16,18},{18,... | collective-permute-start | bytes 2359304 | tf_op jit(solution)/shard_map/ppermute | solution.py:141
  68.0 12.4 %copy-start.13 = (s32[64,8]{0,1:T(8,128)S(1)}, s32[64,8]{0,1:T(8,128)}, u32[]{:S(2)}) copy-start(s32[64,8]{0,1:T(8,128)} %param.23) | copy-start | bytes 6148
  69.8 18.9 %collective-permute-start.3 = (bf16[4,192,2048]{2,1,0:T(8,128)(2,1)}, bf16[4,192,2048]{2,1,0:T(8,128)(2,1)}, u32[]{:S(2)}, u32[]{:S(2)}) collective-permute-start(bf16[4,192,2048]{2,1,0:T(8,128)(2,1)} %pad_maximum_fusion), channel_id=1, source_target_pairs={{0,4},{5,1},{2,6},{7,3},{8,12},{13,9},{10,14},{15,11},{16,20},{21,... | collective-permute-start | bytes 9437192 | tf_op jit(solution)/shard_map/ppermute | solution.py:148
  92.7 28.1 %all-to-all-start = ((bf16[4,64,2048]{2,1,0:T(8,128)(2,1)}), bf16[4,64,2048]{2,1,0:T(8,128)(2,1)S(1)}, u32[]{:S(2)}, u32[]{:S(2)}) async-start(bf16[4,64,2048]{2,1,0:T(8,128)(2,1)} %broadcast_in_dim.61), calls=%async_computation | async-start | bytes 2097152 | tf_op jit(solution)/shard_map/all_to_all | solution.py:29
  103.9 16.9 %copy-start.16 = (f32[64]{0:T(128)}, f32[64]{0:T(128)S(1)}, u32[]{:S(2)}) copy-start(f32[64]{0:T(128)S(1)} %multiply_power_fusion) | copy-start | bytes 772
  103.9 16.9 %copy-start.14 = (pred[256]{0:T(512)(128)(4,1)}, pred[256]{0:T(512)(128)(4,1)S(1)}, u32[]{:S(2)}) copy-start(pred[256]{0:T(512)(128)(4,1)S(1)} %iota_compare_fusion.8) | copy-start | bytes 772
  120.8 77.4 %all-to-all-start.5 = ((bf16[2,64,8,1536]{3,2,1,0:T(8,128)(2,1)}), bf16[2,64,8,1536]{3,2,1,0:T(8,128)(2,1)}, u32[]{:S(2)}, u32[]{:S(2)}) async-start(bf16[2,64,8,1536]{3,2,1,0:T(8,128)(2,1)} %bitcast.156), calls=%async_computation.5 | async-start | bytes 6291456 | tf_op jit(solution)/shard_map/all_to_all | solution.py:156
  198.2 27.9 %all-to-all-start.2 = ((bf16[4,64,2048]{2,1,0:T(8,128)(2,1)}), bf16[4,64,2048]{2,1,0:T(8,128)(2,1)S(1)}, u32[]{:S(2)}, u32[]{:S(2)}) async-start(bf16[4,64,2048]{2,1,0:T(8,128)(2,1)} %bitcast.26), calls=%async_computation.2 | async-start | bytes 2097152 | tf_op jit(solution)/shard_map/all_to_all | solution.py:46
  209.6 16.9 %copy-start.11 = (f32[2048]{0:T(1024)S(1)}, f32[2048]{0:T(1024)}, u32[]{:S(2)}) copy-start(f32[2048]{0:T(1024)} %param.19) | copy-start | bytes 24580
  227.4 18.9 %all-to-all-start.3 = ((bf16[2,64,2048]{2,1,0:T(8,128)(2,1)}), bf16[2,64,2048]{2,1,0:T(8,128)(2,1)S(1)}, u32[]{:S(2)}, u32[]{:S(2)}) async-start(bf16[2,64,2048]{2,1,0:T(8,128)(2,1)} %broadcast_in_dim.64), calls=%async_computation.3 | async-start | bytes 1048576 | tf_op jit(solution)/shard_map/all_to_all | solution.py:29
  246.3 81.1 %all-to-all-start.6 = ((bf16[128,16,768]{2,1,0:T(8,128)(2,1)}), bf16[128,16,768]{2,1,0:T(8,128)(2,1)}, u32[]{:S(2)}, u32[]{:S(2)}) async-start(bf16[128,16,768]{2,1,0:T(8,128)(2,1)} %bitcast.155), calls=%async_computation.6 | async-start | bytes 6291456 | tf_op jit(solution)/shard_map/all_to_all | solution.py:160
  327.5 102.5 %all-to-all-start.4 = ((bf16[64,16,2048]{2,1,0:T(8,128)(2,1)}), bf16[64,16,2048]{2,1,0:T(8,128)(2,1)}, u32[]{:S(2)}, u32[]{:S(2)}) async-start(bf16[64,16,2048]{2,1,0:T(8,128)(2,1)} %bitcast.153), calls=%async_computation.4 | async-start | bytes 8388608 | tf_op jit(solution)/shard_map/all_to_all | solution.py:253
  333.9 25.5 %all-gather.9.cloned.1.call-start = ((), (), s32[]{:S(2)}) async-start(), calls=%async_computation.10 | async-start | bytes 9437184 | tf_op jit(solution)/shard_map/all_gather | solution.py:166
  452.2 8.8 %copy-start.19 = (s32[1,2]{1,0:T(1,128)S(1)}, s32[1,2]{1,0:T(1,128)}, u32[]{:S(2)}) copy-start(s32[1,2]{1,0:T(1,128)} %param.25) | copy-start | bytes 28
  452.2 9.7 %copy-start.15 = (pred[256]{0:T(512)(128)(4,1)S(1)}, pred[256]{0:T(512)(128)(4,1)}, u32[]{:S(2)}) copy-start(pred[256]{0:T(512)(128)(4,1)} %copy-done.14) | copy-start | bytes 772
  452.2 103.6 %all-to-all-start.7 = ((bf16[64,16,2048]{2,1,0:T(8,128)(2,1)}), bf16[64,16,2048]{2,1,0:T(8,128)(2,1)}, u32[]{:S(2)}, u32[]{:S(2)}) async-start(bf16[64,16,2048]{2,1,0:T(8,128)(2,1)} %bitcast.152), calls=%async_computation.7 | async-start | bytes 8388608 | tf_op jit(solution)/shard_map/all_to_all | solution.py:268
  555.9 13.5 %copy-start.7 = (bf16[256,1,64]{2,0,1:T(8,128)(2,1)S(1)}, bf16[256,1,64]{2,0,1:T(8,128)(2,1)}, u32[]{:S(2)}) copy-start(bf16[256,1,64]{2,0,1:T(8,128)(2,1)} %copy-done.6) | copy-start | bytes 98308
  555.9 13.5 %copy-start.9 = (bf16[256,1,64]{2,0,1:T(8,128)(2,1)S(1)}, bf16[256,1,64]{2,0,1:T(8,128)(2,1)}, u32[]{:S(2)}) copy-start(bf16[256,1,64]{2,0,1:T(8,128)(2,1)} %copy-done.8) | copy-start | bytes 98308
  566.4 27.1 %collective-permute-start.4 = (f32[64,2048]{1,0:T(8,128)}, f32[64,2048]{1,0:T(8,128)}, u32[]{:S(2)}, u32[]{:S(2)}) collective-permute-start(f32[64,2048]{1,0:T(8,128)} %fusion), channel_id=1, source_target_pairs={{0,128},{128,0},{1,129},{129,1},{2,130},{130,2},{3,131},{131,3},{4... | collective-permute-start | bytes 1572872 | tf_op jit(solution)/shard_map/ppermute | solution.py:280
  (11 other events, 38.5 us)
Sparse Core Ops, SparseCore 0:
  29.9 50.3 all-gather.4
  82.1 20.3 all-gather.6
  338.3 21.1 all-gather.8

commit v9 on v8

--- a/solution.py
+++ b/solution.py
@@ -250,22 +250,27 @@
         .at[target]
         .set(jnp.repeat(both_rows, TOPK, axis=0), mode="drop")
     )
-    incoming = lax.all_to_all(
-        outgoing.reshape(n_group, capacity, width), group, 0, 0, tiled=True
-    )
-    flat_rows = incoming.reshape(-1, width)
-    both = jnp.dot(flat_rows, expert_gate_up, preferred_element_type=jnp.float32)
-    units = (jax.nn.silu(both[:, :FF]) * both[:, FF:]).astype(jnp.bfloat16)
-    summed = jnp.zeros((flat_rows.shape[0], width), jnp.float32)
-    for slot in range(n_tp):
-        lower = ((tp_place + slot) % n_tp) * ff_quarter
-        block = lax.dynamic_slice_in_dim(units, lower, ff_quarter, axis=1)
-        produced = jnp.dot(block, slots[slot], preferred_element_type=jnp.float32)
-        summed = summed + lax.optimization_barrier(produced.astype(jnp.bfloat16)).astype(
-            jnp.float32
+    outgoing = outgoing.reshape(n_group, capacity, width)
+    chunk = capacity // 2
+    returned_parts = []
+    for part in range(2):
+        incoming = lax.all_to_all(
+            outgoing[:, part * chunk : (part + 1) * chunk], group, 0, 0, tiled=True
         )
-    expert_result = summed.astype(jnp.bfloat16).reshape(n_group, capacity, width)
-    returned = lax.all_to_all(expert_result, group, 0, 0, tiled=True)
+        flat_rows = incoming.reshape(-1, width)
+        both = jnp.dot(flat_rows, expert_gate_up, preferred_element_type=jnp.float32)
+        units = (jax.nn.silu(both[:, :FF]) * both[:, FF:]).astype(jnp.bfloat16)
+        summed = jnp.zeros((flat_rows.shape[0], width), jnp.float32)
+        for slot in range(n_tp):
+            lower = ((tp_place + slot) % n_tp) * ff_quarter
+            block = lax.dynamic_slice_in_dim(units, lower, ff_quarter, axis=1)
+            produced = jnp.dot(block, slots[slot], preferred_element_type=jnp.float32)
+            summed = summed + lax.optimization_barrier(produced.astype(jnp.bfloat16)).astype(
+                jnp.float32
+            )
+        expert_result = summed.astype(jnp.bfloat16).reshape(n_group, chunk, width)
+        returned_parts.append(lax.all_to_all(expert_result, group, 0, 0, tiled=True))
+    returned = jnp.concatenate(returned_parts, axis=1)
     returned = returned.reshape(half_experts * capacity, width)
     pair_gates = jnp.where(local_pair, gates.reshape(-1), 0.0).reshape(n_zh, -1)
     pair_target = jnp.minimum(target, half_experts * capacity - 1).reshape(n_zh, -1)

time: 613 us -> 614 us (level)
  waiting for transfers between devices: 372 us -> 243 us
  blocking collectives: 29.7 us -> 139 us
  local copies, waits for them, and re-layouts: 66.5 us -> 72.9 us
    all_to_all x0 -> x1, blocking collectives: none -> 56.4 us  [on_device(): lax.all_to_all(outgoing[:, part * chunk:(part + 1) * chunk], group, 0, 0,...]
    all_gather x1, blocking collectives: 8.27 us -> 60.9 us  [on_device(): both_routes = lax.all_gather(routes, 'zh', axis=0, tiled=True)]
    all_to_all x1, waiting for transfers between devices: 49 us -> 0.01 us  [on_device(): gate_up_half = lax.all_to_all(gate_up_half, 'zh', 0, 0, tiled=True)]
    all_to_all x2 -> x3, waiting for transfers between devices: 154 us -> 107 us  [the longest x2 71.8 us: on_device(): lax.all_to_all(expert_result, group, 0, 0, tiled=True)]
    all_gather x1, waiting for transfers between devices: 21.2 us -> 0.02 us  [on_device(): expert_gate_up = lax.all_gather(column_half, 'core', axis=1, tiled=True)]
    all_to_all x1, waiting for transfers between devices: 63.5 us -> 49.5 us  [on_device(): pieces = lax.all_to_all(pieces, ('sub2', 'core', 'tp'), 0, 0, tiled=True)]
    all_to_all x1, waiting for transfers between devices: 11.9 us -> 20.7 us  [summed_on_arrival(): lax.all_to_all(in_blocks(array, dim, peers), axis, 0, 0, tiled=True)]
    all_gather x1, waiting for transfers between devices: 7.45 us -> 0.01 us  [on_device(): head_rows = lax.all_gather(head_rows, 'sub2', axis=0, tiled=True)]
  transfers between devices with their start and end apart: 15 -> 16, of which waited for: 13 -> 11; matrix products, arithmetic and copies ran while one was open for 15% -> 20% of each run, Pallas kernels for 0% -> 0%
where the time goes in v9:
time: 614 us; the launch traced here: 603 us
  waiting for transfers between devices  243 us (40%)
  blocking collectives  139 us (23%)
  local copies, waits for them, and re-layouts  72.9 us (12%)
  starting transfers between devices  58.1 us (9%)
  other arithmetic  45.9 us (7%)
  matrix products  28.1 us (5%)
  between operations  15.8 us (3%)
    all_to_all x2, waiting for transfers between devices, on_device(): lax.all_to_all(expert_result, group, 0, 0, tiled=True)  71.8 us
    all_gather x1, blocking collectives, on_device(): both_routes = lax.all_gather(routes, 'zh', axis=0, tiled=True)  60.9 us
    all_to_all x1, blocking collectives, on_device(): lax.all_to_all(outgoing[:, part * chunk:(part + 1) * chunk], group, 0, 0,...  56.4 us
    all_to_all x1, waiting for transfers between devices, on_device(): pieces = lax.all_to_all(pieces, ('sub2', 'core', 'tp'), 0, 0, tiled=True)  49.5 us
    all_to_all x1, waiting for transfers between devices, on_device(): lax.all_to_all(outgoing[:, part * chunk:(part + 1) * chunk], group, 0, 0,...  35.1 us
    ppermute x3, waiting for transfers between devices, on_device(): slots.append(lax.ppermute(sent, everyone, perm=pairs))  31.4 us
    all_to_all x2, waiting for transfers between devices, from_everyone(): lax.all_to_all(jnp.broadcast_to(array[None], (peers, *array.shape)), axis...  21.4 us
    all_to_all x1, waiting for transfers between devices, summed_on_arrival(): lax.all_to_all(in_blocks(array, dim, peers), axis, 0, 0, tiled=True)  20.7 us
  transfers between devices with their start and end apart: 16, of which 11 were waited for; matrix products, arithmetic and copies ran while one was open for 20% of the time, Pallas kernels for 0%

profile of v9, /device:TPU:2, one launch (start us, length us, event | category | flops | bytes accessed | tf_op | source)
XLA Modules:
  0.0 602.6 jit_solution(3214462003678498072)
XLA Ops:
  8.2 11.5 %all_to_all.61 = bf16[8,4,1280]{2,0,1:T(8,128)(2,1)S(1)} all-to-all(bf16[8,4,1280]{2,0,1:T(8,128)(2,1)S(1)} %pad_maximum_fusion.2), channel_id=1, replica_groups=mesh['zh'=2,'sub2'=16,'core'=2,'tp'=4] {'tp'}, dimensions={1} | all-to-all | bytes 163840 | tf_op jit(solution)/shard_map/all_to_all | solution.py:186
  19.7 10.0 %all_gather.16 = bf16[64,1280]{1,0:T(8,128)(2,1)} all-gather(bf16[32,1280]{1,0:T(8,128)(2,1)S(1)} %bitcast.185), channel_id=1, replica_groups=mesh['zh'=2,'sub2'=16,'core'=2,'tp'=4] {'zh'}, dimensions={0}, use_global_device_ids=true | all-gather | bytes 245760 | tf_op jit(solution)/shard_map/all_gather | solution.py:187
  36.6 11.0 %collective-permute-done = bf16[192,2048]{1,0:T(8,128)(2,1)S(1)} collective-permute-done((bf16[192,2048]{1,0:T(8,128)(2,1)S(1)}, bf16[192,2048]{1,0:T(8,128)(2,1)S(1)}, u32[]{:S(2)}, u32[]{:S(2)}) %collective-permute-start) | collective-permute-done | bytes 786464 | tf_op jit(solution)/shard_map/ppermute | solution.py:141
  47.6 14.6 %collective-permute-done.2 = bf16[192,2048]{1,0:T(8,128)(2,1)S(1)} collective-permute-done((bf16[192,2048]{1,0:T(8,128)(2,1)S(1)}, bf16[192,2048]{1,0:T(8,128)(2,1)S(1)}, u32[]{:S(2)}, u32[]{:S(2)}) %collective-permute-start.2) | collective-permute-done | bytes 786464 | tf_op jit(solution)/shard_map/ppermute | solution.py:141
  84.5 60.9 %all-gather = s32[2,64,8]{1,2,0:T(8,128)S(1)} all-gather(s32[1,64,8]{1,2,0:T(8,128)S(1)} %bitcast.195), channel_id=1, replica_groups=mesh['zh'=2,'sub2'=16,'core'=2,'tp'=4] {'zh'}, dimensions={0}, use_global_device_ids=true | all-gather | bytes 6144 | tf_op jit(solution)/shard_map/all_gather | solution.py:149
  149.7 7.4 %all-to-all-start = ((bf16[4,64,2048]{2,1,0:T(8,128)(2,1)}), bf16[4,64,2048]{2,1,0:T(8,128)(2,1)S(1)}, u32[]{:S(2)}, u32[]{:S(2)}) async-start(bf16[4,64,2048]{2,1,0:T(8,128)(2,1)} %broadcast_in_dim.61), calls=%async_computation | async-start | bytes 2097152 | tf_op jit(solution)/shard_map/all_to_all | solution.py:29
  157.1 7.5 %reshape.801 = bf16[2,16,4,8,2,768]{5,4,3,2,1,0:T(2,128)(2,1)} reshape(bf16[2,64,8,1536]{3,2,1,0:T(8,128)(2,1)} %all-to-all-done.5) | data formatting | bytes 6291456 | tf_op jit(solution)/shard_map/reshape | solution.py:157
  175.2 7.7 %all-to-all-done = bf16[4,64,2048]{2,1,0:T(8,128)(2,1)S(1)} async-done(((bf16[4,64,2048]{2,1,0:T(8,128)(2,1)}), bf16[4,64,2048]{2,1,0:T(8,128)(2,1)S(1)}, u32[]{:S(2)}, u32[]{:S(2)}) %all-to-all-start) | async-done | bytes 1048608 | tf_op jit(solution)/shard_map/all_to_all | solution.py:29
  182.9 11.3 %all-to-all-start.6 = ((bf16[128,16,768]{2,1,0:T(8,128)(2,1)}), bf16[128,16,768]{2,1,0:T(8,128)(2,1)}, u32[]{:S(2)}, u32[]{:S(2)}) async-start(bf16[128,16,768]{2,1,0:T(8,128)(2,1)} %bitcast.172), calls=%async_computation.6 | async-start | bytes 6291456 | tf_op jit(solution)/shard_map/all_to_all | solution.py:160
  218.2 49.5 %all-to-all-done.6 = bf16[128,16,768]{2,1,0:T(8,128)(2,1)} async-done(((bf16[128,16,768]{2,1,0:T(8,128)(2,1)}), bf16[128,16,768]{2,1,0:T(8,128)(2,1)}, u32[]{:S(2)}, u32[]{:S(2)}) %all-to-all-start.6) | async-done | bytes 3145760 | tf_op jit(solution)/shard_map/all_to_all | solution.py:160
  275.6 20.7 %all-to-all-done.2 = bf16[4,64,2048]{2,1,0:T(8,128)(2,1)S(1)} async-done(((bf16[4,64,2048]{2,1,0:T(8,128)(2,1)}), bf16[4,64,2048]{2,1,0:T(8,128)(2,1)S(1)}, u32[]{:S(2)}, u32[]{:S(2)}) %all-to-all-start.2) | async-done | bytes 1048608 | tf_op jit(solution)/shard_map/all_to_all | solution.py:46
  302.1 13.7 %all-to-all-done.3 = bf16[2,64,2048]{2,1,0:T(8,128)(2,1)S(1)} async-done(((bf16[2,64,2048]{2,1,0:T(8,128)(2,1)}), bf16[2,64,2048]{2,1,0:T(8,128)(2,1)S(1)}, u32[]{:S(2)}, u32[]{:S(2)}) %all-to-all-start.3) | async-done | bytes 524320 | tf_op jit(solution)/shard_map/all_to_all | solution.py:29
  315.7 9.1 %scatter_custom_fusion = bf16[1024,2048]{1,0:T(8,128)(2,1)} fusion(s32[1024]{0:T(1024)S(1)} %bitcast.196, bf16[128,2048]{1,0:T(8,128)(2,1)S(1)} %bitcast.175, bf16[]{:T(256)} %constant.249.clone.1), kind=kCustom, calls=%fused_computation.10 | custom fusion | bytes 4718594 | tf_op jit(solution)/shard_map/scatter | solution.py:251
  329.0 56.4 %all_to_all.62 = bf16[64,8,2048]{2,1,0:T(8,128)(2,1)} all-to-all(bf16[64,8,2048]{2,1,0:T(8,128)(2,1)S(1)} %get-tuple-element.25), channel_id=1, replica_groups=mesh['zh'=2,'sub2'=16,'core'=2,'tp'=4] {'sub2','tp'}, dimensions={0} | all-to-all | bytes 4194304 | tf_op jit(solution)/shard_map/all_to_all | solution.py:257
  391.3 6.2 %fusion.7 = f32[512,1536]{1,0:T(8,128)S(1)} fusion(bf16[2048,1536]{1,0:T(8,128)(2,1)} %all-gather.9.cloned.1.call-done, bf16[64,8,2048]{2,1,0:T(8,128)(2,1)} %all_to_all.62), kind=kOutput, calls=%fused_computation.31 | convolution fusion | flops 3221225472 | bytes 11534336 | tf_op jit(solution)/shard_map/dot_general | solution.py:261
  405.7 35.1 %all-to-all-done.4 = bf16[64,8,2048]{2,1,0:T(8,128)(2,1)S(1)} async-done(((bf16[64,8,2048]{2,1,0:T(8,128)(2,1)}), bf16[64,8,2048]{2,1,0:T(8,128)(2,1)S(1)}, u32[]{:S(2)}, u32[]{:S(2)}) %all-to-all-start.4) | async-done | bytes 2097184 | tf_op jit(solution)/shard_map/all_to_all | solution.py:257
  448.3 6.2 %fusion.9 = f32[512,1536]{1,0:T(8,128)S(1)} fusion(bf16[2048,1536]{1,0:T(8,128)(2,1)} %all-gather.9.cloned.1.call-done, bf16[64,8,2048]{2,1,0:T(8,128)(2,1)} %copy-done.8), kind=kOutput, calls=%fused_computation.33 | convolution fusion | flops 3221225472 | bytes 11534336 | tf_op jit(solution)/shard_map/dot_general | solution.py:261
  462.6 35.3 %all-to-all-done.9 = bf16[64,8,2048]{2,1,0:T(8,128)(2,1)S(1)} async-done(((bf16[64,8,2048]{2,1,0:T(8,128)(2,1)}), bf16[64,8,2048]{2,1,0:T(8,128)(2,1)S(1)}, u32[]{:S(2)}, u32[]{:S(2)}) %all-to-all-start.9) | async-done | bytes 2097184 | tf_op jit(solution)/shard_map/all_to_all | solution.py:272
  497.9 6.9 %all-to-all-start.7 = ((bf16[64,8,2048]{2,1,0:T(8,128)(2,1)}), bf16[64,8,2048]{2,1,0:T(8,128)(2,1)}, u32[]{:S(2)}, u32[]{:S(2)}) async-start(bf16[64,8,2048]{2,1,0:T(8,128)(2,1)} %fusion.5), calls=%async_computation.7 | async-start | bytes 4194304 | tf_op jit(solution)/shard_map/all_to_all | solution.py:272
  509.2 6.8 %gather_fusion.2 = f32[1024]{0:T(1024)S(1)} fusion(f32[128,128]{1,0:T(8,128)S(1)} %fusion.106, s32[1024]{0:T(1024)S(1)} %reshape.828), kind=kCustom, calls=%fused_computation.2 | custom fusion | bytes 16384 | tf_op jit(solution)/shard_map/jit(take_along_axis)/gather | solution.py:229
  517.5 36.5 %all-to-all-done.7 = bf16[64,8,2048]{2,1,0:T(8,128)(2,1)} async-done(((bf16[64,8,2048]{2,1,0:T(8,128)(2,1)}), bf16[64,8,2048]{2,1,0:T(8,128)(2,1)}, u32[]{:S(2)}, u32[]{:S(2)}) %all-to-all-start.7) | async-done | bytes 2097184 | tf_op jit(solution)/shard_map/all_to_all | solution.py:272
  558.8 7.2 %gather_fusion.1 = bf16[512,2048]{1,0:T(8,128)(2,1)S(1)} fusion(bf16[1024,2048]{1,0:T(8,128)(2,1)} %bitcast.168, s32[1024]{0:T(1024)S(1)} %pad_clamp_fusion), kind=kCustom, calls=%fused_computation.1 | custom fusion | bytes 4196352 | tf_op jit(solution)/shard_map/gather | solution.py:279
  572.4 7.1 %gather_fusion = bf16[512,2048]{1,0:T(8,128)(2,1)S(1)} fusion(bf16[1024,2048]{1,0:T(8,128)(2,1)} %bitcast.169, s32[1024]{0:T(1024)S(1)} %pad_clamp_fusion.1), kind=kCustom, calls=%fused_computation | custom fusion | bytes 4196352 | tf_op jit(solution)/shard_map/gather | solution.py:279
  581.4 12.2 %collective-permute-done.4 = f32[64,2048]{1,0:T(8,128)} collective-permute-done((f32[64,2048]{1,0:T(8,128)}, f32[64,2048]{1,0:T(8,128)}, u32[]{:S(2)}, u32[]{:S(2)}) %collective-permute-start.4) | collective-permute-done | bytes 524320 | tf_op jit(solution)/shard_map/ppermute | solution.py:285
  (173 shorter events, 136.0 us)
Async XLA Ops:
  7.2 500.7 %copy-start = (bf16[2048,128]{1,0:T(8,128)(2,1)S(1)}, bf16[2048,128]{1,0:T(8,128)(2,1)}, u32[]{:S(2)}) copy-start(bf16[2048,128]{1,0:T(8,128)(2,1)} %param.20) | copy-start | bytes 1572868
  7.2 76.6 %all-gather.5.cloned.1.call-start = ((), (), s32[]{:S(2)}) async-start(), calls=%async_computation.10 | async-start | bytes 2785280 | tf_op jit(solution)/shard_map/all_gather | solution.py:188
  32.1 15.5 %collective-permute-start = (bf16[192,2048]{1,0:T(8,128)(2,1)S(1)}, bf16[192,2048]{1,0:T(8,128)(2,1)S(1)}, u32[]{:S(2)}, u32[]{:S(2)}) collective-permute-start(bf16[192,2048]{1,0:T(8,128)(2,1)S(1)} %get-tuple-element.31), channel_id=1, source_target_pairs={{1,0},{3,2},{4,7},{6,5},{9,8},{11,10},{12,15},{14,13},{17,16},{19,... | collective-permute-start | bytes 2359304 | tf_op jit(solution)/shard_map/ppermute | solution.py:141
  33.4 28.8 %collective-permute-start.2 = (bf16[192,2048]{1,0:T(8,128)(2,1)S(1)}, bf16[192,2048]{1,0:T(8,128)(2,1)S(1)}, u32[]{:S(2)}, u32[]{:S(2)}) collective-permute-start(bf16[192,2048]{1,0:T(8,128)(2,1)S(1)} %get-tuple-element.32), channel_id=1, source_target_pairs={{1,2},{3,0},{4,5},{6,7},{9,10},{11,8},{12,13},{14,15},{17,18},{19,... | collective-permute-start | bytes 2359304 | tf_op jit(solution)/shard_map/ppermute | solution.py:141
  34.7 33.4 %collective-permute-start.1 = (bf16[192,2048]{1,0:T(8,128)(2,1)S(1)}, bf16[192,2048]{1,0:T(8,128)(2,1)S(1)}, u32[]{:S(2)}, u32[]{:S(2)}) collective-permute-start(bf16[192,2048]{1,0:T(8,128)(2,1)S(1)} %get-tuple-element.33), channel_id=1, source_target_pairs={{0,2},{2,0},{5,7},{7,5},{8,10},{10,8},{13,15},{15,13},{16,18},{18,... | collective-permute-start | bytes 2359304 | tf_op jit(solution)/shard_map/ppermute | solution.py:141
  70.0 75.4 %collective-permute-start.3 = (bf16[4,192,2048]{2,1,0:T(8,128)(2,1)}, bf16[4,192,2048]{2,1,0:T(8,128)(2,1)}, u32[]{:S(2)}, u32[]{:S(2)}) collective-permute-start(bf16[4,192,2048]{2,1,0:T(8,128)(2,1)} %pad_maximum_fusion.1), channel_id=1, source_target_pairs={{0,4},{5,1},{2,6},{7,3},{8,12},{13,9},{10,14},{15,11},{16,20},{21,... | collective-permute-start | bytes 9437192 | tf_op jit(solution)/shard_map/ppermute | solution.py:148
  77.9 70.7 %all-to-all-start.5 = ((bf16[2,64,8,1536]{3,2,1,0:T(8,128)(2,1)}), bf16[2,64,8,1536]{3,2,1,0:T(8,128)(2,1)}, u32[]{:S(2)}, u32[]{:S(2)}) async-start(bf16[2,64,8,1536]{3,2,1,0:T(8,128)(2,1)} %bitcast.173), calls=%async_computation.5 | async-start | bytes 6291456 | tf_op jit(solution)/shard_map/all_to_all | solution.py:156
  83.7 120.5 %all-gather.7.cloned.1.call-start = ((), (), s32[]{:S(2)}) async-start(), calls=%async_computation.11 | async-start | bytes 7864320 | tf_op jit(solution)/shard_map/all_gather | solution.py:189
  149.7 33.2 %all-to-all-start = ((bf16[4,64,2048]{2,1,0:T(8,128)(2,1)}), bf16[4,64,2048]{2,1,0:T(8,128)(2,1)S(1)}, u32[]{:S(2)}, u32[]{:S(2)}) async-start(bf16[4,64,2048]{2,1,0:T(8,128)(2,1)} %broadcast_in_dim.61), calls=%async_computation | async-start | bytes 2097152 | tf_op jit(solution)/shard_map/all_to_all | solution.py:29
  182.9 12.0 %copy-start.16 = (f32[2048]{0:T(1024)S(1)}, f32[2048]{0:T(1024)}, u32[]{:S(2)}) copy-start(f32[2048]{0:T(1024)} %param.14) | copy-start | bytes 24580
  182.9 84.8 %all-to-all-start.6 = ((bf16[128,16,768]{2,1,0:T(8,128)(2,1)}), bf16[128,16,768]{2,1,0:T(8,128)(2,1)}, u32[]{:S(2)}, u32[]{:S(2)}) async-start(bf16[128,16,768]{2,1,0:T(8,128)(2,1)} %bitcast.172), calls=%async_computation.6 | async-start | bytes 6291456 | tf_op jit(solution)/shard_map/all_to_all | solution.py:160
  267.7 28.6 %all-to-all-start.2 = ((bf16[4,64,2048]{2,1,0:T(8,128)(2,1)}), bf16[4,64,2048]{2,1,0:T(8,128)(2,1)S(1)}, u32[]{:S(2)}, u32[]{:S(2)}) async-start(bf16[4,64,2048]{2,1,0:T(8,128)(2,1)} %bitcast.26), calls=%async_computation.2 | async-start | bytes 2097152 | tf_op jit(solution)/shard_map/all_to_all | solution.py:46
  271.3 120.1 %all-gather.9.cloned.1.call-start = ((), (), s32[]{:S(2)}) async-start(), calls=%async_computation.12 | async-start | bytes 9437184 | tf_op jit(solution)/shard_map/all_gather | solution.py:166
  275.6 21.1 %copy-start.15 = (f32[2048]{0:T(1024)S(1)}, f32[2048]{0:T(1024)}, u32[]{:S(2)}) copy-start(f32[2048]{0:T(1024)} %param.19) | copy-start | bytes 24580
  297.7 18.1 %all-to-all-start.3 = ((bf16[2,64,2048]{2,1,0:T(8,128)(2,1)}), bf16[2,64,2048]{2,1,0:T(8,128)(2,1)S(1)}, u32[]{:S(2)}, u32[]{:S(2)}) async-start(bf16[2,64,2048]{2,1,0:T(8,128)(2,1)} %broadcast_in_dim.64), calls=%async_computation.3 | async-start | bytes 1048576 | tf_op jit(solution)/shard_map/all_to_all | solution.py:29
  315.7 13.2 %copy-start.5 = (bf16[2,64,2048]{2,1,0:T(8,128)(2,1)}, bf16[2,64,2048]{2,1,0:T(8,128)(2,1)S(1)}, u32[]{:S(2)}) copy-start(bf16[2,64,2048]{2,1,0:T(8,128)(2,1)S(1)} %all-to-all-done.3) | copy-start | bytes 1572868
  385.3 55.6 %all-to-all-start.4 = ((bf16[64,8,2048]{2,1,0:T(8,128)(2,1)}), bf16[64,8,2048]{2,1,0:T(8,128)(2,1)S(1)}, u32[]{:S(2)}, u32[]{:S(2)}) async-start(bf16[64,8,2048]{2,1,0:T(8,128)(2,1)} %get-tuple-element.24), calls=%async_computation.4 | async-start | bytes 4194304 | tf_op jit(solution)/shard_map/all_to_all | solution.py:257
  442.3 55.7 %all-to-all-start.9 = ((bf16[64,8,2048]{2,1,0:T(8,128)(2,1)}), bf16[64,8,2048]{2,1,0:T(8,128)(2,1)S(1)}, u32[]{:S(2)}, u32[]{:S(2)}) async-start(bf16[64,8,2048]{2,1,0:T(8,128)(2,1)} %fusion.6), calls=%async_computation.9 | async-start | bytes 4194304 | tf_op jit(solution)/shard_map/all_to_all | solution.py:272
  462.6 42.7 %copy-start.23 = (s32[1,2]{1,0:T(1,128)S(1)}, s32[1,2]{1,0:T(1,128)}, u32[]{:S(2)}) copy-start(s32[1,2]{1,0:T(1,128)} %param.25) | copy-start | bytes 28
  462.6 43.6 %copy-start.19 = (pred[256]{0:T(512)(128)(4,1)S(1)}, pred[256]{0:T(512)(128)(4,1)}, u32[]{:S(2)}) copy-start(pred[256]{0:T(512)(128)(4,1)} %copy-done.18) | copy-start | bytes 772
  497.9 56.1 %all-to-all-start.7 = ((bf16[64,8,2048]{2,1,0:T(8,128)(2,1)}), bf16[64,8,2048]{2,1,0:T(8,128)(2,1)}, u32[]{:S(2)}, u32[]{:S(2)}) async-start(bf16[64,8,2048]{2,1,0:T(8,128)(2,1)} %fusion.5), calls=%async_computation.7 | async-start | bytes 4194304 | tf_op jit(solution)/shard_map/all_to_all | solution.py:272
  558.8 10.6 %copy-start.11 = (bf16[256,1,64]{2,0,1:T(8,128)(2,1)S(1)}, bf16[256,1,64]{2,0,1:T(8,128)(2,1)}, u32[]{:S(2)}) copy-start(bf16[256,1,64]{2,0,1:T(8,128)(2,1)} %copy-done.10) | copy-start | bytes 98308
  558.8 10.6 %copy-start.13 = (bf16[256,1,64]{2,0,1:T(8,128)(2,1)S(1)}, bf16[256,1,64]{2,0,1:T(8,128)(2,1)}, u32[]{:S(2)}) copy-start(bf16[256,1,64]{2,0,1:T(8,128)(2,1)} %copy-done.12) | copy-start | bytes 98308
  569.4 24.2 %collective-permute-start.4 = (f32[64,2048]{1,0:T(8,128)}, f32[64,2048]{1,0:T(8,128)}, u32[]{:S(2)}, u32[]{:S(2)}) collective-permute-start(f32[64,2048]{1,0:T(8,128)} %fusion), channel_id=1, source_target_pairs={{0,128},{128,0},{1,129},{129,1},{2,130},{130,2},{3,131},{131,3},{4... | collective-permute-start | bytes 1572872 | tf_op jit(solution)/shard_map/ppermute | solution.py:285
  (16 other events, 55.9 us)
Sparse Core Ops, SparseCore 0:
  29.9 50.3 all-gather.4
  86.3 22.2 all-gather.6
  275.8 18.3 all-gather.8

commit v10 on v8

--- a/solution.py
+++ b/solution.py
@@ -163,7 +163,6 @@
         .transpose(3, 0, 1, 2, 4, 5)
         .reshape(-1, FF)
     )
-    expert_gate_up = lax.all_gather(column_half, "core", axis=1, tiled=True)
 
     prompt_rows = collect(hidden_in, "tp", 0)
     column_span = prompt_rows.shape[0]
@@ -215,6 +214,8 @@
         values_local_rows,
         prompt_length,
     )
+    column_half, context_rows = lax.optimization_barrier((column_half, context_rows))
+    expert_gate_up = lax.all_gather(column_half, "core", axis=1, tiled=True)
     attention_sums = summed_on_arrival(
         jnp.dot(context_rows, output_proj, preferred_element_type=jnp.float32).astype(jnp.bfloat16),
         "tp",

time: 613 us -> 629 us (1.026)
  blocking collectives: 29.7 us -> 85.2 us
  waiting for transfers between devices: 372 us -> 325 us
  starting transfers between devices: 53.4 us -> 60.5 us
    all_gather x1, blocking collectives: 9.99 us -> 76.9 us  [on_device(): head_rows = lax.all_gather(head_rows, 'zh', axis=0, tiled=True)]
    all_to_all x1, waiting for transfers between devices: 49 us -> 0.01 us  [on_device(): gate_up_half = lax.all_to_all(gate_up_half, 'zh', 0, 0, tiled=True)]
    all_to_all x1, waiting for transfers between devices: 11.9 us -> 24.7 us  [summed_on_arrival(): lax.all_to_all(in_blocks(array, dim, peers), axis, 0, 0, tiled=True)]
    all_to_all x1 -> x0, blocking collectives: 11.5 us -> none  [on_device(): lax.all_to_all(joined, 'tp', split_axis=1, concat_axis=0, tiled=True)]
    all_gather x1, waiting for transfers between devices: 7.45 us -> 0.02 us  [on_device(): head_rows = lax.all_gather(head_rows, 'sub2', axis=0, tiled=True)]
  transfers between devices with their start and end apart: 15 -> 16, of which waited for: 13 -> 11; matrix products, arithmetic and copies ran while one was open for 15% -> 11% of each run, Pallas kernels for 0% -> 0%
where the time goes in v10:
time: 629 us; the launch traced here: 618 us
  waiting for transfers between devices  325 us (52%)
  blocking collectives  85.2 us (14%)
  local copies, waits for them, and re-layouts  65.4 us (10%)
  starting transfers between devices  60.5 us (10%)
  other arithmetic  40.1 us (6%)
  matrix products  26.1 us (4%)
  between operations  15.6 us (2%)
    all_to_all x1, waiting for transfers between devices, on_device(): returned = lax.all_to_all(expert_result, group, 0, 0, tiled=True)  81.4 us
    all_gather x1, blocking collectives, on_device(): head_rows = lax.all_gather(head_rows, 'zh', axis=0, tiled=True)  76.9 us
    all_to_all x1, waiting for transfers between devices, on_device(): lax.all_to_all(outgoing.reshape(n_group, capacity, width), group, 0, 0, t...  70.4 us
    all_to_all x1, waiting for transfers between devices, on_device(): pieces = lax.all_to_all(pieces, ('sub2', 'core', 'tp'), 0, 0, tiled=True)  60.2 us
    ppermute x3, waiting for transfers between devices, on_device(): slots.append(lax.ppermute(sent, everyone, perm=pairs))  31.8 us
    all_to_all x1, waiting for transfers between devices, summed_on_arrival(): lax.all_to_all(in_blocks(array, dim, peers), axis, 0, 0, tiled=True)  24.7 us
    all_gather x1, waiting for transfers between devices, on_device(): expert_gate_up = lax.all_gather(column_half, 'core', axis=1, tiled=True)  23 us
    all_to_all x2, waiting for transfers between devices, from_everyone(): lax.all_to_all(jnp.broadcast_to(array[None], (peers, *array.shape)), axis...  20.1 us
  transfers between devices with their start and end apart: 16, of which 11 were waited for; matrix products, arithmetic and copies ran while one was open for 11% of the time, Pallas kernels for 0%

profile of v10, /device:TPU:2, one launch (start us, length us, event | category | flops | bytes accessed | tf_op | source)
XLA Modules:
  0.0 618.3 jit_solution(1686067526125205548)
XLA Ops:
  17.2 8.4 %collective-permute-done = bf16[192,2048]{1,0:T(8,128)(2,1)S(1)} collective-permute-done((bf16[192,2048]{1,0:T(8,128)(2,1)S(1)}, bf16[192,2048]{1,0:T(8,128)(2,1)S(1)}, u32[]{:S(2)}, u32[]{:S(2)}) %collective-permute-start) | collective-permute-done | bytes 786464 | tf_op jit(solution)/shard_map/ppermute | solution.py:141
  25.6 23.4 %collective-permute-done.1 = bf16[192,2048]{1,0:T(8,128)(2,1)S(1)} collective-permute-done((bf16[192,2048]{1,0:T(8,128)(2,1)S(1)}, bf16[192,2048]{1,0:T(8,128)(2,1)S(1)}, u32[]{:S(2)}, u32[]{:S(2)}) %collective-permute-start.1) | collective-permute-done | bytes 786464 | tf_op jit(solution)/shard_map/ppermute | solution.py:141
  54.7 5.3 all-to-all-start.3
  65.8 5.9 all-to-all-start
  71.7 76.9 %all_gather.16 = bf16[64,1280]{1,0:T(8,128)(2,1)} all-gather(bf16[32,1280]{1,0:T(8,128)(2,1)S(1)} %bitcast.166), channel_id=1, replica_groups=mesh['zh'=2,'sub2'=16,'core'=2,'tp'=4] {'zh'}, dimensions={0}, use_global_device_ids=true | all-gather | bytes 245760 | tf_op jit(solution)/shard_map/all_gather | solution.py:186
  148.7 8.3 %all-gather = s32[2,64,8]{1,2,0:T(8,128)S(1)} all-gather(s32[1,64,8]{1,2,0:T(8,128)S(1)} %bitcast.176), channel_id=1, replica_groups=mesh['zh'=2,'sub2'=16,'core'=2,'tp'=4] {'zh'}, dimensions={0}, use_global_device_ids=true | all-gather | bytes 6144 | tf_op jit(solution)/shard_map/all_gather | solution.py:149
  165.3 7.5 %reshape.779 = bf16[2,16,4,8,2,768]{5,4,3,2,1,0:T(2,128)(2,1)} reshape(bf16[2,64,8,1536]{3,2,1,0:T(8,128)(2,1)} %all-to-all-done) | data formatting | bytes 6291456 | tf_op jit(solution)/shard_map/reshape | solution.py:157
  183.3 6.4 %all-to-all-done.2 = bf16[4,64,2048]{2,1,0:T(8,128)(2,1)S(1)} async-done(((bf16[4,64,2048]{2,1,0:T(8,128)(2,1)}), bf16[4,64,2048]{2,1,0:T(8,128)(2,1)S(1)}, u32[]{:S(2)}, u32[]{:S(2)}) %all-to-all-start.2) | async-done | bytes 1048608 | tf_op jit(solution)/shard_map/all_to_all | solution.py:29
  189.8 10.2 %all-to-all-start.1 = ((bf16[128,16,768]{2,1,0:T(8,128)(2,1)}), bf16[128,16,768]{2,1,0:T(8,128)(2,1)}, u32[]{:S(2)}, u32[]{:S(2)}) async-start(bf16[128,16,768]{2,1,0:T(8,128)(2,1)} %bitcast.153), calls=%async_computation.1 | async-start | bytes 6291456 | tf_op jit(solution)/shard_map/all_to_all | solution.py:160
  205.8 5.3 reshape.801
  213.5 60.2 %all-to-all-done.1 = bf16[128,16,768]{2,1,0:T(8,128)(2,1)} async-done(((bf16[128,16,768]{2,1,0:T(8,128)(2,1)}), bf16[128,16,768]{2,1,0:T(8,128)(2,1)}, u32[]{:S(2)}, u32[]{:S(2)}) %all-to-all-start.1) | async-done | bytes 3145760 | tf_op jit(solution)/shard_map/all_to_all | solution.py:160
  295.8 24.7 %all-to-all-done.4 = bf16[4,64,2048]{2,1,0:T(8,128)(2,1)S(1)} async-done(((bf16[4,64,2048]{2,1,0:T(8,128)(2,1)}), bf16[4,64,2048]{2,1,0:T(8,128)(2,1)S(1)}, u32[]{:S(2)}, u32[]{:S(2)}) %all-to-all-start.4) | async-done | bytes 1048608 | tf_op jit(solution)/shard_map/all_to_all | solution.py:46
  326.3 13.7 %all-to-all-done.5 = bf16[2,64,2048]{2,1,0:T(8,128)(2,1)S(1)} async-done(((bf16[2,64,2048]{2,1,0:T(8,128)(2,1)}), bf16[2,64,2048]{2,1,0:T(8,128)(2,1)S(1)}, u32[]{:S(2)}, u32[]{:S(2)}) %all-to-all-start.5) | async-done | bytes 524320 | tf_op jit(solution)/shard_map/all_to_all | solution.py:29
  339.9 9.1 %scatter_custom_fusion = bf16[1024,2048]{1,0:T(8,128)(2,1)} fusion(s32[1024]{0:T(1024)S(1)} %bitcast.177, bf16[128,2048]{1,0:T(8,128)(2,1)S(1)} %bitcast.156, bf16[]{:T(256)} %constant.240.clone.1), kind=kCustom, calls=%fused_computation.10 | custom fusion | bytes 4718594 | tf_op jit(solution)/shard_map/scatter | solution.py:252
  349.1 7.8 %all-to-all-start.6 = ((bf16[64,16,2048]{2,1,0:T(8,128)(2,1)}), bf16[64,16,2048]{2,1,0:T(8,128)(2,1)}, u32[]{:S(2)}, u32[]{:S(2)}) async-start(bf16[64,16,2048]{2,1,0:T(8,128)(2,1)} %bitcast.151), calls=%async_computation.6 | async-start | bytes 8388608 | tf_op jit(solution)/shard_map/all_to_all | solution.py:254
  357.7 23.0 %all-gather.9.cloned.1.call-done = bf16[2048,1536]{1,0:T(8,128)(2,1)} async-done(((bf16[2048,768]{1,0:T(8,128)(2,1)}), bf16[2048,1536]{1,0:T(8,128)(2,1)}) %all-gather.9.cloned.1.call-update) | async-done | bytes 6291472 | tf_op jit(solution)/shard_map/all_gather | solution.py:218
  380.7 70.4 %all-to-all-done.6 = bf16[64,16,2048]{2,1,0:T(8,128)(2,1)} async-done(((bf16[64,16,2048]{2,1,0:T(8,128)(2,1)}), bf16[64,16,2048]{2,1,0:T(8,128)(2,1)}, u32[]{:S(2)}, u32[]{:S(2)}) %all-to-all-start.6) | async-done | bytes 4194336 | tf_op jit(solution)/shard_map/all_to_all | solution.py:254
  451.1 10.0 %fusion.83 = f32[1024,1536]{1,0:T(8,128)S(1)} fusion(bf16[1024,2048]{1,0:T(8,128)(2,1)} %bitcast.39, bf16[2048,1536]{1,0:T(8,128)(2,1)} %all-gather.9.cloned.1.call-done), kind=kOutput, calls=%fused_computation.213 | convolution fusion | flops 6442450944 | bytes 16777216 | tf_op jit(solution)/shard_map/dot_general | solution.py:258
  473.4 7.4 %all-to-all-start.7 = ((bf16[64,16,2048]{2,1,0:T(8,128)(2,1)}), bf16[64,16,2048]{2,1,0:T(8,128)(2,1)}, u32[]{:S(2)}, u32[]{:S(2)}) async-start(bf16[64,16,2048]{2,1,0:T(8,128)(2,1)} %bitcast.150), calls=%async_computation.7 | async-start | bytes 8388608 | tf_op jit(solution)/shard_map/all_to_all | solution.py:269
  484.6 6.8 %gather_fusion.2 = f32[1024]{0:T(1024)S(1)} fusion(f32[128,128]{1,0:T(8,128)S(1)} %fusion.82, s32[1024]{0:T(1024)S(1)} %reshape.820), kind=kCustom, calls=%fused_computation.2 | custom fusion | bytes 16384 | tf_op jit(solution)/shard_map/jit(take_along_axis)/gather | solution.py:230
  492.9 81.4 %all-to-all-done.7 = bf16[64,16,2048]{2,1,0:T(8,128)(2,1)} async-done(((bf16[64,16,2048]{2,1,0:T(8,128)(2,1)}), bf16[64,16,2048]{2,1,0:T(8,128)(2,1)}, u32[]{:S(2)}, u32[]{:S(2)}) %all-to-all-start.7) | async-done | bytes 4194336 | tf_op jit(solution)/shard_map/all_to_all | solution.py:269
  574.3 7.2 %gather_fusion.1 = bf16[512,2048]{1,0:T(8,128)(2,1)S(1)} fusion(bf16[1024,2048]{1,0:T(8,128)(2,1)} %bitcast.45, s32[1024]{0:T(1024)S(1)} %pad_clamp_fusion), kind=kCustom, calls=%fused_computation.1 | custom fusion | bytes 4196352 | tf_op jit(solution)/shard_map/gather | solution.py:275
  588.2 7.1 %gather_fusion = bf16[512,2048]{1,0:T(8,128)(2,1)S(1)} fusion(bf16[1024,2048]{1,0:T(8,128)(2,1)} %bitcast.45, s32[1024]{0:T(1024)S(1)} %pad_clamp_fusion.1), kind=kCustom, calls=%fused_computation | custom fusion | bytes 4196352 | tf_op jit(solution)/shard_map/gather | solution.py:275
  597.2 12.3 %collective-permute-done.4 = f32[64,2048]{1,0:T(8,128)} collective-permute-done((f32[64,2048]{1,0:T(8,128)}, f32[64,2048]{1,0:T(8,128)}, u32[]{:S(2)}, u32[]{:S(2)}) %collective-permute-start.4) | collective-permute-done | bytes 524320 | tf_op jit(solution)/shard_map/ppermute | solution.py:281
  (154 shorter events, 104.1 us)
Async XLA Ops:
  7.2 477.1 %copy-start = (bf16[2048,128]{1,0:T(8,128)(2,1)S(1)}, bf16[2048,128]{1,0:T(8,128)(2,1)}, u32[]{:S(2)}) copy-start(bf16[2048,128]{1,0:T(8,128)(2,1)} %param.20) | copy-start | bytes 1572868
  9.6 16.0 %collective-permute-start = (bf16[192,2048]{1,0:T(8,128)(2,1)S(1)}, bf16[192,2048]{1,0:T(8,128)(2,1)S(1)}, u32[]{:S(2)}, u32[]{:S(2)}) collective-permute-start(bf16[192,2048]{1,0:T(8,128)(2,1)S(1)} %get-tuple-element.33), channel_id=1, source_target_pairs={{1,0},{3,2},{4,7},{6,5},{9,8},{11,10},{12,15},{14,13},{17,16},{19,... | collective-permute-start | bytes 2359304 | tf_op jit(solution)/shard_map/ppermute | solution.py:141
  10.9 38.1 %collective-permute-start.1 = (bf16[192,2048]{1,0:T(8,128)(2,1)S(1)}, bf16[192,2048]{1,0:T(8,128)(2,1)S(1)}, u32[]{:S(2)}, u32[]{:S(2)}) collective-permute-start(bf16[192,2048]{1,0:T(8,128)(2,1)S(1)} %get-tuple-element.35), channel_id=1, source_target_pairs={{0,2},{2,0},{5,7},{7,5},{8,10},{10,8},{13,15},{15,13},{16,18},{18,... | collective-permute-start | bytes 2359304 | tf_op jit(solution)/shard_map/ppermute | solution.py:141
  15.9 33.1 %collective-permute-start.2 = (bf16[192,2048]{1,0:T(8,128)(2,1)S(1)}, bf16[192,2048]{1,0:T(8,128)(2,1)S(1)}, u32[]{:S(2)}, u32[]{:S(2)}) collective-permute-start(bf16[192,2048]{1,0:T(8,128)(2,1)S(1)} %get-tuple-element.34), channel_id=1, source_target_pairs={{1,2},{3,0},{4,5},{6,7},{9,10},{11,8},{12,13},{14,15},{17,18},{19,... | collective-permute-start | bytes 2359304 | tf_op jit(solution)/shard_map/ppermute | solution.py:141
  51.0 106.0 %collective-permute-start.3 = (bf16[4,192,2048]{2,1,0:T(8,128)(2,1)}, bf16[4,192,2048]{2,1,0:T(8,128)(2,1)}, u32[]{:S(2)}, u32[]{:S(2)}) collective-permute-start(bf16[4,192,2048]{2,1,0:T(8,128)(2,1)} %pad_maximum_fusion), channel_id=1, source_target_pairs={{0,4},{5,1},{2,6},{7,3},{8,12},{13,9},{10,14},{15,11},{16,20},{21,... | collective-permute-start | bytes 9437192 | tf_op jit(solution)/shard_map/ppermute | solution.py:148
  54.7 11.1 %all-to-all-start.3 = ((bf16[8,4,1280]{2,0,1:T(8,128)(2,1)}), bf16[8,4,1280]{2,0,1:T(8,128)(2,1)S(1)}, u32[]{:S(2)}, u32[]{:S(2)}) async-start(bf16[8,4,1280]{2,0,1:T(8,128)(2,1)} %pad_maximum_fusion.1), calls=%async_computation.3 | async-start | bytes 163840 | tf_op jit(solution)/shard_map/all_to_all | solution.py:185
  65.8 82.9 %copy-start.14 = (s32[64,8]{0,1:T(8,128)S(1)}, s32[64,8]{0,1:T(8,128)}, u32[]{:S(2)}) copy-start(s32[64,8]{0,1:T(8,128)} %param.23) | copy-start | bytes 6148
  65.8 94.2 %all-to-all-start = ((bf16[2,64,8,1536]{3,2,1,0:T(8,128)(2,1)}), bf16[2,64,8,1536]{3,2,1,0:T(8,128)(2,1)}, u32[]{:S(2)}, u32[]{:S(2)}) async-start(bf16[2,64,8,1536]{3,2,1,0:T(8,128)(2,1)} %bitcast.154), calls=%async_computation | async-start | bytes 6291456 | tf_op jit(solution)/shard_map/all_to_all | solution.py:156
  71.7 128.9 %all-gather.5.cloned.1.call-start = ((), (), s32[]{:S(2)}) async-start(), calls=%async_computation.8 | async-start | bytes 2785280 | tf_op jit(solution)/shard_map/all_gather | solution.py:187
  161.1 28.7 %all-to-all-start.2 = ((bf16[4,64,2048]{2,1,0:T(8,128)(2,1)}), bf16[4,64,2048]{2,1,0:T(8,128)(2,1)S(1)}, u32[]{:S(2)}, u32[]{:S(2)}) async-start(bf16[4,64,2048]{2,1,0:T(8,128)(2,1)} %broadcast_in_dim.61), calls=%async_computation.2 | async-start | bytes 2097152 | tf_op jit(solution)/shard_map/all_to_all | solution.py:29
  189.8 11.0 %copy-start.13 = (f32[2048]{0:T(1024)S(1)}, f32[2048]{0:T(1024)}, u32[]{:S(2)}) copy-start(f32[2048]{0:T(1024)} %param.14) | copy-start | bytes 24580
  189.8 83.9 %all-to-all-start.1 = ((bf16[128,16,768]{2,1,0:T(8,128)(2,1)}), bf16[128,16,768]{2,1,0:T(8,128)(2,1)}, u32[]{:S(2)}, u32[]{:S(2)}) async-start(bf16[128,16,768]{2,1,0:T(8,128)(2,1)} %bitcast.153), calls=%async_computation.1 | async-start | bytes 6291456 | tf_op jit(solution)/shard_map/all_to_all | solution.py:160
  200.0 77.6 %all-gather.7.cloned.1.call-start = ((), (), s32[]{:S(2)}) async-start(), calls=%async_computation.9 | async-start | bytes 7864320 | tf_op jit(solution)/shard_map/all_gather | solution.py:188
  291.8 29.1 %copy-start.12 = (f32[2048]{0:T(1024)S(1)}, f32[2048]{0:T(1024)}, u32[]{:S(2)}) copy-start(f32[2048]{0:T(1024)} %param.19) | copy-start | bytes 24580
  291.8 28.7 %all-to-all-start.4 = ((bf16[4,64,2048]{2,1,0:T(8,128)(2,1)}), bf16[4,64,2048]{2,1,0:T(8,128)(2,1)S(1)}, u32[]{:S(2)}, u32[]{:S(2)}) async-start(bf16[4,64,2048]{2,1,0:T(8,128)(2,1)} %bitcast.32), calls=%async_computation.4 | async-start | bytes 2097152 | tf_op jit(solution)/shard_map/all_to_all | solution.py:46
  321.9 18.1 %all-to-all-start.5 = ((bf16[2,64,2048]{2,1,0:T(8,128)(2,1)}), bf16[2,64,2048]{2,1,0:T(8,128)(2,1)S(1)}, u32[]{:S(2)}, u32[]{:S(2)}) async-start(bf16[2,64,2048]{2,1,0:T(8,128)(2,1)} %broadcast_in_dim.64), calls=%async_computation.5 | async-start | bytes 1048576 | tf_op jit(solution)/shard_map/all_to_all | solution.py:29
  349.1 102.0 %all-to-all-start.6 = ((bf16[64,16,2048]{2,1,0:T(8,128)(2,1)}), bf16[64,16,2048]{2,1,0:T(8,128)(2,1)}, u32[]{:S(2)}, u32[]{:S(2)}) async-start(bf16[64,16,2048]{2,1,0:T(8,128)(2,1)} %bitcast.151), calls=%async_computation.6 | async-start | bytes 8388608 | tf_op jit(solution)/shard_map/all_to_all | solution.py:254
  356.9 23.8 %all-gather.9.cloned.1.call-start = ((), (), s32[]{:S(2)}) async-start(), calls=%async_computation.10 | async-start | bytes 9437184 | tf_op jit(solution)/shard_map/all_gather | solution.py:218
  473.4 100.9 %all-to-all-start.7 = ((bf16[64,16,2048]{2,1,0:T(8,128)(2,1)}), bf16[64,16,2048]{2,1,0:T(8,128)(2,1)}, u32[]{:S(2)}, u32[]{:S(2)}) async-start(bf16[64,16,2048]{2,1,0:T(8,128)(2,1)} %bitcast.150), calls=%async_computation.7 | async-start | bytes 8388608 | tf_op jit(solution)/shard_map/all_to_all | solution.py:269
  574.3 11.5 %copy-start.7 = (bf16[256,1,64]{2,0,1:T(8,128)(2,1)S(1)}, bf16[256,1,64]{2,0,1:T(8,128)(2,1)}, u32[]{:S(2)}) copy-start(bf16[256,1,64]{2,0,1:T(8,128)(2,1)} %get-tuple-element.40) | copy-start | bytes 98308
  574.3 11.5 %copy-start.9 = (bf16[256,1,64]{2,0,1:T(8,128)(2,1)S(1)}, bf16[256,1,64]{2,0,1:T(8,128)(2,1)}, u32[]{:S(2)}) copy-start(bf16[256,1,64]{2,0,1:T(8,128)(2,1)} %get-tuple-element.41) | copy-start | bytes 98308
  574.3 11.5 %copy-start.18 = (pred[2,128]{1,0:T(4,128)(4,1)S(1)}, pred[2,128]{1,0:T(4,128)(4,1)}, u32[]{:S(2)}) copy-start(pred[2,128]{1,0:T(4,128)(4,1)} %add_compare_fusion) | copy-start | bytes 772
  584.9 24.6 %collective-permute-start.4 = (f32[64,2048]{1,0:T(8,128)}, f32[64,2048]{1,0:T(8,128)}, u32[]{:S(2)}, u32[]{:S(2)}) collective-permute-start(f32[64,2048]{1,0:T(8,128)} %fusion), channel_id=1, source_target_pairs={{0,128},{128,0},{1,129},{129,1},{2,130},{130,2},{3,131},{131,3},{4... | collective-permute-start | bytes 1572872 | tf_op jit(solution)/shard_map/ppermute | solution.py:281
  588.2 21.2 %copy-start.16 = (pred[64]{0:T(512)(128)(4,1)S(1)}, pred[64]{0:T(512)(128)(4,1)}, u32[]{:S(2)}) copy-start(pred[64]{0:T(512)(128)(4,1)} %add_compare_fusion.1) | copy-start | bytes 196
  (12 other events, 36.7 us)
Sparse Core Ops, SparseCore 0:
  148.8 48.7 all-gather.4
  202.6 22.0 all-gather.6
  359.5 21.1 all-gather.8
